TPU v7x, 32 devices: a whole 2x2x4 slice. The times are simulated.
32 devices in a mesh: member: 4 (over y, core), band: 8 (over z, x).
Axes of the slice: x: 2, y: 2, z: 4, core: 2. Of those that a mesh axis runs over, the one named last changes fastest.
Arguments:
- obs_values: bfloat16 [65536, 128], P(('member', 'band')), parts along dimension 0, may hold values from -6 to 6
- obs_band: int32 [65536, 1], P(('member', 'band')), parts along dimension 0, may hold values from 0 to 7; in each aligned block of 2048 rows (0 to 2047, 2048 to 4095, ...) at most 256 rows name the same one
- obs_cell: int32 [65536], P(('member', 'band')), parts along dimension 0, may hold values from 0 to 2047
- obs_offset: int32 [65536], P(('member', 'band')), parts along dimension 0, may hold values from 0 to 7
- sat_values: bfloat16 [65536, 128], P(('member', 'band')), parts along dimension 0, may hold values from -6 to 6
- sat_cell: int32 [65536], P(('member', 'band')), parts along dimension 0, may hold values from 0 to 2047
- sat_offset: int32 [65536], P(('member', 'band')), parts along dimension 0, may hold values from 0 to 7
- density_embed: float32 [128], replicated, may hold values from -3 to 3
- conv1_weight: bfloat16 [3, 3, 128, 128], replicated, may hold values from -0.1875 to 0.1875
- conv1_bias: float32 [128], replicated, may hold values from -3 to 3
- conv2_weight: bfloat16 [3, 3, 128, 256], replicated, may hold values from -0.1875 to 0.1875
- conv2_bias: float32 [256], replicated, may hold values from -3 to 3
- proj_weight: bfloat16 [256, 256], replicated, may hold values from -0.375 to 0.375
Outputs:
- latents: bfloat16 [64, 64, 256], P('member'), parts along dimension 0
There are 4 independent parts, one for each index of `member`. A program takes and returns all parts, laid end to end along the dimension named above; an argument that names none is the same for every part. Nothing has to cross between parts.
Inputs may be any that keep to these rules, and one draw needn't show every extreme that they name: `obs_band`: among the station rows of one device, at most 256 name the same band, and in every draw some band is named by exactly 256 rows of some device.
All inputs are finite; a program needn't handle non-finite values.
Results may differ from a plain program's by a relative error of at most 0.0061.
Values may be sent and summed in bfloat16 or wider, within the bound.
No kernel may reach another device: no remote copies, remote signals or barrier semaphores. Data moves between devices by JAX's collectives and lax.ppermute only.
A program may use at most 64 MiB of HBM per device.

v0:
```python
import jax
import jax.numpy as jnp
from jax import lax
from jax.sharding import PartitionSpec as P

LAT_DEV = 8
LON = 256


def passed_along(value, axis, by):
    length = lax.axis_size(axis)
    pairs = [(i, i + by) for i in range(length) if 0 <= i + by < length]
    return lax.ppermute(value, axis, pairs)


def weights_of(offsets):
    return jnp.exp(-offsets.astype(jnp.float32) ** 2 / 32.0).astype(jnp.bfloat16)


def deposit(values, cells, offsets, total_cells):
    weight = weights_of(offsets)
    block = min(512, total_cells)
    count = total_cells // block

    def one_block(start):
        ids = start + jnp.arange(block, dtype=jnp.int32)
        table = jnp.where(
            ids[:, None] == cells[None, :], weight[None, :], jnp.zeros((), jnp.bfloat16)
        )
        sums = jnp.dot(table, values, preferred_element_type=jnp.float32)
        density = jnp.sum(table, axis=1, dtype=jnp.float32)
        return (sums, density)

    starts = jnp.arange(count, dtype=jnp.int32) * block
    sums, density = lax.map(one_block, starts)
    return (sums.reshape(total_cells, values.shape[1]), density.reshape(total_cells))


def strided(padded, weight, bias):
    count, width, chans = padded.shape
    grid = jnp.pad(padded, ((0, 1), (1, 1), (0, 0)))
    parted = grid.reshape((count + 1) // 2, 2, (width + 2) // 2, 2, chans)
    rows = (count - 1) // 2
    cols = width // 2
    total = jnp.zeros((rows * cols, weight.shape[3]), jnp.float32)
    for first in range(3):
        for second in range(3):
            piece = parted[
                first // 2 : first // 2 + rows,
                first % 2,
                second // 2 : second // 2 + cols,
                second % 2,
                :,
            ]
            total = total + jnp.dot(
                piece.reshape(rows * cols, chans),
                weight[first, second],
                preferred_element_type=jnp.float32,
            )
    return jax.nn.gelu(total + bias, approximate=False).reshape(rows, cols, weight.shape[3])


def project(latent, proj_weight):
    flat = jnp.dot(
        latent.reshape(-1, latent.shape[2]), proj_weight, preferred_element_type=jnp.float32
    )
    return flat.astype(jnp.bfloat16).reshape(latent.shape)


def body(
    obs_values,
    obs_band,
    obs_cell,
    obs_offset,
    sat_values,
    sat_cell,
    sat_offset,
    density_embed,
    conv1_weight,
    conv1_bias,
    conv2_weight,
    conv2_bias,
    proj_weight,
):
    bands = lax.axis_size("band")
    position_index = lax.axis_index("band")
    obs_rows, d_in = obs_values.shape
    capacity = obs_rows // 8
    band_cells = LAT_DEV * LON
    target = obs_band[:, 0]
    choose = (target[:, None] == jnp.arange(bands, dtype=jnp.int32)[None, :]).astype(jnp.int32)
    rank = jnp.cumsum(choose, axis=0) - 1
    slot = jnp.sum(rank * choose, axis=1)
    position = target * capacity + slot
    send_values = jnp.zeros((bands * capacity, d_in), jnp.bfloat16).at[position].set(obs_values)
    send_cells = jnp.full((bands * capacity,), -1, jnp.int32).at[position].set(obs_cell)
    send_offsets = jnp.zeros((bands * capacity,), jnp.int32).at[position].set(obs_offset)
    got_values, got_cells, got_offsets = (
        lax.all_to_all(
            send_values.reshape(bands, capacity, d_in),
            "band",
            split_axis=0,
            concat_axis=0,
            tiled=True,
        ),
        lax.all_to_all(
            send_cells.reshape(bands, capacity), "band", split_axis=0, concat_axis=0, tiled=True
        ),
        lax.all_to_all(
            send_offsets.reshape(bands, capacity), "band", split_axis=0, concat_axis=0, tiled=True
        ),
    )
    sat_sums, sat_density = deposit(sat_values, sat_cell, sat_offset, band_cells)
    flat_values = got_values.reshape(bands * capacity, d_in)
    flat_cells = got_cells.reshape(bands * capacity)
    flat_offsets = got_offsets.reshape(bands * capacity)
    sta_sums, sta_density = deposit(flat_values, flat_cells, flat_offsets, band_cells)
    sums = sat_sums + sta_sums
    density = sat_density + sta_density
    grid0 = sums / jnp.maximum(density, 1.0)[:, None] + density[:, None] * density_embed[None, :]
    grid0 = grid0.astype(jnp.bfloat16).reshape(LAT_DEV, LON, d_in)
    above = passed_along(grid0[-3:], "band", 1)
    hidden1 = strided(jnp.concatenate([above, grid0], axis=0), conv1_weight, conv1_bias)
    keep_rows = (jnp.arange(hidden1.shape[0]) > 0) | (position_index > 0)
    hidden1 = jnp.where(keep_rows[:, None, None], hidden1, 0.0).astype(jnp.bfloat16)
    latent = strided(hidden1, conv2_weight, conv2_bias).astype(jnp.bfloat16)
    return project(lax.all_gather(latent, "band", axis=0, tiled=True), proj_weight)


def solution(mesh):
    placed = (
        P(("member", "band"), None),
        P(("member", "band"), None),
        P(("member", "band")),
        P(("member", "band")),
        P(("member", "band"), None),
        P(("member", "band")),
        P(("member", "band")),
        P(),
        P(),
        P(),
        P(),
        P(),
        P(),
    )
    return jax.shard_map(
        body, mesh=mesh, in_specs=placed, out_specs=P("member", None, None), check_vma=False
    )
```

profile of v0, /device:TPU:0, one launch (start us, length us, event | category | flops | bytes accessed | tf_op | source)
XLA Modules:
  0.0 124.4 jit_solution(5386460355857521245)
XLA Ops:
  0.0 0.7 fusion.69
  0.7 2.3 %reduce-window.6 = s32[8,16,128]{2,1,0:T(8,128)S(1)} reduce-window(s32[8,16,128]{2,1,0:T(8,128)S(1)} %fusion.69, s32[]{:T(128)} %constant.58.clone.1), window={size=1x1x128 pad=0_0x0_0x127_0}, to_apply=%region_3.4 | reduce-window | flops 2080768 | bytes 131076 | tf_op jit(solution)/shard_map/reduce-window
  3.0 0.3 slice_reduce_fusion
  3.6 0.7 fusion.49
  4.3 0.7 compare_select_fusion.12
  5.0 8.8 %scatter_custom_fusion = s32[2048]{0:T(1024)} fusion(s32[2048]{0:T(1024)S(1)} %bitcast.206, s32[2048]{0:T(1024)} %param.19, s32[]{:T(128)} %constant.63.clone.1), kind=kCustom, calls=%fused_computation.158 | custom fusion | bytes 8704 | tf_op jit(solution)/shard_map/scatter | solution.py:96
  13.8 7.3 %all-to-all-start = ((s32[8,1,256]{2,1,0:T(1,128)}), s32[8,1,256]{2,1,0:T(1,128)S(1)}, u32[]{:S(2)}, u32[]{:S(2)}) async-start(s32[8,1,256]{2,1,0:T(1,128)} %bitcast.11), calls=%async_computation | async-start | bytes 16384 | tf_op jit(solution)/shard_map/all_to_all | solution.py:106
  21.1 0.7 exponential_convert_fusion
  21.8 8.8 %scatter_custom_fusion.1 = s32[2048]{0:T(1024)} fusion(s32[2048]{0:T(1024)S(1)} %bitcast.207, s32[2048]{0:T(1024)} %param.20, s32[]{:T(128)} %constant.58.clone.1), kind=kCustom, calls=%fused_computation.156 | custom fusion | bytes 8704 | tf_op jit(solution)/shard_map/scatter | solution.py:97
  30.6 6.0 %all-to-all-start.1 = ((s32[8,1,256]{2,1,0:T(1,128)}), s32[8,1,256]{2,1,0:T(1,128)S(1)}, u32[]{:S(2)}, u32[]{:S(2)}) async-start(s32[8,1,256]{2,1,0:T(1,128)} %bitcast.12), calls=%async_computation.1 | async-start | bytes 16384 | tf_op jit(solution)/shard_map/all_to_all | solution.py:109
  36.6 6.8 %scatter_custom_fusion.2 = bf16[2048,128]{1,0:T(8,128)(2,1)} fusion(s32[2048]{0:T(1024)S(1)} %bitcast.208, bf16[2048,128]{1,0:T(8,128)(2,1)} %param.17, bf16[]{:T(256)} %constant.66.clone.1), kind=kCustom, calls=%fused_computation.77 | custom fusion | bytes 524800 | tf_op jit(solution)/shard_map/scatter | solution.py:95
  43.4 6.1 %all-to-all-start.2 = ((bf16[8,256,128]{2,1,0:T(8,128)(2,1)}), bf16[8,256,128]{2,1,0:T(8,128)(2,1)S(1)}, u32[]{:S(2)}, u32[]{:S(2)}) async-start(bf16[8,256,128]{2,1,0:T(8,128)(2,1)} %bitcast.13), calls=%async_computation.2 | async-start | bytes 1048576 | tf_op jit(solution)/shard_map/all_to_all | solution.py:99
  49.7 11.0 %while.24 = (s32[]{:T(128)}, f32[4,512,128]{2,1,0:T(8,128)S(1)}, f32[4,512]{1,0:T(4,128)S(1)}, s32[4]{0:T(128)S(1)}, s32[2048]{0:T(1024)S(1)}, /*index=5*/bf16[2...) while((s32[]{:T(128)}, f32[4,512,128]{2,1,0:T(8,128)S(1)}, ...), condition=%wide.region_2.3_spmd, body=%wide.region_0.2_spmd.sunk | while | flops 274726912 | bytes 823413 | solution.py:35
  49.7 0.7 dynamic_slice.9
  50.3 0.7 iota_add_fusion.4
  51.0 0.8 fusion.128
  51.8 0.5 convert_reduce_fusion.4
  52.4 0.7 dynamic_slice.9
  53.1 0.7 iota_add_fusion.4
  53.8 0.8 fusion.128
  54.6 0.5 convert_reduce_fusion.4
  55.2 0.7 dynamic_slice.9
  55.8 0.7 iota_add_fusion.4
  56.5 0.8 fusion.128
  57.3 0.5 convert_reduce_fusion.4
  57.9 0.7 dynamic_slice.9
  58.6 0.7 iota_add_fusion.4
  59.3 0.8 fusion.128
  60.0 0.5 convert_reduce_fusion.4
  60.7 2.2 %all-to-all-done.2 = bf16[8,256,128]{2,1,0:T(8,128)(2,1)S(1)} async-done(((bf16[8,256,128]{2,1,0:T(8,128)(2,1)}), bf16[8,256,128]{2,1,0:T(8,128)(2,1)S(1)}, u32[]{:S(2)}, u32[]{:S(2)}) %all-to-all-start.2) | async-done | bytes 524320 | tf_op jit(solution)/shard_map/all_to_all | solution.py:99
  63.0 10.6 %while.25 = (s32[]{:T(128)}, f32[4,512,128]{2,1,0:T(8,128)S(1)}, f32[4,512]{1,0:T(4,128)S(1)}, s32[4]{0:T(128)S(1)}, s32[8,256]{1,0:T(8,128)S(1)}, /*index=5*/bf...) while((s32[]{:T(128)}, f32[4,512,128]{2,1,0:T(8,128)S(1)}, ...), condition=%wide.region_11.12_spmd, body=%wide.region_9.11_spmd.sunk | while | flops 274726912 | bytes 839797 | solution.py:35
  63.0 0.6 dynamic_slice.10
  63.6 0.6 iota_add_fusion.5
  64.3 0.8 fusion.130
  65.0 0.5 convert_reduce_fusion.5
  65.7 0.6 dynamic_slice.10
  66.2 0.6 iota_add_fusion.5
  66.9 0.8 fusion.130
  67.7 0.5 convert_reduce_fusion.5
  68.3 0.6 dynamic_slice.10
  68.9 0.6 iota_add_fusion.5
  69.5 0.8 fusion.130
  70.3 0.5 convert_reduce_fusion.5
  70.9 0.6 dynamic_slice.10
  71.5 0.6 iota_add_fusion.5
  72.2 0.8 fusion.130
  73.0 0.5 convert_reduce_fusion.5
  73.8 0.5 copy-done.4
  74.3 0.3 fusion.26
  74.6 3.6 %collective-permute-start = (bf16[3,256,128]{2,1,0:T(8,128)(2,1)S(1)}, bf16[3,256,128]{2,1,0:T(8,128)(2,1)S(1)}, u32[]{:S(2)}, u32[]{:S(2)}) collective-permute-start(bf16[3,256,128]{2,1,0:T(8,128)(2,1)S(1)} %bitcast.185), channel_id=1, source_target_pairs={{0,1},{1,2},{2,3},{3,4},{4,5},{5,6},{6,7},{8,9},{9,10},{10,11},{11... | collective-permute-start | bytes 589832 | tf_op jit(solution)/shard_map/ppermute | solution.py:13
  78.2 0.7 add_convert_fusion
  78.9 2.2 %collective-permute-done = bf16[3,256,128]{2,1,0:T(8,128)(2,1)S(1)} collective-permute-done((bf16[3,256,128]{2,1,0:T(8,128)(2,1)S(1)}, bf16[3,256,128]{2,1,0:T(8,128)(2,1)S(1)}, u32[]{:S(2)}, u32[]{:S(2)}) %collective-permute-start) | collective-permute-done | bytes 196640 | tf_op jit(solution)/shard_map/ppermute | solution.py:13
  81.1 0.2 fusion.23
  81.3 0.3 reshape.126
  81.6 3.2 %fusion.99 = (bf16[5,1,128,1,128]{4,3,2,1,0:T(2,128)(2,1)S(1)}, bf16[5,1,128,1,128]{4,3,2,1,0:T(2,128)(2,1)S(1)}, bf16[5,1,128,1,128]{4,3,2,1,0:T(2,128)(2,1)S(1...) fusion(bf16[6,2,129,2,128]{4,3,2,1,0:T(2,128)(2,1)S(1)} %reshap, ...), kind=kLoop, calls=%fused_computation.162 | loop fusion | bytes 2949120 | tf_op jit(solution)/shard_map/slice | solution.py:48
  85.1 0.8 copy-done.2
  87.4 0.3 copy-done.7
  87.7 0.9 fusion.28
  88.8 0.2 reshape.128
  89.0 0.4 fusion.100
  89.5 0.5 copy-done.1
  91.3 0.4 fusion.40
  91.7 31.6 %all_gather.3 = bf16[16,64,256]{2,1,0:T(8,128)(2,1)S(1)} all-gather(bf16[2,64,256]{2,1,0:T(8,128)(2,1)S(1)} %bitcast.200), channel_id=1, replica_groups=mesh['member'=4,'band'=8] {'band'}, dimensions={0}, use_global_device_ids=true | all-gather | bytes 589824 | tf_op jit(solution)/shard_map/all_gather | solution.py:127
  123.3 1.1 convolution_convert_fusion
  (81 shorter events, 4.1 us)
Async XLA Ops:
  0.0 123.3 %copy-start = (bf16[256,256]{1,0:T(8,128)(2,1)S(1)}, bf16[256,256]{1,0:T(8,128)(2,1)}, u32[]{:S(2)}) copy-start(bf16[256,256]{1,0:T(8,128)(2,1)} %param.29) | copy-start | bytes 393220
  13.8 16.8 %all-to-all-start = ((s32[8,1,256]{2,1,0:T(1,128)}), s32[8,1,256]{2,1,0:T(1,128)S(1)}, u32[]{:S(2)}, u32[]{:S(2)}) async-start(s32[8,1,256]{2,1,0:T(1,128)} %bitcast.11), calls=%async_computation | async-start | bytes 16384 | tf_op jit(solution)/shard_map/all_to_all | solution.py:106
  30.6 12.9 %all-to-all-start.1 = ((s32[8,1,256]{2,1,0:T(1,128)}), s32[8,1,256]{2,1,0:T(1,128)S(1)}, u32[]{:S(2)}, u32[]{:S(2)}) async-start(s32[8,1,256]{2,1,0:T(1,128)} %bitcast.12), calls=%async_computation.1 | async-start | bytes 16384 | tf_op jit(solution)/shard_map/all_to_all | solution.py:109
  43.4 6.2 %copy-start.3 = (s32[2048]{0:T(1024)S(1)}, s32[2048]{0:T(1024)}, u32[]{:S(2)}) copy-start(s32[2048]{0:T(1024)} %param.22) | copy-start | bytes 24580
  43.4 6.2 %copy-start.5 = (bf16[2048,128]{1,0:T(8,128)(2,1)S(1)}, bf16[2048,128]{1,0:T(8,128)(2,1)}, u32[]{:S(2)}) copy-start(bf16[2048,128]{1,0:T(8,128)(2,1)} %param.21) | copy-start | bytes 1572868
  43.4 19.5 %all-to-all-start.2 = ((bf16[8,256,128]{2,1,0:T(8,128)(2,1)}), bf16[8,256,128]{2,1,0:T(8,128)(2,1)S(1)}, u32[]{:S(2)}, u32[]{:S(2)}) async-start(bf16[8,256,128]{2,1,0:T(8,128)(2,1)} %bitcast.13), calls=%async_computation.2 | async-start | bytes 1048576 | tf_op jit(solution)/shard_map/all_to_all | solution.py:99
  73.6 0.7 copy-start.4
  74.6 6.5 %collective-permute-start = (bf16[3,256,128]{2,1,0:T(8,128)(2,1)S(1)}, bf16[3,256,128]{2,1,0:T(8,128)(2,1)S(1)}, u32[]{:S(2)}, u32[]{:S(2)}) collective-permute-start(bf16[3,256,128]{2,1,0:T(8,128)(2,1)S(1)} %bitcast.185), channel_id=1, source_target_pairs={{0,1},{1,2},{2,3},{3,4},{4,5},{5,6},{6,7},{8,9},{9,10},{10,11},{11... | collective-permute-start | bytes 589832 | tf_op jit(solution)/shard_map/ppermute | solution.py:13
  85.0 1.0 copy-start.2
  87.1 0.7 copy-start.7
  89.0 1.1 copy-start.1
  90.3 0.9 copy-start.6
where the time goes:
time: 125 us; the launch traced here: 124 us
  local copies, waits for them, and re-layouts  36.9 us (30%)
  blocking collectives  31.6 us (25%)
  starting transfers between devices  23 us (18%)
  other arithmetic  16.6 us (13%)
  matrix products  11.1 us (9%)
  waiting for transfers between devices  4.46 us (4%)
    all_gather x1, blocking collectives, body(): lax.all_gather(latent, 'band', axis=0, tiled=True)  31.6 us
    scatter x1, local copies, waits for them, and re-layouts, body(): jnp.full((bands * capacity,), -1, jnp.int32).at[position].set(obs_cell)  8.78 us
    scatter x1, local copies, waits for them, and re-layouts, body(): jnp.zeros((bands * capacity,), jnp.int32).at[position].set(obs_offset)  8.78 us
    all_to_all x1, starting transfers between devices, body(): lax.all_to_all(send_cells.reshape(bands, capacity), 'band', split_axis=0,...  7.28 us
    scatter x1, local copies, waits for them, and re-layouts, body(): jnp.zeros((bands * capacity, d_in), jnp.bfloat16).at[position]  6.85 us
    all_to_all x1, starting transfers between devices, body(): lax.all_to_all(send_values.reshape(bands, capacity, d_in), 'band', split_...  6.12 us
    dot_general x8, matrix products, one_block(): sums = jnp.dot(table, values, preferred_element_type=jnp.float32)  6.09 us
    all_to_all x1, starting transfers between devices, body(): lax.all_to_all(send_offsets.reshape(bands, capacity), 'band', split_axis=...  6 us
  transfers between devices with their start and end apart: 4, of which 2 were waited for; matrix products, arithmetic and copies ran while one was open for 23% of the time, Pallas kernels for 0%

commit v1 on v0

--- a/solution.py
+++ b/solution.py
@@ -5,6 +5,7 @@
 
 LAT_DEV = 8
 LON = 256
+META = 16
 
 
 def passed_along(value, axis, by):
@@ -17,8 +18,7 @@
     return jnp.exp(-offsets.astype(jnp.float32) ** 2 / 32.0).astype(jnp.bfloat16)
 
 
-def deposit(values, cells, offsets, total_cells):
-    weight = weights_of(offsets)
+def deposit(values, cells, weight, total_cells):
     block = min(512, total_cells)
     count = total_cells // block
 
@@ -67,6 +67,38 @@
     return flat.astype(jnp.bfloat16).reshape(latent.shape)
 
 
+def route(obs_values, obs_band, obs_cell, obs_offset, bands):
+    obs_rows, d_in = obs_values.shape
+    capacity = obs_rows // 8
+    slots = bands * capacity
+    target = obs_band[:, 0]
+    choose = (target[:, None] == jnp.arange(bands, dtype=jnp.int32)[None, :]).astype(jnp.bfloat16)
+    earlier = (
+        jnp.arange(obs_rows, dtype=jnp.int32)[:, None] > jnp.arange(obs_rows, dtype=jnp.int32)[None, :]
+    ).astype(jnp.bfloat16)
+    before = jnp.dot(earlier, choose, preferred_element_type=jnp.float32)
+    rank = jnp.sum(before * choose.astype(jnp.float32), axis=1).astype(jnp.int32)
+    position = target * capacity + rank
+    table = (jnp.arange(slots, dtype=jnp.int32)[:, None] == position[None, :]).astype(jnp.bfloat16)
+    sent = jnp.dot(table, obs_values, preferred_element_type=jnp.float32).astype(jnp.bfloat16)
+    meta = jnp.stack(
+        [obs_cell // 64, obs_cell % 64, obs_offset + 1], axis=0
+    ).astype(jnp.bfloat16)
+    meta_sent = jnp.dot(meta, table.T, preferred_element_type=jnp.float32).astype(jnp.bfloat16)
+    meta_sent = meta_sent.reshape(3, bands, capacity).transpose(1, 0, 2)
+    meta_sent = meta_sent.reshape(bands, 3 * capacity // d_in, d_in)
+    pad = jnp.zeros((bands, META - 3 * capacity // d_in, d_in), jnp.bfloat16)
+    packet = jnp.concatenate([sent.reshape(bands, capacity, d_in), meta_sent, pad], axis=1)
+    got = lax.all_to_all(packet, "band", split_axis=0, concat_axis=0, tiled=True)
+    got_values = got[:, :capacity, :].reshape(slots, d_in)
+    got_meta = got[:, capacity : capacity + 3 * capacity // d_in, :]
+    got_meta = got_meta.reshape(bands, 3, capacity).transpose(1, 0, 2).reshape(3, slots)
+    got_meta = got_meta.astype(jnp.int32)
+    cells = got_meta[0] * 64 + got_meta[1]
+    weight = jnp.where(got_meta[2] > 0, weights_of(got_meta[2] - 1), jnp.zeros((), jnp.bfloat16))
+    return got_values, cells, weight
+
+
 def body(
     obs_values,
     obs_band,
@@ -84,37 +116,11 @@
 ):
     bands = lax.axis_size("band")
     position_index = lax.axis_index("band")
-    obs_rows, d_in = obs_values.shape
-    capacity = obs_rows // 8
+    d_in = obs_values.shape[1]
     band_cells = LAT_DEV * LON
-    target = obs_band[:, 0]
-    choose = (target[:, None] == jnp.arange(bands, dtype=jnp.int32)[None, :]).astype(jnp.int32)
-    rank = jnp.cumsum(choose, axis=0) - 1
-    slot = jnp.sum(rank * choose, axis=1)
-    position = target * capacity + slot
-    send_values = jnp.zeros((bands * capacity, d_in), jnp.bfloat16).at[position].set(obs_values)
-    send_cells = jnp.full((bands * capacity,), -1, jnp.int32).at[position].set(obs_cell)
-    send_offsets = jnp.zeros((bands * capacity,), jnp.int32).at[position].set(obs_offset)
-    got_values, got_cells, got_offsets = (
-        lax.all_to_all(
-            send_values.reshape(bands, capacity, d_in),
-            "band",
-            split_axis=0,
-            concat_axis=0,
-            tiled=True,
-        ),
-        lax.all_to_all(
-            send_cells.reshape(bands, capacity), "band", split_axis=0, concat_axis=0, tiled=True
-        ),
-        lax.all_to_all(
-            send_offsets.reshape(bands, capacity), "band", split_axis=0, concat_axis=0, tiled=True
-        ),
-    )
-    sat_sums, sat_density = deposit(sat_values, sat_cell, sat_offset, band_cells)
-    flat_values = got_values.reshape(bands * capacity, d_in)
-    flat_cells = got_cells.reshape(bands * capacity)
-    flat_offsets = got_offsets.reshape(bands * capacity)
-    sta_sums, sta_density = deposit(flat_values, flat_cells, flat_offsets, band_cells)
+    got_values, got_cells, got_weight = route(obs_values, obs_band, obs_cell, obs_offset, bands)
+    sat_sums, sat_density = deposit(sat_values, sat_cell, weights_of(sat_offset), band_cells)
+    sta_sums, sta_density = deposit(got_values, got_cells, got_weight, band_cells)
     sums = sat_sums + sta_sums
     density = sat_density + sta_density
     grid0 = sums / jnp.maximum(density, 1.0)[:, None] + density[:, None] * density_embed[None, :]
@@ -124,7 +130,10 @@
     keep_rows = (jnp.arange(hidden1.shape[0]) > 0) | (position_index > 0)
     hidden1 = jnp.where(keep_rows[:, None, None], hidden1, 0.0).astype(jnp.bfloat16)
     latent = strided(hidden1, conv2_weight, conv2_bias).astype(jnp.bfloat16)
-    return project(lax.all_gather(latent, "band", axis=0, tiled=True), proj_weight)
+    mine = project(latent, proj_weight)
+    spread = jnp.broadcast_to(mine[None], (bands,) + mine.shape)
+    gathered = lax.all_to_all(spread, "band", split_axis=0, concat_axis=0, tiled=True)
+    return gathered.reshape((bands * mine.shape[0],) + mine.shape[1:])
 
 
 def solution(mesh):

time: 125 us -> 81.9 us (0.66)
  local copies, waits for them, and re-layouts: 36.9 us -> 13.2 us
  blocking collectives: 31.6 us -> 19.2 us
  starting transfers between devices: 23 us -> 11 us
  matrix products: 11.1 us -> 18.2 us
  other arithmetic: 16.6 us -> 11.9 us
  waiting for transfers between devices: 4.46 us -> 6.95 us
    all_gather x1 -> x0, blocking collectives: 31.6 us -> none  [body(): lax.all_gather(latent, 'band', axis=0, tiled=True)]
    scatter x3 -> x0, local copies, waits for them, and re-layouts: 24.4 us -> none  [the longest x1 8.78 us: body(): jnp.full((bands * capacity,), -1, jnp.int32).at[position].set(obs_cell)]
    all_to_all x0 -> x1, blocking collectives: none -> 19.2 us  [body(): lax.all_to_all(spread, 'band', split_axis=0, concat_axis=0, tiled=True)]
    all_to_all x3 -> x1, starting transfers between devices: 19.4 us -> 7.41 us  [route(): lax.all_to_all(packet, 'band', split_axis=0, concat_axis=0, tiled=True)]
    dot_general x0 -> x3, matrix products: none -> 8.1 us  [the longest x1 2.98 us: route(): jnp.dot(table, obs_values, preferred_element_type=jnp.float32)]
    another operation x2, other arithmetic: 2.43 us -> 0.02 us
    all_to_all x3 -> x1, waiting for transfers between devices: 2.22 us -> 4.46 us  [route(): lax.all_to_all(packet, 'band', split_axis=0, concat_axis=0, tiled=True)]
    unnamed x37 -> x47, local copies, waits for them, and re-layouts: 2.49 us -> 3.3 us
  transfers between devices with their start and end apart: 4 -> 2, of which waited for: 2 -> 2; matrix products, arithmetic and copies ran while one was open for 23% -> 14% of each run, Pallas kernels for 0% -> 0%
where the time goes in v1:
time: 81.9 us; the launch traced here: 81.4 us
  blocking collectives  19.2 us (23%)
  matrix products  18.2 us (22%)
  local copies, waits for them, and re-layouts  13.2 us (16%)
  other arithmetic  11.9 us (15%)
  starting transfers between devices  11 us (13%)
  waiting for transfers between devices  6.95 us (8%)
    all_to_all x1, blocking collectives, body(): lax.all_to_all(spread, 'band', split_axis=0, concat_axis=0, tiled=True)  19.2 us
    all_to_all x1, starting transfers between devices, route(): lax.all_to_all(packet, 'band', split_axis=0, concat_axis=0, tiled=True)  7.41 us
    dot_general x8, matrix products, one_block(): sums = jnp.dot(table, values, preferred_element_type=jnp.float32)  6.09 us
    dynamic_slice x8, local copies, waits for them, and re-layouts, deposit(): sums, density = lax.map(one_block, starts)  5.03 us
    add x8, other arithmetic, one_block(): ids = start + jnp.arange(block, dtype=jnp.int32)  5.03 us
    all_to_all x1, waiting for transfers between devices, route(): lax.all_to_all(packet, 'band', split_axis=0, concat_axis=0, tiled=True)  4.46 us
    reduce_sum x8, other arithmetic, one_block(): density = jnp.sum(table, axis=1, dtype=jnp.float32)  4.39 us
    slice x2, local copies, waits for them, and re-layouts, strided(): parted[first // 2:first // 2 + rows, first % 2, second // 2:second // 2 +...  3.59 us
  transfers between devices with their start and end apart: 2, of which 2 were waited for; matrix products, arithmetic and copies ran while one was open for 14% of the time, Pallas kernels for 0%

profile of v1, /device:TPU:0, one launch (start us, length us, event | category | flops | bytes accessed | tf_op | source)
XLA Modules:
  0.0 81.4 jit_solution(3472863240591698468)
XLA Ops:
  0.0 2.2 %fusion.30 = f32[2048]{0:T(1024)S(1)} fusion(s32[2048]{0:T(1024)} %bitcast.178), kind=kOutput, calls=%fused_computation.58 | convolution fusion | flops 71399424 | bytes 16384 | tf_op jit(solution)/shard_map/dot_general | solution.py:79
  2.4 2.9 %fusion.23 = bf16[3,2048]{1,0:T(4,128)(2,1)S(1)} fusion(s32[2048]{0:T(1024)S(1)} %convert_add_fusion, bf16[1,2048]{1,0:T(2,128)(2,1)S(1)} %stack.18, bf16[1,2048]{1,0:T(2,128)(2,1)S(1)} %stack.17, bf16[1,2048]{1,0:T(2,128)(2,1)S(1)} %stack.16), kind=kOutput, calls=%fused_computation.33 | convolution fusion | flops 29403136 | bytes 32768 | tf_op jit(solution)/shard_map/dot_general | solution.py:87
  5.3 3.0 %fusion.21 = bf16[2048,128]{1,0:T(8,128)(2,1)S(1)} fusion(bf16[2048,128]{1,0:T(8,128)(2,1)S(1)} %copy-done, s32[2048]{0:T(1024)S(1)} %convert_add_fusion), kind=kOutput, calls=%fused_computation.31 | convolution fusion | flops 1078198272 | bytes 1056768 | tf_op jit(solution)/shard_map/dot_general | solution.py:83
  8.4 1.0 %maximum_maximum_fusion = bf16[8,272,128]{2,1,0:T(8,128)(2,1)} fusion(bf16[8,6,128]{2,1,0:T(8,128)(2,1)S(1)} %reshape.133, bf16[8,256,128]{2,1,0:T(8,128)(2,1)S(1)} %bitcast.152, bf16[272]{0:T(512)(128)(2,1)S(1)} %pad.14.clone), kind=kLoop, calls=%fused_computation.63 | loop fusion | flops 1671168 | bytes 1094176 | tf_op jit(solution)/shard_map/concatenate | solution.py:91
  9.4 7.4 %all-to-all-start = ((bf16[8,272,128]{2,1,0:T(8,128)(2,1)}), bf16[8,272,128]{2,1,0:T(8,128)(2,1)S(1)}, u32[]{:S(2)}, u32[]{:S(2)}) async-start(bf16[8,272,128]{2,1,0:T(8,128)(2,1)} %maximum_maximum_fusion), calls=%async_computation | async-start | bytes 1114112 | tf_op jit(solution)/shard_map/all_to_all | solution.py:92
  16.9 10.6 %while.24 = (s32[]{:T(128)}, f32[4,512,128]{2,1,0:T(8,128)S(1)}, f32[4,512]{1,0:T(4,128)S(1)}, s32[4]{0:T(128)S(1)}, s32[2048]{0:T(1024)S(1)}, /*index=5*/bf16[2...) while((s32[]{:T(128)}, f32[4,512,128]{2,1,0:T(8,128)S(1)}, ...), condition=%wide.region_2.3_spmd, body=%wide.region_0.2_spmd.sunk | while | flops 274726912 | bytes 823413 | solution.py:35
  16.9 0.6 dynamic_slice.9
  17.5 0.6 iota_add_fusion.4
  18.2 0.8 fusion.198
  18.9 0.5 convert_reduce_fusion.4
  19.6 0.6 dynamic_slice.9
  20.2 0.6 iota_add_fusion.4
  20.8 0.8 fusion.198
  21.6 0.5 convert_reduce_fusion.4
  22.2 0.6 dynamic_slice.9
  22.8 0.6 iota_add_fusion.4
  23.5 0.8 fusion.198
  24.2 0.5 convert_reduce_fusion.4
  24.8 0.6 dynamic_slice.9
  25.5 0.6 iota_add_fusion.4
  26.1 0.8 fusion.198
  26.9 0.5 convert_reduce_fusion.4
  27.5 4.5 %all-to-all-done = bf16[8,272,128]{2,1,0:T(8,128)(2,1)S(1)} async-done(((bf16[8,272,128]{2,1,0:T(8,128)(2,1)}), bf16[8,272,128]{2,1,0:T(8,128)(2,1)S(1)}, u32[]{:S(2)}, u32[]{:S(2)}) %all-to-all-start) | async-done | bytes 557088 | tf_op jit(solution)/shard_map/all_to_all | solution.py:92
  32.2 10.6 %while.25 = (s32[]{:T(128)}, f32[4,512,128]{2,1,0:T(8,128)S(1)}, f32[4,512]{1,0:T(4,128)S(1)}, s32[4]{0:T(128)S(1)}, s32[2048]{0:T(1024)S(1)}, /*index=5*/bf16[2...) while((s32[]{:T(128)}, f32[4,512,128]{2,1,0:T(8,128)S(1)}, ...), condition=%wide.region_6.7_spmd, body=%wide.region_4.6_spmd.sunk | while | flops 274726912 | bytes 823413 | solution.py:35
  32.2 0.6 dynamic_slice.10
  32.9 0.6 iota_add_fusion.5
  33.5 0.8 fusion.200
  34.3 0.5 convert_reduce_fusion.5
  34.9 0.6 dynamic_slice.10
  35.5 0.6 iota_add_fusion.5
  36.1 0.8 fusion.200
  36.9 0.5 convert_reduce_fusion.5
  37.5 0.6 dynamic_slice.10
  38.2 0.6 iota_add_fusion.5
  38.8 0.8 fusion.200
  39.6 0.5 convert_reduce_fusion.5
  40.2 0.6 dynamic_slice.10
  40.8 0.6 iota_add_fusion.5
  41.4 0.8 fusion.200
  42.2 0.5 convert_reduce_fusion.5
  43.0 0.5 copy-done.8
  43.6 0.3 fusion.35
  43.8 3.6 %collective-permute-start = (bf16[3,256,128]{2,1,0:T(8,128)(2,1)S(1)}, bf16[3,256,128]{2,1,0:T(8,128)(2,1)S(1)}, u32[]{:S(2)}, u32[]{:S(2)}) collective-permute-start(bf16[3,256,128]{2,1,0:T(8,128)(2,1)S(1)} %bitcast.157), channel_id=1, source_target_pairs={{0,1},{1,2},{2,3},{3,4},{4,5},{5,6},{6,7},{8,9},{9,10},{10,11},{11... | collective-permute-start | bytes 589832 | tf_op jit(solution)/shard_map/ppermute | solution.py:14
  47.4 0.7 add_convert_fusion
  48.1 2.5 %collective-permute-done = bf16[3,256,128]{2,1,0:T(8,128)(2,1)S(1)} collective-permute-done((bf16[3,256,128]{2,1,0:T(8,128)(2,1)S(1)}, bf16[3,256,128]{2,1,0:T(8,128)(2,1)S(1)}, u32[]{:S(2)}, u32[]{:S(2)}) %collective-permute-start) | collective-permute-done | bytes 196640 | tf_op jit(solution)/shard_map/ppermute | solution.py:14
  50.6 0.2 fusion.32
  50.8 0.3 reshape.135
  51.1 3.2 %fusion.169 = (bf16[5,1,128,1,128]{4,3,2,1,0:T(2,128)(2,1)S(1)}, bf16[5,1,128,1,128]{4,3,2,1,0:T(2,128)(2,1)S(1)}, bf16[5,1,128,1,128]{4,3,2,1,0:T(2,128)(2,1)S(...) fusion(bf16[6,2,129,2,128]{4,3,2,1,0:T(2,128)(2,1)S(1)} %reshap, ...), kind=kLoop, calls=%fused_computation.235 | loop fusion | bytes 2949120 | tf_op jit(solution)/shard_map/slice | solution.py:48
  54.6 0.8 %copy-done.2 = bf16[3,3,128,128]{3,2,1,0:T(8,128)(2,1)S(1)} copy-done((bf16[3,3,128,128]{3,2,1,0:T(8,128)(2,1)S(1)}, bf16[3,3,128,128]{3,2,1,0:T(8,128)(2,1)}, u32[]{:S(2)}) %copy-start.2) | copy-done | bytes 294936
  55.6 0.2 convolution_add_fusion.7
  55.8 0.2 convolution_add_fusion.6
  56.0 0.2 convolution_add_fusion.5
  56.2 0.2 convolution_add_fusion.4
  56.4 0.2 convolution_add_fusion.3
  56.6 0.2 convolution_add_fusion.2
  56.8 0.2 convolution_add_fusion.1
  57.0 0.3 copy-done.12
  57.2 0.9 %fusion.37 = bf16[640,128]{1,0:T(8,128)(2,1)S(1)} fusion(f32[640,128]{1,0:T(8,128)S(1)} %convolution_add_fusion.1, bf16[640,128]{1,0:T(8,128)(2,1)S(1)} %bitcast.159, f32[128]{0:T(128)S(1)} %copy-done.12, bf16[3,3,128,128]{3,2,1,0:T(8,128)(2,1)S(1)} %copy-done.2), kind=kOutput, calls=%fused_computation.69 | convolution fusion | flops 26460160 | bytes 688640 | tf_op jit(solution)/shard_map/dot_general | solution.py:55
  58.3 0.2 reshape.137
  58.5 0.4 fusion.170
  59.0 0.5 copy-done.1
  60.8 0.6 convolution_convert_fusion
  61.4 19.2 %all_to_all.10 = bf16[8,2,64,256]{3,2,1,0:T(8,128)(2,1)S(1)} all-to-all(bf16[8,2,64,256]{3,2,1,0:T(8,128)(2,1)S(1)} %broadcast_in_dim.82), channel_id=1, replica_groups=mesh['member'=4,'band'=8] {'band'}, dimensions={0} | all-to-all | bytes 1048576 | tf_op jit(solution)/shard_map/all_to_all | solution.py:135
  80.6 0.8 copy.61
  (90 shorter events, 2.9 us)
Async XLA Ops:
  0.0 5.3 %copy-start = (bf16[2048,128]{1,0:T(8,128)(2,1)S(1)}, bf16[2048,128]{1,0:T(8,128)(2,1)}, u32[]{:S(2)}) copy-start(bf16[2048,128]{1,0:T(8,128)(2,1)} %param.17) | copy-start | bytes 1572868
  0.0 2.2 %copy-start.4 = (s32[2048,1]{0,1:T(1,128)S(1)}, s32[2048,1]{0,1:T(1,128)}, u32[]{:S(2)}) copy-start(s32[2048,1]{0,1:T(1,128)} %param.18) | copy-start | bytes 24580
  0.0 2.3 %copy-start.7 = (s32[2048]{0:T(1024)S(1)}, s32[2048]{0:T(1024)}, u32[]{:S(2)}) copy-start(s32[2048]{0:T(1024)} %param.19) | copy-start | bytes 24580
  0.0 2.3 %copy-start.5 = (s32[2048]{0:T(1024)S(1)}, s32[2048]{0:T(1024)}, u32[]{:S(2)}) copy-start(s32[2048]{0:T(1024)} %param.20) | copy-start | bytes 24580
  8.4 8.4 %copy-start.6 = (s32[2048]{0:T(1024)S(1)}, s32[2048]{0:T(1024)}, u32[]{:S(2)}) copy-start(s32[2048]{0:T(1024)} %param.23) | copy-start | bytes 24580
  9.4 7.5 %copy-start.3 = (s32[2048]{0:T(1024)S(1)}, s32[2048]{0:T(1024)}, u32[]{:S(2)}) copy-start(s32[2048]{0:T(1024)} %param.22) | copy-start | bytes 24580
  9.4 7.5 %copy-start.9 = (bf16[2048,128]{1,0:T(8,128)(2,1)S(1)}, bf16[2048,128]{1,0:T(8,128)(2,1)}, u32[]{:S(2)}) copy-start(bf16[2048,128]{1,0:T(8,128)(2,1)} %param.21) | copy-start | bytes 1572868
  9.4 22.6 %all-to-all-start = ((bf16[8,272,128]{2,1,0:T(8,128)(2,1)}), bf16[8,272,128]{2,1,0:T(8,128)(2,1)S(1)}, u32[]{:S(2)}, u32[]{:S(2)}) async-start(bf16[8,272,128]{2,1,0:T(8,128)(2,1)} %maximum_maximum_fusion), calls=%async_computation | async-start | bytes 1114112 | tf_op jit(solution)/shard_map/all_to_all | solution.py:92
  42.9 0.7 copy-start.8
  43.8 6.8 %collective-permute-start = (bf16[3,256,128]{2,1,0:T(8,128)(2,1)S(1)}, bf16[3,256,128]{2,1,0:T(8,128)(2,1)S(1)}, u32[]{:S(2)}, u32[]{:S(2)}) collective-permute-start(bf16[3,256,128]{2,1,0:T(8,128)(2,1)S(1)} %bitcast.157), channel_id=1, source_target_pairs={{0,1},{1,2},{2,3},{3,4},{4,5},{5,6},{6,7},{8,9},{9,10},{10,11},{11... | collective-permute-start | bytes 589832 | tf_op jit(solution)/shard_map/ppermute | solution.py:14
  54.5 1.0 %copy-start.2 = (bf16[3,3,128,128]{3,2,1,0:T(8,128)(2,1)S(1)}, bf16[3,3,128,128]{3,2,1,0:T(8,128)(2,1)}, u32[]{:S(2)}) copy-start(bf16[3,3,128,128]{3,2,1,0:T(8,128)(2,1)} %param.25) | copy-start | bytes 884740
  56.6 0.7 copy-start.12
  58.5 1.1 %copy-start.1 = (bf16[3,3,128,256]{3,2,1,0:T(8,128)(2,1)S(1)}, bf16[3,3,128,256]{3,2,1,0:T(8,128)(2,1)}, u32[]{:S(2)}) copy-start(bf16[3,3,128,256]{3,2,1,0:T(8,128)(2,1)} %param.27) | copy-start | bytes 1769476
  59.9 0.9 %copy-start.10 = (bf16[256,256]{1,0:T(8,128)(2,1)S(1)}, bf16[256,256]{1,0:T(8,128)(2,1)}, u32[]{:S(2)}) copy-start(bf16[256,256]{1,0:T(8,128)(2,1)} %param.29) | copy-start | bytes 393220
  59.9 0.9 %copy-start.11 = (f32[256]{0:T(256)S(1)}, f32[256]{0:T(256)}, u32[]{:S(2)}) copy-start(f32[256]{0:T(256)} %param.28) | copy-start | bytes 3076

commit v2 on v1

--- a/solution.py
+++ b/solution.py
@@ -131,8 +131,9 @@
     hidden1 = jnp.where(keep_rows[:, None, None], hidden1, 0.0).astype(jnp.bfloat16)
     latent = strided(hidden1, conv2_weight, conv2_bias).astype(jnp.bfloat16)
     mine = project(latent, proj_weight)
-    spread = jnp.broadcast_to(mine[None], (bands,) + mine.shape)
-    gathered = lax.all_to_all(spread, "band", split_axis=0, concat_axis=0, tiled=True)
+    full = jnp.zeros((bands,) + mine.shape, mine.dtype)
+    full = lax.dynamic_update_slice(full, mine[None], (position_index, 0, 0, 0))
+    gathered = lax.psum(full, "band")
     return gathered.reshape((bands * mine.shape[0],) + mine.shape[1:])
 
 

time: 81.9 us -> 152 us (1.86)
  waiting for transfers between devices: 6.95 us -> 81 us
  blocking collectives: 19.2 us -> 0 us
  between operations: 0.64 us -> 14.1 us
  local copies, waits for them, and re-layouts: 13.2 us -> 14.9 us
    psum x0 -> x1, waiting for transfers between devices: none -> 74 us  [body(): gathered = lax.psum(full, 'band')]
    all_to_all x1 -> x0, blocking collectives: 19.2 us -> none  [body(): lax.all_to_all(spread, 'band', split_axis=0, concat_axis=0, tiled=True)]
    unnamed x47 -> x49, local copies, waits for them, and re-layouts: 3.3 us -> 5.18 us
  transfers between devices with their start and end apart: 2 -> 3, of which waited for: 2 -> 3; matrix products, arithmetic and copies ran while one was open for 14% -> 7% of each run, Pallas kernels for 0% -> 0%
where the time goes in v2:
time: 152 us; the launch traced here: 151 us
  waiting for transfers between devices  81 us (53%)
  matrix products  18.2 us (12%)
  local copies, waits for them, and re-layouts  14.9 us (10%)
  between operations  14.1 us (9%)
  other arithmetic  11.9 us (8%)
  starting transfers between devices  11 us (7%)
    psum x1, waiting for transfers between devices, body(): gathered = lax.psum(full, 'band')  74 us
    all_to_all x1, starting transfers between devices, route(): lax.all_to_all(packet, 'band', split_axis=0, concat_axis=0, tiled=True)  7.41 us
    dot_general x8, matrix products, one_block(): sums = jnp.dot(table, values, preferred_element_type=jnp.float32)  6.09 us
    unnamed x49, local copies, waits for them, and re-layouts  5.18 us
    add x8, other arithmetic, one_block(): ids = start + jnp.arange(block, dtype=jnp.int32)  5.01 us
    dynamic_slice x8, local copies, waits for them, and re-layouts, deposit(): sums, density = lax.map(one_block, starts)  4.82 us
    all_to_all x1, waiting for transfers between devices, route(): lax.all_to_all(packet, 'band', split_axis=0, concat_axis=0, tiled=True)  4.57 us
    reduce_sum x8, other arithmetic, one_block(): density = jnp.sum(table, axis=1, dtype=jnp.float32)  4.39 us
  transfers between devices with their start and end apart: 3, of which 3 were waited for; matrix products, arithmetic and copies ran while one was open for 7% of the time, Pallas kernels for 0%

profile of v2, /device:TPU:0, one launch (start us, length us, event | category | flops | bytes accessed | tf_op | source)
XLA Modules:
  0.0 151.4 jit_solution(4917465896632138708)
XLA Ops:
  6.5 2.2 %fusion.30 = f32[2048]{0:T(1024)S(1)} fusion(s32[2048]{0:T(1024)} %bitcast.178), kind=kOutput, calls=%fused_computation.58 | convolution fusion | flops 71399424 | bytes 16384 | tf_op jit(solution)/shard_map/dot_general | solution.py:79
  8.9 2.9 %fusion.23 = bf16[3,2048]{1,0:T(4,128)(2,1)S(1)} fusion(s32[2048]{0:T(1024)S(1)} %convert_add_fusion, bf16[1,2048]{1,0:T(2,128)(2,1)S(1)} %stack.18, bf16[1,2048]{1,0:T(2,128)(2,1)S(1)} %stack.17, bf16[1,2048]{1,0:T(2,128)(2,1)S(1)} %stack.16), kind=kOutput, calls=%fused_computation.33 | convolution fusion | flops 29403136 | bytes 32768 | tf_op jit(solution)/shard_map/dot_general | solution.py:87
  11.8 3.0 %fusion.21 = bf16[2048,128]{1,0:T(8,128)(2,1)S(1)} fusion(bf16[2048,128]{1,0:T(8,128)(2,1)S(1)} %copy-done, s32[2048]{0:T(1024)S(1)} %convert_add_fusion), kind=kOutput, calls=%fused_computation.31 | convolution fusion | flops 1078198272 | bytes 1056768 | tf_op jit(solution)/shard_map/dot_general | solution.py:83
  14.9 1.0 maximum_maximum_fusion
  15.9 7.4 %all-to-all-start = ((bf16[8,272,128]{2,1,0:T(8,128)(2,1)}), bf16[8,272,128]{2,1,0:T(8,128)(2,1)S(1)}, u32[]{:S(2)}, u32[]{:S(2)}) async-start(bf16[8,272,128]{2,1,0:T(8,128)(2,1)} %maximum_maximum_fusion), calls=%async_computation | async-start | bytes 1114112 | tf_op jit(solution)/shard_map/all_to_all | solution.py:92
  23.5 10.4 %while.24 = (s32[]{:T(128)}, f32[4,512,128]{2,1,0:T(8,128)S(1)}, f32[4,512]{1,0:T(4,128)S(1)}, s32[4]{0:T(128)S(1)}, s32[2048]{0:T(1024)S(1)}, /*index=5*/bf16[2...) while((s32[]{:T(128)}, f32[4,512,128]{2,1,0:T(8,128)S(1)}, ...), condition=%wide.region_2.3_spmd, body=%wide.region_0.2_spmd.sunk | while | flops 274726912 | bytes 823413 | solution.py:35
  23.5 0.6 dynamic_slice.9
  24.1 0.6 iota_add_fusion.4
  24.7 0.8 fusion.198
  25.5 0.5 convert_reduce_fusion.4
  26.1 0.6 dynamic_slice.9
  26.7 0.6 iota_add_fusion.4
  27.3 0.8 fusion.198
  28.1 0.5 convert_reduce_fusion.4
  28.7 0.6 dynamic_slice.9
  29.3 0.6 iota_add_fusion.4
  29.9 0.8 fusion.198
  30.7 0.5 convert_reduce_fusion.4
  31.3 0.6 dynamic_slice.9
  31.9 0.6 iota_add_fusion.4
  32.5 0.8 fusion.198
  33.3 0.5 convert_reduce_fusion.4
  33.9 4.6 %all-to-all-done = bf16[8,272,128]{2,1,0:T(8,128)(2,1)S(1)} async-done(((bf16[8,272,128]{2,1,0:T(8,128)(2,1)}), bf16[8,272,128]{2,1,0:T(8,128)(2,1)S(1)}, u32[]{:S(2)}, u32[]{:S(2)}) %all-to-all-start) | async-done | bytes 557088 | tf_op jit(solution)/shard_map/all_to_all | solution.py:92
  38.8 10.5 %while.25 = (s32[]{:T(128)}, f32[4,512,128]{2,1,0:T(8,128)S(1)}, f32[4,512]{1,0:T(4,128)S(1)}, s32[4]{0:T(128)S(1)}, s32[2048]{0:T(1024)S(1)}, /*index=5*/bf16[2...) while((s32[]{:T(128)}, f32[4,512,128]{2,1,0:T(8,128)S(1)}, ...), condition=%wide.region_6.7_spmd, body=%wide.region_4.6_spmd.sunk | while | flops 274726912 | bytes 823413 | solution.py:35
  38.8 0.6 dynamic_slice.10
  39.4 0.6 iota_add_fusion.5
  40.0 0.8 fusion.200
  40.8 0.5 convert_reduce_fusion.5
  41.4 0.6 dynamic_slice.10
  42.0 0.6 iota_add_fusion.5
  42.7 0.8 fusion.200
  43.4 0.5 convert_reduce_fusion.5
  44.0 0.6 dynamic_slice.10
  44.7 0.6 iota_add_fusion.5
  45.3 0.8 fusion.200
  46.1 0.5 convert_reduce_fusion.5
  46.7 0.6 dynamic_slice.10
  47.3 0.6 iota_add_fusion.5
  47.9 0.8 fusion.200
  48.7 0.5 convert_reduce_fusion.5
  49.5 0.5 copy-done.9
  50.0 0.3 fusion.35
  50.3 3.6 %collective-permute-start = (bf16[3,256,128]{2,1,0:T(8,128)(2,1)S(1)}, bf16[3,256,128]{2,1,0:T(8,128)(2,1)S(1)}, u32[]{:S(2)}, u32[]{:S(2)}) collective-permute-start(bf16[3,256,128]{2,1,0:T(8,128)(2,1)S(1)} %bitcast.157), channel_id=1, source_target_pairs={{0,1},{1,2},{2,3},{3,4},{4,5},{5,6},{6,7},{8,9},{9,10},{10,11},{11... | collective-permute-start | bytes 589832 | tf_op jit(solution)/shard_map/ppermute | solution.py:14
  53.9 0.7 add_convert_fusion
  54.6 2.5 %collective-permute-done = bf16[3,256,128]{2,1,0:T(8,128)(2,1)S(1)} collective-permute-done((bf16[3,256,128]{2,1,0:T(8,128)(2,1)S(1)}, bf16[3,256,128]{2,1,0:T(8,128)(2,1)S(1)}, u32[]{:S(2)}, u32[]{:S(2)}) %collective-permute-start) | collective-permute-done | bytes 196640 | tf_op jit(solution)/shard_map/ppermute | solution.py:14
  57.1 0.2 fusion.32
  57.3 0.3 reshape.134
  57.6 3.2 %fusion.169 = (bf16[5,1,128,1,128]{4,3,2,1,0:T(2,128)(2,1)S(1)}, bf16[5,1,128,1,128]{4,3,2,1,0:T(2,128)(2,1)S(1)}, bf16[5,1,128,1,128]{4,3,2,1,0:T(2,128)(2,1)S(...) fusion(bf16[6,2,129,2,128]{4,3,2,1,0:T(2,128)(2,1)S(1)} %reshap, ...), kind=kLoop, calls=%fused_computation.236 | loop fusion | bytes 2949120 | tf_op jit(solution)/shard_map/slice | solution.py:48
  61.1 0.8 copy-done.3
  62.1 0.2 convolution_add_fusion.7
  62.3 0.2 convolution_add_fusion.6
  62.4 0.2 convolution_add_fusion.5
  62.6 0.2 convolution_add_fusion.4
  62.8 0.2 convolution_add_fusion.3
  63.2 0.2 convolution_add_fusion.1
  63.4 0.3 copy-done.13
  63.7 0.9 fusion.37
  64.7 0.2 reshape.136
  64.9 0.4 fusion.170
  65.5 0.5 copy-done.2
  67.3 0.6 convolution_convert_fusion
  67.9 0.8 copy-done.1
  68.7 74.0 %all-reduce.4.cloned.1.call-done = bf16[16,64,256]{2,1,0:T(8,128)(2,1)} async-done(((bf16[16,64,256]{2,1,0:T(8,128)(2,1)}), bf16[16,64,256]{2,1,0:T(8,128)(2,1)}) %all-reduce.4.cloned.1.call-update) | async-done | bytes 524304 | tf_op jit(solution)/shard_map/psum | solution.py:136
  142.7 1.9 %copy.62 = bf16[16,64,256]{2,1,0:T(8,128)(2,1)} copy(bf16[16,64,256]{2,1,0:T(8,128)(2,1)} %all-reduce.4.cloned.1.call-done) | data formatting | bytes 1048576
  (95 shorter events, 3.1 us)
Async XLA Ops:
  6.5 5.3 %copy-start = (bf16[2048,128]{1,0:T(8,128)(2,1)S(1)}, bf16[2048,128]{1,0:T(8,128)(2,1)}, u32[]{:S(2)}) copy-start(bf16[2048,128]{1,0:T(8,128)(2,1)} %param.17) | copy-start | bytes 1572868
  6.5 2.2 %copy-start.5 = (s32[2048,1]{0,1:T(1,128)S(1)}, s32[2048,1]{0,1:T(1,128)}, u32[]{:S(2)}) copy-start(s32[2048,1]{0,1:T(1,128)} %param.18) | copy-start | bytes 24580
  6.5 2.3 %copy-start.8 = (s32[2048]{0:T(1024)S(1)}, s32[2048]{0:T(1024)}, u32[]{:S(2)}) copy-start(s32[2048]{0:T(1024)} %param.19) | copy-start | bytes 24580
  6.5 2.3 %copy-start.6 = (s32[2048]{0:T(1024)S(1)}, s32[2048]{0:T(1024)}, u32[]{:S(2)}) copy-start(s32[2048]{0:T(1024)} %param.20) | copy-start | bytes 24580
  14.9 8.5 %copy-start.7 = (s32[2048]{0:T(1024)S(1)}, s32[2048]{0:T(1024)}, u32[]{:S(2)}) copy-start(s32[2048]{0:T(1024)} %param.23) | copy-start | bytes 24580
  15.9 7.6 %copy-start.4 = (s32[2048]{0:T(1024)S(1)}, s32[2048]{0:T(1024)}, u32[]{:S(2)}) copy-start(s32[2048]{0:T(1024)} %param.22) | copy-start | bytes 24580
  15.9 7.6 %copy-start.10 = (bf16[2048,128]{1,0:T(8,128)(2,1)S(1)}, bf16[2048,128]{1,0:T(8,128)(2,1)}, u32[]{:S(2)}) copy-start(bf16[2048,128]{1,0:T(8,128)(2,1)} %param.21) | copy-start | bytes 1572868
  15.9 22.6 %all-to-all-start = ((bf16[8,272,128]{2,1,0:T(8,128)(2,1)}), bf16[8,272,128]{2,1,0:T(8,128)(2,1)S(1)}, u32[]{:S(2)}, u32[]{:S(2)}) async-start(bf16[8,272,128]{2,1,0:T(8,128)(2,1)} %maximum_maximum_fusion), calls=%async_computation | async-start | bytes 1114112 | tf_op jit(solution)/shard_map/all_to_all | solution.py:92
  23.3 119.4 %all-reduce.4.cloned.1.call-start = ((), (), s32[]{:S(2)}) async-start(), calls=%async_computation.1 | async-start | bytes 1048576 | tf_op jit(solution)/shard_map/psum | solution.py:136
  49.4 0.7 copy-start.9
  50.3 6.8 %collective-permute-start = (bf16[3,256,128]{2,1,0:T(8,128)(2,1)S(1)}, bf16[3,256,128]{2,1,0:T(8,128)(2,1)S(1)}, u32[]{:S(2)}, u32[]{:S(2)}) collective-permute-start(bf16[3,256,128]{2,1,0:T(8,128)(2,1)S(1)} %bitcast.157), channel_id=1, source_target_pairs={{0,1},{1,2},{2,3},{3,4},{4,5},{5,6},{6,7},{8,9},{9,10},{10,11},{11... | collective-permute-start | bytes 589832 | tf_op jit(solution)/shard_map/ppermute | solution.py:14
  60.9 1.0 copy-start.3
  63.0 0.7 copy-start.13
  64.9 1.1 copy-start.2
  66.3 0.9 copy-start.11
  66.3 0.9 copy-start.12
  67.9 0.8 copy-start.1
Sparse Core Ops, SparseCore 0:
  68.8 73.8 all-reduce.3

commit v3 on v1

--- a/solution.py
+++ b/solution.py
@@ -1,6 +1,10 @@
+import functools
+
 import jax
 import jax.numpy as jnp
 from jax import lax
+from jax.experimental import pallas as pl
+from jax.experimental.pallas import tpu as pltpu
 from jax.sharding import PartitionSpec as P
 
 LAT_DEV = 8
@@ -18,22 +22,71 @@
     return jnp.exp(-offsets.astype(jnp.float32) ** 2 / 32.0).astype(jnp.bfloat16)
 
 
-def deposit(values, cells, weight, total_cells):
-    block = min(512, total_cells)
-    count = total_cells // block
-
-    def one_block(start):
-        ids = start + jnp.arange(block, dtype=jnp.int32)
-        table = jnp.where(
-            ids[:, None] == cells[None, :], weight[None, :], jnp.zeros((), jnp.bfloat16)
-        )
-        sums = jnp.dot(table, values, preferred_element_type=jnp.float32)
-        density = jnp.sum(table, axis=1, dtype=jnp.float32)
-        return (sums, density)
-
-    starts = jnp.arange(count, dtype=jnp.int32) * block
-    sums, density = lax.map(one_block, starts)
-    return (sums.reshape(total_cells, values.shape[1]), density.reshape(total_cells))
+CELL_BLOCK = 256
+OBS_CHUNK = 512
+
+
+def deposit_kernel(n_sat, n_sta, sat_v, sat_c, sat_w, sta_v, sta_c, sta_w, embed, out, acc_v, acc_d):
+    base = pl.program_id(0) * CELL_BLOCK
+    ids = base + lax.broadcasted_iota(jnp.int32, (CELL_BLOCK, OBS_CHUNK), 0)
+    ones = jnp.ones((OBS_CHUNK, acc_d.shape[1]), jnp.bfloat16)
+    acc_v[...] = jnp.zeros_like(acc_v)
+    acc_d[...] = jnp.zeros_like(acc_d)
+
+    def run(vals, cells_ref, w_ref, chunks):
+        def step(i, carry):
+            at = pl.ds(pl.multiple_of(i * OBS_CHUNK, OBS_CHUNK), OBS_CHUNK)
+            cells = cells_ref[:, at]
+            w = w_ref[:, at]
+            table = jnp.where(cells == ids, w, 0.0).astype(jnp.bfloat16)
+            acc_v[...] += jnp.dot(table, vals[at, :], preferred_element_type=jnp.float32)
+            acc_d[...] += jnp.dot(table, ones, preferred_element_type=jnp.float32)
+            return carry
+
+        lax.fori_loop(0, chunks, step, 0)
+
+    run(sat_v, sat_c, sat_w, n_sat // OBS_CHUNK)
+    run(sta_v, sta_c, sta_w, n_sta // OBS_CHUNK)
+    density = acc_d[...]
+    grid = acc_v[...] / jnp.maximum(density, 1.0) + density * embed[...]
+    out[...] = grid.astype(out.dtype)
+
+
+def deposit_all(sat_values, sat_cells, sat_weight, sta_values, sta_cells, sta_weight, embed, total_cells):
+    n_sat, d_in = sat_values.shape
+    n_sta = sta_values.shape[0]
+    whole = lambda shape: pl.BlockSpec(shape, lambda c: (0,) * len(shape))
+    flops = 4 * total_cells * (n_sat + n_sta) * d_in
+    return pl.pallas_call(
+        functools.partial(deposit_kernel, n_sat, n_sta),
+        grid=(total_cells // CELL_BLOCK,),
+        in_specs=[
+            whole((n_sat, d_in)),
+            whole((1, n_sat)),
+            whole((1, n_sat)),
+            whole((n_sta, d_in)),
+            whole((1, n_sta)),
+            whole((1, n_sta)),
+            whole((1, d_in)),
+        ],
+        out_specs=pl.BlockSpec((CELL_BLOCK, d_in), lambda c: (c, 0)),
+        out_shape=jax.ShapeDtypeStruct((total_cells, d_in), jnp.bfloat16),
+        scratch_shapes=[
+            pltpu.VMEM((CELL_BLOCK, d_in), jnp.float32),
+            pltpu.VMEM((CELL_BLOCK, d_in), jnp.float32),
+        ],
+        cost_estimate=pl.CostEstimate(
+            flops=flops, transcendentals=0, bytes_accessed=2 * (n_sat + n_sta) * (d_in + 4)
+        ),
+    )(
+        sat_values,
+        sat_cells.reshape(1, n_sat),
+        sat_weight.astype(jnp.float32).reshape(1, n_sat),
+        sta_values,
+        sta_cells.reshape(1, n_sta),
+        sta_weight.astype(jnp.float32).reshape(1, n_sta),
+        embed.reshape(1, d_in),
+    )
 
 
 def strided(padded, weight, bias):
@@ -119,12 +172,10 @@
     d_in = obs_values.shape[1]
     band_cells = LAT_DEV * LON
     got_values, got_cells, got_weight = route(obs_values, obs_band, obs_cell, obs_offset, bands)
-    sat_sums, sat_density = deposit(sat_values, sat_cell, weights_of(sat_offset), band_cells)
-    sta_sums, sta_density = deposit(got_values, got_cells, got_weight, band_cells)
-    sums = sat_sums + sta_sums
-    density = sat_density + sta_density
-    grid0 = sums / jnp.maximum(density, 1.0)[:, None] + density[:, None] * density_embed[None, :]
-    grid0 = grid0.astype(jnp.bfloat16).reshape(LAT_DEV, LON, d_in)
+    grid0 = deposit_all(
+        sat_values, sat_cell, weights_of(sat_offset), got_values, got_cells, got_weight,
+        density_embed, band_cells,
+    ).reshape(LAT_DEV, LON, d_in)
     above = passed_along(grid0[-3:], "band", 1)
     hidden1 = strided(jnp.concatenate([above, grid0], axis=0), conv1_weight, conv1_bias)
     keep_rows = (jnp.arange(hidden1.shape[0]) > 0) | (position_index > 0)

time: 81.9 us -> 95.5 us (1.17)
  Pallas kernels: 0 us -> 21.1 us
  waiting for transfers between devices: 6.95 us -> 17.8 us
  other arithmetic: 11.9 us -> 4.21 us
  matrix products: 18.2 us -> 12.2 us
  local copies, waits for them, and re-layouts: 13.2 us -> 9.16 us
    pallas_call x0 -> x1, Pallas kernels: none -> 21.1 us  [deposit_all(): pl.pallas_call(functools.partial(deposit_kernel, n_sat, n_sta), grid=(tot...]
    all_to_all x1, waiting for transfers between devices: 4.46 us -> 14.6 us  [route(): lax.all_to_all(packet, 'band', split_axis=0, concat_axis=0, tiled=True)]
    dot_general x8 -> x0, matrix products: 6.09 us -> none  [one_block(): sums = jnp.dot(table, values, preferred_element_type=jnp.float32)]
    add x10 -> x0, other arithmetic: 5.14 us -> none  [the longest x8 5.03 us: one_block(): ids = start + jnp.arange(block, dtype=jnp.int32)]
    dynamic_slice x8 -> x0, local copies, waits for them, and re-layouts: 5.03 us -> none  [deposit(): sums, density = lax.map(one_block, starts)]
    reduce_sum x8 -> x0, other arithmetic: 4.39 us -> none  [one_block(): density = jnp.sum(table, axis=1, dtype=jnp.float32)]
    concatenate x1, other arithmetic: 0.21 us -> 1.25 us  [body(): jnp.concatenate([above, grid0], axis=0)]
    unnamed x47 -> x39, local copies, waits for them, and re-layouts: 3.3 us -> 3.06 us
  transfers between devices with their start and end apart: 2 -> 2, of which waited for: 2 -> 2; matrix products, arithmetic and copies ran while one was open for 14% -> 1% of each run, Pallas kernels for 0% -> 0%
where the time goes in v3:
time: 95.5 us; the launch traced here: 95 us
  Pallas kernels  21.1 us (22%)
  blocking collectives  19.2 us (20%)
  waiting for transfers between devices  17.8 us (19%)
  matrix products  12.2 us (13%)
  starting transfers between devices  11 us (12%)
  local copies, waits for them, and re-layouts  9.16 us (10%)
  other arithmetic  4.21 us (4%)
    pallas_call x1, Pallas kernels, deposit_all(): pl.pallas_call(functools.partial(deposit_kernel, n_sat, n_sta), grid=(tot...  21.1 us
    all_to_all x1, blocking collectives, body(): lax.all_to_all(spread, 'band', split_axis=0, concat_axis=0, tiled=True)  19.2 us
    all_to_all x1, waiting for transfers between devices, route(): lax.all_to_all(packet, 'band', split_axis=0, concat_axis=0, tiled=True)  14.6 us
    all_to_all x1, starting transfers between devices, route(): lax.all_to_all(packet, 'band', split_axis=0, concat_axis=0, tiled=True)  7.41 us
    slice x2, local copies, waits for them, and re-layouts, strided(): parted[first // 2:first // 2 + rows, first % 2, second // 2:second // 2 +...  3.59 us
    ppermute x1, starting transfers between devices, passed_along(): return lax.ppermute(value, axis, pairs)  3.56 us
    dot_general x17, matrix products, strided(): jnp.dot(piece.reshape(rows * cols, chans), weight[first, second], preferr...  3.5 us
    ppermute x1, waiting for transfers between devices, passed_along(): return lax.ppermute(value, axis, pairs)  3.21 us
  transfers between devices with their start and end apart: 2, of which 2 were waited for; matrix products, arithmetic and copies ran while one was open for 1% of the time, Pallas kernels for 0%

profile of v3, /device:TPU:0, one launch (start us, length us, event | category | flops | bytes accessed | tf_op | source)
XLA Modules:
  0.0 95.0 jit_solution(1287258893825393044)
XLA Ops:
  0.0 0.0 copy-start
  0.0 0.0 copy-start.3
  0.0 0.0 copy-start.5
  0.0 0.0 copy-start.4
  0.0 2.2 %fusion.14 = f32[2048]{0:T(1024)S(1)} fusion(s32[2048]{0:T(1024)} %bitcast.140), kind=kOutput, calls=%fused_computation.36 | convolution fusion | flops 71399424 | bytes 16384 | tf_op jit(solution)/shard_map/dot_general | solution.py:132
  2.2 0.0 copy-done.3
  2.3 0.0 copy-done.5
  2.3 0.0 copy-done.4
  2.4 2.9 %fusion.7 = bf16[3,2048]{1,0:T(4,128)(2,1)S(1)} fusion(s32[2048]{0:T(1024)S(1)} %convert_add_fusion, bf16[1,2048]{1,0:T(2,128)(2,1)S(1)} %stack.18, bf16[1,2048]{1,0:T(2,128)(2,1)S(1)} %stack.17, bf16[1,2048]{1,0:T(2,128)(2,1)S(1)} %stack.16), kind=kOutput, calls=%fused_computation.11 | convolution fusion | flops 29403136 | bytes 32768 | tf_op jit(solution)/shard_map/dot_general | solution.py:140
  5.3 0.0 copy-done
  5.3 3.0 %fusion.5 = bf16[2048,128]{1,0:T(8,128)(2,1)S(1)} fusion(bf16[2048,128]{1,0:T(8,128)(2,1)S(1)} %copy-done, s32[2048]{0:T(1024)S(1)} %convert_add_fusion), kind=kOutput, calls=%fused_computation.9 | convolution fusion | flops 1078198272 | bytes 1056768 | tf_op jit(solution)/shard_map/dot_general | solution.py:136
  8.3 0.1 pad.14.clone
  8.4 1.0 %maximum_maximum_fusion = bf16[8,272,128]{2,1,0:T(8,128)(2,1)} fusion(bf16[8,6,128]{2,1,0:T(8,128)(2,1)S(1)} %reshape.82, bf16[8,256,128]{2,1,0:T(8,128)(2,1)S(1)} %bitcast.121, bf16[272]{0:T(512)(128)(2,1)S(1)} %pad.14.clone), kind=kLoop, calls=%fused_computation.40 | loop fusion | flops 1671168 | bytes 1094176 | tf_op jit(solution)/shard_map/concatenate | solution.py:144
  9.4 0.0 copy-start.6
  9.4 7.4 %all-to-all-start = ((bf16[8,272,128]{2,1,0:T(8,128)(2,1)}), bf16[8,272,128]{2,1,0:T(8,128)(2,1)S(1)}, u32[]{:S(2)}, u32[]{:S(2)}) async-start(bf16[8,272,128]{2,1,0:T(8,128)(2,1)} %maximum_maximum_fusion), calls=%async_computation | async-start | bytes 1114112 | tf_op jit(solution)/shard_map/all_to_all | solution.py:145
  16.8 0.0 copy-done.6
  16.8 0.6 fusion.119
  17.4 14.6 %all-to-all-done = bf16[8,272,128]{2,1,0:T(8,128)(2,1)S(1)} async-done(((bf16[8,272,128]{2,1,0:T(8,128)(2,1)}), bf16[8,272,128]{2,1,0:T(8,128)(2,1)S(1)}, u32[]{:S(2)}, u32[]{:S(2)}) %all-to-all-start) | async-done | bytes 557088 | tf_op jit(solution)/shard_map/all_to_all | solution.py:145
  32.0 0.6 slice_add_fusion
  32.6 0.6 convert.18.sta_w
  33.2 0.8 slice.176
  34.1 21.1 %shard_map.127 = bf16[2048,128]{1,0:T(8,128)(2,1)} custom-call(bf16[2048,128]{1,0:T(8,128)(2,1)} %sat_v.1, s32[1,2048]{1,0:T(1,128)} %bitcast.144, f32[1,2048]{1,0:T(1,128)} %bitcast.143, bf16[2048,128]{1,0:T(8,128)(2,1)} %bitcast.122, s32[1,2048]{1,0:T(1,128)} %bitcast.142, f32[1,2048]{1,0:T(1,128)} %convert.18.sta_w, f32[1,128]{1,0:T(1,128)} %bitcast.145), custom_call_target="tpu_custom_call" | custom-call | flops 4294967296 | bytes 1081344 | tf_op jit(solution)/shard_map/pallas_call | solution.py:60
  55.2 0.9 slice.181
  56.1 3.6 %collective-permute-start = (bf16[3,256,128]{2,1,0:T(8,128)(2,1)S(1)}, bf16[3,256,128]{2,1,0:T(8,128)(2,1)S(1)}, u32[]{:S(2)}, u32[]{:S(2)}) collective-permute-start(bf16[3,256,128]{2,1,0:T(8,128)(2,1)S(1)} %bitcast.123), channel_id=1, source_target_pairs={{0,1},{1,2},{2,3},{3,4},{4,5},{5,6},{6,7},{8,9},{9,10},{10,11},{11... | collective-permute-start | bytes 589832 | tf_op jit(solution)/shard_map/ppermute | solution.py:18
  59.7 3.2 %collective-permute-done = bf16[3,256,128]{2,1,0:T(8,128)(2,1)S(1)} collective-permute-done((bf16[3,256,128]{2,1,0:T(8,128)(2,1)S(1)}, bf16[3,256,128]{2,1,0:T(8,128)(2,1)S(1)}, u32[]{:S(2)}, u32[]{:S(2)}) %collective-permute-start) | collective-permute-done | bytes 196640 | tf_op jit(solution)/shard_map/ppermute | solution.py:18
  62.9 1.2 %fusion.16 = bf16[12,258,128]{2,1,0:T(8,128)(2,1)S(1)} fusion(bf16[8,256,128]{2,1,0:T(8,128)(2,1)} %bitcast.112, bf16[3,256,128]{2,1,0:T(8,128)(2,1)S(1)} %collective-permute-done), kind=kLoop, calls=%fused_computation.38 | loop fusion | flops 5151744 | bytes 1513472 | tf_op jit(solution)/shard_map/concatenate | solution.py:180
  64.2 0.3 reshape.86
  64.4 3.2 %fusion.151 = (bf16[5,1,128,1,128]{4,3,2,1,0:T(2,128)(2,1)S(1)}, bf16[5,1,128,1,128]{4,3,2,1,0:T(2,128)(2,1)S(1)}, bf16[5,1,128,1,128]{4,3,2,1,0:T(2,128)(2,1)S(...) fusion(bf16[6,2,129,2,128]{4,3,2,1,0:T(2,128)(2,1)S(1)} %reshape.86), kind=kLoop, calls=%fused_computation.206 | loop fusion | bytes 2949120 | tf_op jit(solution)/shard_map/slice | solution.py:101
  67.8 0.0 copy-start.2
  67.9 0.9 copy-done.2
  68.8 0.2 fusion.98
  69.0 0.2 convolution_add_fusion.7
  69.2 0.2 convolution_add_fusion.6
  69.4 0.2 convolution_add_fusion.5
  69.5 0.2 convolution_add_fusion.4
  69.7 0.2 convolution_add_fusion.3
  69.9 0.0 copy-start.9
  69.9 0.2 convolution_add_fusion.2
  70.1 0.2 convolution_add_fusion.1
  70.3 0.3 copy-done.9
  70.6 0.9 fusion.19
  71.4 0.1 select_convert_fusion
  71.6 0.2 reshape.88
  71.8 0.0 copy-start.1
  71.9 0.4 fusion.152
  72.4 0.5 copy-done.1
  72.9 0.1 fusion.46
  73.1 0.2 convolution_add_fusion.15
  73.2 0.1 convolution_add_fusion.14
  73.4 0.1 convolution_add_fusion.13
  73.5 0.0 copy-start.7
  73.5 0.0 copy-start.8
  73.5 0.1 convolution_add_fusion.12
  73.7 0.1 convolution_add_fusion.11
  73.8 0.1 convolution_add_fusion.10
  74.0 0.1 convolution_add_fusion.9
  74.1 0.3 copy-done.7
  74.4 0.0 copy-done.8
  74.4 0.6 convolution_convert_fusion
  75.0 0.1 broadcast_in_dim.39
  75.0 19.2 %all_to_all.10 = bf16[8,2,64,256]{3,2,1,0:T(8,128)(2,1)S(1)} all-to-all(bf16[8,2,64,256]{3,2,1,0:T(8,128)(2,1)S(1)} %broadcast_in_dim.39), channel_id=1, replica_groups=mesh['member'=4,'band'=8] {'band'}, dimensions={0} | all-to-all | bytes 1048576 | tf_op jit(solution)/shard_map/all_to_all | solution.py:186
  94.2 0.8 copy.36
  (31 shorter events, 0.5 us)
Async XLA Ops:
  0.0 5.3 %copy-start = (bf16[2048,128]{1,0:T(8,128)(2,1)S(1)}, bf16[2048,128]{1,0:T(8,128)(2,1)}, u32[]{:S(2)}) copy-start(bf16[2048,128]{1,0:T(8,128)(2,1)} %param.13) | copy-start | bytes 1572868
  0.0 2.2 %copy-start.3 = (s32[2048,1]{0,1:T(1,128)S(1)}, s32[2048,1]{0,1:T(1,128)}, u32[]{:S(2)}) copy-start(s32[2048,1]{0,1:T(1,128)} %param.14) | copy-start | bytes 24580
  0.0 2.3 %copy-start.5 = (s32[2048]{0:T(1024)S(1)}, s32[2048]{0:T(1024)}, u32[]{:S(2)}) copy-start(s32[2048]{0:T(1024)} %param.15) | copy-start | bytes 24580
  0.0 2.3 %copy-start.4 = (s32[2048]{0:T(1024)S(1)}, s32[2048]{0:T(1024)}, u32[]{:S(2)}) copy-start(s32[2048]{0:T(1024)} %param.16) | copy-start | bytes 24580
  9.4 7.4 %copy-start.6 = (s32[2048]{0:T(1024)S(1)}, s32[2048]{0:T(1024)}, u32[]{:S(2)}) copy-start(s32[2048]{0:T(1024)} %param.19) | copy-start | bytes 24580
  9.4 22.6 %all-to-all-start = ((bf16[8,272,128]{2,1,0:T(8,128)(2,1)}), bf16[8,272,128]{2,1,0:T(8,128)(2,1)S(1)}, u32[]{:S(2)}, u32[]{:S(2)}) async-start(bf16[8,272,128]{2,1,0:T(8,128)(2,1)} %maximum_maximum_fusion), calls=%async_computation | async-start | bytes 1114112 | tf_op jit(solution)/shard_map/all_to_all | solution.py:145
  56.1 6.8 %collective-permute-start = (bf16[3,256,128]{2,1,0:T(8,128)(2,1)S(1)}, bf16[3,256,128]{2,1,0:T(8,128)(2,1)S(1)}, u32[]{:S(2)}, u32[]{:S(2)}) collective-permute-start(bf16[3,256,128]{2,1,0:T(8,128)(2,1)S(1)} %bitcast.123), channel_id=1, source_target_pairs={{0,1},{1,2},{2,3},{3,4},{4,5},{5,6},{6,7},{8,9},{9,10},{10,11},{11... | collective-permute-start | bytes 589832 | tf_op jit(solution)/shard_map/ppermute | solution.py:18
  67.8 1.0 %copy-start.2 = (bf16[3,3,128,128]{3,2,1,0:T(8,128)(2,1)S(1)}, bf16[3,3,128,128]{3,2,1,0:T(8,128)(2,1)}, u32[]{:S(2)}) copy-start(bf16[3,3,128,128]{3,2,1,0:T(8,128)(2,1)} %param.21) | copy-start | bytes 884740
  69.9 0.7 copy-start.9
  71.8 1.1 %copy-start.1 = (bf16[3,3,128,256]{3,2,1,0:T(8,128)(2,1)S(1)}, bf16[3,3,128,256]{3,2,1,0:T(8,128)(2,1)}, u32[]{:S(2)}) copy-start(bf16[3,3,128,256]{3,2,1,0:T(8,128)(2,1)} %param.23) | copy-start | bytes 1769476
  73.5 0.9 copy-start.7
  73.5 0.9 copy-start.8

commit v4 on v1

--- a/solution.py
+++ b/solution.py
@@ -1,6 +1,10 @@
+import functools
+
 import jax
 import jax.numpy as jnp
 from jax import lax
+from jax.experimental import pallas as pl
+from jax.experimental.pallas import tpu as pltpu
 from jax.sharding import PartitionSpec as P
 
 LAT_DEV = 8
@@ -18,22 +22,70 @@
     return jnp.exp(-offsets.astype(jnp.float32) ** 2 / 32.0).astype(jnp.bfloat16)
 
 
-def deposit(values, cells, weight, total_cells):
-    block = min(512, total_cells)
-    count = total_cells // block
-
-    def one_block(start):
-        ids = start + jnp.arange(block, dtype=jnp.int32)
-        table = jnp.where(
-            ids[:, None] == cells[None, :], weight[None, :], jnp.zeros((), jnp.bfloat16)
-        )
-        sums = jnp.dot(table, values, preferred_element_type=jnp.float32)
-        density = jnp.sum(table, axis=1, dtype=jnp.float32)
-        return (sums, density)
-
-    starts = jnp.arange(count, dtype=jnp.int32) * block
-    sums, density = lax.map(one_block, starts)
-    return (sums.reshape(total_cells, values.shape[1]), density.reshape(total_cells))
+CELL_BLOCK = 256
+OBS_CHUNK = 2048
+
+
+def deposit_rows(v_ref, c_ref, w_ref, aug, block):
+    n, d_in = v_ref.shape
+    aug[:, :d_in] = v_ref[...]
+    aug[:, d_in:] = jnp.ones((n, aug.shape[1] - d_in), jnp.bfloat16)
+    chunk = min(n, OBS_CHUNK)
+    ids = lax.broadcasted_iota(jnp.int32, (CELL_BLOCK, chunk), 0).astype(jnp.float32)
+    ids = ids.astype(jnp.bfloat16)
+    base = block * CELL_BLOCK
+    total = jnp.zeros((CELL_BLOCK, aug.shape[1]), jnp.float32)
+    for start in range(0, n, chunk):
+        rel = c_ref[:, start : start + chunk] - base
+        rel = jnp.where((rel >= 0) & (rel < CELL_BLOCK), rel, -1).astype(jnp.float32)
+        w = w_ref[:, start : start + chunk].astype(jnp.bfloat16)
+        table = jnp.where(rel.astype(jnp.bfloat16) == ids, w, jnp.zeros((), jnp.bfloat16))
+        total = total + jnp.dot(table, aug[start : start + chunk, :], preferred_element_type=jnp.float32)
+    return total
+
+
+def sat_kernel(v_ref, c_ref, w_ref, out, aug):
+    block = pl.program_id(0)
+    out[...] = deposit_rows(v_ref, c_ref, w_ref, aug, block)
+
+
+def station_kernel(acc, v_ref, c_ref, w_ref, embed, out, aug):
+    block = pl.program_id(0)
+    total = acc[...] + deposit_rows(v_ref, c_ref, w_ref, aug, block)
+    d_in = out.shape[1]
+    sums = total[:, :d_in]
+    density = total[:, d_in:]
+    grid = sums / jnp.maximum(density, 1.0) + density * embed[...]
+    out[...] = grid.astype(out.dtype)
+
+
+def whole(shape):
+    return pl.BlockSpec(shape, lambda c: (0,) * len(shape))
+
+
+def deposit_call(kernel, acc, values, cells, weight, extra, out_dtype, total_cells):
+    n, d_in = values.shape
+    wide = 2 * d_in
+    ins = [values, cells.reshape(1, n), weight.astype(jnp.float32).reshape(1, n)]
+    specs = [whole((n, d_in)), whole((1, n)), whole((1, n))]
+    if acc is not None:
+        ins = [acc] + ins
+        specs = [pl.BlockSpec((CELL_BLOCK, wide), lambda c: (c, 0))] + specs
+    for e in extra:
+        ins.append(e)
+        specs.append(whole(e.shape))
+    out_cols = wide if out_dtype == jnp.float32 else d_in
+    return pl.pallas_call(
+        kernel,
+        grid=(total_cells // CELL_BLOCK,),
+        in_specs=specs,
+        out_specs=pl.BlockSpec((CELL_BLOCK, out_cols), lambda c: (c, 0)),
+        out_shape=jax.ShapeDtypeStruct((total_cells, out_cols), out_dtype),
+        scratch_shapes=[pltpu.VMEM((n, wide), jnp.bfloat16)],
+        cost_estimate=pl.CostEstimate(
+            flops=2 * total_cells * n * wide, transcendentals=0, bytes_accessed=2 * n * (d_in + 4)
+        ),
+    )(*ins)
 
 
 def strided(padded, weight, bias):
@@ -119,12 +171,13 @@
     d_in = obs_values.shape[1]
     band_cells = LAT_DEV * LON
     got_values, got_cells, got_weight = route(obs_values, obs_band, obs_cell, obs_offset, bands)
-    sat_sums, sat_density = deposit(sat_values, sat_cell, weights_of(sat_offset), band_cells)
-    sta_sums, sta_density = deposit(got_values, got_cells, got_weight, band_cells)
-    sums = sat_sums + sta_sums
-    density = sat_density + sta_density
-    grid0 = sums / jnp.maximum(density, 1.0)[:, None] + density[:, None] * density_embed[None, :]
-    grid0 = grid0.astype(jnp.bfloat16).reshape(LAT_DEV, LON, d_in)
+    sat_acc = deposit_call(
+        sat_kernel, None, sat_values, sat_cell, weights_of(sat_offset), (), jnp.float32, band_cells
+    )
+    grid0 = deposit_call(
+        station_kernel, sat_acc, got_values, got_cells, got_weight,
+        (density_embed.reshape(1, d_in),), jnp.bfloat16, band_cells,
+    ).reshape(LAT_DEV, LON, d_in)
     above = passed_along(grid0[-3:], "band", 1)
     hidden1 = strided(jnp.concatenate([above, grid0], axis=0), conv1_weight, conv1_bias)
     keep_rows = (jnp.arange(hidden1.shape[0]) > 0) | (position_index > 0)

time: 81.9 us -> 80.8 us (0.987)
  Pallas kernels: 0 us -> 14 us
  other arithmetic: 11.9 us -> 4.25 us
  matrix products: 18.2 us -> 12.1 us
  local copies, waits for them, and re-layouts: 13.2 us -> 8.06 us
  waiting for transfers between devices: 6.95 us -> 11.3 us
    pallas_call x0 -> x2, Pallas kernels: none -> 14 us  [deposit_call(): pl.pallas_call(kernel, grid=(total_cells // CELL_BLOCK,), in_specs=specs,...]
    dot_general x8 -> x0, matrix products: 6.09 us -> none  [one_block(): sums = jnp.dot(table, values, preferred_element_type=jnp.float32)]
    add x10 -> x0, other arithmetic: 5.14 us -> none  [the longest x8 5.03 us: one_block(): ids = start + jnp.arange(block, dtype=jnp.int32)]
    dynamic_slice x8 -> x0, local copies, waits for them, and re-layouts: 5.03 us -> none  [deposit(): sums, density = lax.map(one_block, starts)]
    reduce_sum x8 -> x0, other arithmetic: 4.39 us -> none  [one_block(): density = jnp.sum(table, axis=1, dtype=jnp.float32)]
    all_to_all x1, waiting for transfers between devices: 4.46 us -> 8.07 us  [route(): lax.all_to_all(packet, 'band', split_axis=0, concat_axis=0, tiled=True)]
    unnamed x47 -> x39, local copies, waits for them, and re-layouts: 3.3 us -> 1.96 us
    concatenate x1, other arithmetic: 0.21 us -> 1.25 us  [body(): jnp.concatenate([above, grid0], axis=0)]
  transfers between devices with their start and end apart: 2 -> 2, of which waited for: 2 -> 2; matrix products, arithmetic and copies ran while one was open for 14% -> 1% of each run, Pallas kernels for 0% -> 8%
where the time goes in v4:
time: 80.8 us; the launch traced here: 80.2 us
  blocking collectives  19.2 us (24%)
  Pallas kernels  14 us (17%)
  matrix products  12.1 us (15%)
  waiting for transfers between devices  11.3 us (14%)
  starting transfers between devices  10.8 us (13%)
  local copies, waits for them, and re-layouts  8.06 us (10%)
  other arithmetic  4.25 us (5%)
    all_to_all x1, blocking collectives, body(): lax.all_to_all(spread, 'band', split_axis=0, concat_axis=0, tiled=True)  19.2 us
    pallas_call x2, Pallas kernels, deposit_call(): pl.pallas_call(kernel, grid=(total_cells // CELL_BLOCK,), in_specs=specs,...  14 us
    all_to_all x1, waiting for transfers between devices, route(): lax.all_to_all(packet, 'band', split_axis=0, concat_axis=0, tiled=True)  8.07 us
    all_to_all x1, starting transfers between devices, route(): lax.all_to_all(packet, 'band', split_axis=0, concat_axis=0, tiled=True)  7.28 us
    slice x2, local copies, waits for them, and re-layouts, strided(): parted[first // 2:first // 2 + rows, first % 2, second // 2:second // 2 +...  3.59 us
    ppermute x1, starting transfers between devices, passed_along(): return lax.ppermute(value, axis, pairs)  3.56 us
    dot_general x17, matrix products, strided(): jnp.dot(piece.reshape(rows * cols, chans), weight[first, second], preferr...  3.49 us
    ppermute x1, waiting for transfers between devices, passed_along(): return lax.ppermute(value, axis, pairs)  3.21 us
  transfers between devices with their start and end apart: 2, of which 2 were waited for; matrix products, arithmetic and copies ran while one was open for 1% of the time, Pallas kernels for 8%

profile of v4, /device:TPU:0, one launch (start us, length us, event | category | flops | bytes accessed | tf_op | source)
XLA Modules:
  0.0 80.2 jit_solution(14675920045257542260)
XLA Ops:
  0.0 0.0 copy-start
  0.0 0.0 copy-start.3
  0.0 0.0 copy-start.5
  0.0 0.0 copy-start.4
  0.0 2.2 %fusion.14 = f32[2048]{0:T(1024)S(1)} fusion(s32[2048]{0:T(1024)} %bitcast.140), kind=kOutput, calls=%fused_computation.36 | convolution fusion | flops 71399424 | bytes 16384 | tf_op jit(solution)/shard_map/dot_general | solution.py:131
  2.2 0.0 copy-done.3
  2.3 0.0 copy-done.5
  2.3 0.0 copy-done.4
  2.4 2.9 %fusion.7 = bf16[3,2048]{1,0:T(4,128)(2,1)S(1)} fusion(s32[2048]{0:T(1024)S(1)} %convert_add_fusion, bf16[1,2048]{1,0:T(2,128)(2,1)S(1)} %stack.18, bf16[1,2048]{1,0:T(2,128)(2,1)S(1)} %stack.17, bf16[1,2048]{1,0:T(2,128)(2,1)S(1)} %stack.16), kind=kOutput, calls=%fused_computation.11 | convolution fusion | flops 29403136 | bytes 32768 | tf_op jit(solution)/shard_map/dot_general | solution.py:139
  5.3 0.0 copy-done
  5.3 3.0 %fusion.5 = bf16[2048,128]{1,0:T(8,128)(2,1)S(1)} fusion(bf16[2048,128]{1,0:T(8,128)(2,1)S(1)} %copy-done, s32[2048]{0:T(1024)S(1)} %convert_add_fusion), kind=kOutput, calls=%fused_computation.9 | convolution fusion | flops 1078198272 | bytes 1056768 | tf_op jit(solution)/shard_map/dot_general | solution.py:135
  8.3 0.0 copy-start.6
  8.3 0.1 pad.14.clone
  8.4 1.0 %maximum_maximum_fusion = bf16[8,272,128]{2,1,0:T(8,128)(2,1)} fusion(bf16[8,6,128]{2,1,0:T(8,128)(2,1)S(1)} %reshape.82, bf16[8,256,128]{2,1,0:T(8,128)(2,1)S(1)} %bitcast.121, bf16[272]{0:T(512)(128)(2,1)S(1)} %pad.14.clone), kind=kLoop, calls=%fused_computation.40 | loop fusion | flops 1671168 | bytes 1094176 | tf_op jit(solution)/shard_map/concatenate | solution.py:143
  9.4 7.3 %all-to-all-start = ((bf16[8,272,128]{2,1,0:T(8,128)(2,1)}), bf16[8,272,128]{2,1,0:T(8,128)(2,1)S(1)}, u32[]{:S(2)}, u32[]{:S(2)}) async-start(bf16[8,272,128]{2,1,0:T(8,128)(2,1)} %maximum_maximum_fusion), calls=%async_computation | async-start | bytes 1114112 | tf_op jit(solution)/shard_map/all_to_all | solution.py:144
  16.7 0.0 copy-done.6
  16.7 0.6 fusion.119
  17.3 6.5 %shard_map.127.acc = f32[2048,256]{1,0:T(8,128)} custom-call(bf16[2048,128]{1,0:T(8,128)(2,1)} %v_ref.1, s32[1,2048]{1,0:T(1,128)} %bitcast.144, f32[1,2048]{1,0:T(1,128)} %bitcast.143), custom_call_target="tpu_custom_call" | custom-call | flops 2147483648 | bytes 540672 | tf_op jit(solution)/shard_map/pallas_call | solution.py:78
  23.8 8.1 %all-to-all-done = bf16[8,272,128]{2,1,0:T(8,128)(2,1)S(1)} async-done(((bf16[8,272,128]{2,1,0:T(8,128)(2,1)}), bf16[8,272,128]{2,1,0:T(8,128)(2,1)S(1)}, u32[]{:S(2)}, u32[]{:S(2)}) %all-to-all-start) | async-done | bytes 557088 | tf_op jit(solution)/shard_map/all_to_all | solution.py:144
  31.9 0.6 slice_add_fusion
  32.5 0.6 convert.18.w_ref
  33.1 0.8 %slice.176 = bf16[8,256,128]{2,1,0:T(8,128)(2,1)} slice(bf16[8,272,128]{2,1,0:T(8,128)(2,1)S(1)} %all-to-all-done), slice={[0:8], [0:256], [0:128]} | slice | bytes 1048576 | tf_op jit(solution)/shard_map/slice | solution.py:145
  34.0 7.5 %shard_map.128 = bf16[2048,128]{1,0:T(8,128)(2,1)} custom-call(f32[2048,256]{1,0:T(8,128)} %shard_map.127.acc, bf16[2048,128]{1,0:T(8,128)(2,1)} %bitcast.122, s32[1,2048]{1,0:T(1,128)} %bitcast.142, f32[1,2048]{1,0:T(1,128)} %convert.18.w_ref, f32[1,128]{1,0:T(1,128)} %bitcast.145), custom_call_target="tpu_custom_call" | custom-call | flops 2147483648 | bytes 540672 | tf_op jit(solution)/shard_map/pallas_call | solution.py:78
  41.5 0.9 %slice.181 = bf16[768,128]{1,0:T(8,128)(2,1)S(1)} slice(bf16[2048,128]{1,0:T(8,128)(2,1)} %shard_map.128), slice={[1280:2048], [0:128]} | slice | bytes 393216 | tf_op jit(solution)/shard_map/slice | solution.py:181
  42.4 3.6 %collective-permute-start = (bf16[3,256,128]{2,1,0:T(8,128)(2,1)S(1)}, bf16[3,256,128]{2,1,0:T(8,128)(2,1)S(1)}, u32[]{:S(2)}, u32[]{:S(2)}) collective-permute-start(bf16[3,256,128]{2,1,0:T(8,128)(2,1)S(1)} %bitcast.123), channel_id=1, source_target_pairs={{0,1},{1,2},{2,3},{3,4},{4,5},{5,6},{6,7},{8,9},{9,10},{10,11},{11... | collective-permute-start | bytes 589832 | tf_op jit(solution)/shard_map/ppermute | solution.py:18
  46.0 3.2 %collective-permute-done = bf16[3,256,128]{2,1,0:T(8,128)(2,1)S(1)} collective-permute-done((bf16[3,256,128]{2,1,0:T(8,128)(2,1)S(1)}, bf16[3,256,128]{2,1,0:T(8,128)(2,1)S(1)}, u32[]{:S(2)}, u32[]{:S(2)}) %collective-permute-start) | collective-permute-done | bytes 196640 | tf_op jit(solution)/shard_map/ppermute | solution.py:18
  49.2 1.2 %fusion.16 = bf16[12,258,128]{2,1,0:T(8,128)(2,1)S(1)} fusion(bf16[8,256,128]{2,1,0:T(8,128)(2,1)} %bitcast.112, bf16[3,256,128]{2,1,0:T(8,128)(2,1)S(1)} %collective-permute-done), kind=kLoop, calls=%fused_computation.38 | loop fusion | flops 5151744 | bytes 1513472 | tf_op jit(solution)/shard_map/concatenate | solution.py:182
  50.5 0.3 reshape.86
  50.7 3.2 %fusion.151 = (bf16[5,1,128,1,128]{4,3,2,1,0:T(2,128)(2,1)S(1)}, bf16[5,1,128,1,128]{4,3,2,1,0:T(2,128)(2,1)S(1)}, bf16[5,1,128,1,128]{4,3,2,1,0:T(2,128)(2,1)S(...) fusion(bf16[6,2,129,2,128]{4,3,2,1,0:T(2,128)(2,1)S(1)} %reshape.86), kind=kLoop, calls=%fused_computation.206 | loop fusion | bytes 2949120 | tf_op jit(solution)/shard_map/slice | solution.py:100
  54.0 0.0 copy-start.2
  54.3 0.7 copy-done.2
  55.0 0.2 fusion.98
  55.2 0.2 convolution_add_fusion.7
  55.3 0.2 convolution_add_fusion.6
  55.5 0.2 convolution_add_fusion.5
  55.7 0.0 copy-start.9
  55.7 0.2 convolution_add_fusion.4
  55.9 0.2 convolution_add_fusion.3
  56.1 0.2 convolution_add_fusion.2
  56.3 0.2 convolution_add_fusion.1
  56.5 0.0 copy-done.9
  56.5 0.9 %fusion.19 = bf16[640,128]{1,0:T(8,128)(2,1)S(1)} fusion(f32[640,128]{1,0:T(8,128)S(1)} %convolution_add_fusion.1, bf16[640,128]{1,0:T(8,128)(2,1)S(1)} %bitcast.125, f32[128]{0:T(128)S(1)} %copy-done.9, bf16[3,3,128,128]{3,2,1,0:T(8,128)(2,1)S(1)} %copy-done.2), kind=kOutput, calls=%fused_computation.43 | convolution fusion | flops 26460160 | bytes 688640 | tf_op jit(solution)/shard_map/dot_general | solution.py:107
  57.4 0.0 copy-start.1
  57.4 0.1 select_convert_fusion
  57.5 0.2 reshape.88
  57.8 0.4 fusion.152
  58.2 0.0 copy-start.7
  58.2 0.0 copy-start.8
  58.3 0.1 copy-done.1
  58.4 0.1 fusion.46
  58.6 0.2 convolution_add_fusion.15
  58.7 0.1 convolution_add_fusion.14
  58.9 0.1 convolution_add_fusion.13
  59.0 0.1 convolution_add_fusion.12
  59.2 0.1 convolution_add_fusion.11
  59.3 0.1 convolution_add_fusion.10
  59.5 0.1 convolution_add_fusion.9
  59.6 0.0 copy-done.7
  59.6 0.0 copy-done.8
  59.7 0.6 convolution_convert_fusion
  60.2 0.1 broadcast_in_dim.39
  60.3 19.2 %all_to_all.10 = bf16[8,2,64,256]{3,2,1,0:T(8,128)(2,1)S(1)} all-to-all(bf16[8,2,64,256]{3,2,1,0:T(8,128)(2,1)S(1)} %broadcast_in_dim.39), channel_id=1, replica_groups=mesh['member'=4,'band'=8] {'band'}, dimensions={0} | all-to-all | bytes 1048576 | tf_op jit(solution)/shard_map/all_to_all | solution.py:188
  79.5 0.8 copy.36
  (31 shorter events, 0.5 us)
Async XLA Ops:
  0.0 5.3 %copy-start = (bf16[2048,128]{1,0:T(8,128)(2,1)S(1)}, bf16[2048,128]{1,0:T(8,128)(2,1)}, u32[]{:S(2)}) copy-start(bf16[2048,128]{1,0:T(8,128)(2,1)} %param.13) | copy-start | bytes 1572868
  0.0 2.2 %copy-start.3 = (s32[2048,1]{0,1:T(1,128)S(1)}, s32[2048,1]{0,1:T(1,128)}, u32[]{:S(2)}) copy-start(s32[2048,1]{0,1:T(1,128)} %param.14) | copy-start | bytes 24580
  0.0 2.3 %copy-start.5 = (s32[2048]{0:T(1024)S(1)}, s32[2048]{0:T(1024)}, u32[]{:S(2)}) copy-start(s32[2048]{0:T(1024)} %param.15) | copy-start | bytes 24580
  0.0 2.3 %copy-start.4 = (s32[2048]{0:T(1024)S(1)}, s32[2048]{0:T(1024)}, u32[]{:S(2)}) copy-start(s32[2048]{0:T(1024)} %param.16) | copy-start | bytes 24580
  8.3 8.4 %copy-start.6 = (s32[2048]{0:T(1024)S(1)}, s32[2048]{0:T(1024)}, u32[]{:S(2)}) copy-start(s32[2048]{0:T(1024)} %param.19) | copy-start | bytes 24580
  9.4 22.5 %all-to-all-start = ((bf16[8,272,128]{2,1,0:T(8,128)(2,1)}), bf16[8,272,128]{2,1,0:T(8,128)(2,1)S(1)}, u32[]{:S(2)}, u32[]{:S(2)}) async-start(bf16[8,272,128]{2,1,0:T(8,128)(2,1)} %maximum_maximum_fusion), calls=%async_computation | async-start | bytes 1114112 | tf_op jit(solution)/shard_map/all_to_all | solution.py:144
  42.4 6.8 %collective-permute-start = (bf16[3,256,128]{2,1,0:T(8,128)(2,1)S(1)}, bf16[3,256,128]{2,1,0:T(8,128)(2,1)S(1)}, u32[]{:S(2)}, u32[]{:S(2)}) collective-permute-start(bf16[3,256,128]{2,1,0:T(8,128)(2,1)S(1)} %bitcast.123), channel_id=1, source_target_pairs={{0,1},{1,2},{2,3},{3,4},{4,5},{5,6},{6,7},{8,9},{9,10},{10,11},{11... | collective-permute-start | bytes 589832 | tf_op jit(solution)/shard_map/ppermute | solution.py:18
  54.0 1.0 %copy-start.2 = (bf16[3,3,128,128]{3,2,1,0:T(8,128)(2,1)S(1)}, bf16[3,3,128,128]{3,2,1,0:T(8,128)(2,1)}, u32[]{:S(2)}) copy-start(bf16[3,3,128,128]{3,2,1,0:T(8,128)(2,1)} %param.21) | copy-start | bytes 884740
  55.7 0.8 copy-start.9
  57.4 1.1 %copy-start.1 = (bf16[3,3,128,256]{3,2,1,0:T(8,128)(2,1)S(1)}, bf16[3,3,128,256]{3,2,1,0:T(8,128)(2,1)}, u32[]{:S(2)}) copy-start(bf16[3,3,128,256]{3,2,1,0:T(8,128)(2,1)} %param.23) | copy-start | bytes 1769476
  58.2 1.4 %copy-start.7 = (bf16[256,256]{1,0:T(8,128)(2,1)S(1)}, bf16[256,256]{1,0:T(8,128)(2,1)}, u32[]{:S(2)}) copy-start(bf16[256,256]{1,0:T(8,128)(2,1)} %param.25) | copy-start | bytes 393220
  58.2 1.4 %copy-start.8 = (f32[256]{0:T(256)S(1)}, f32[256]{0:T(256)}, u32[]{:S(2)}) copy-start(f32[256]{0:T(256)} %param.24) | copy-start | bytes 3076

commit v5 on v4

--- a/solution.py
+++ b/solution.py
@@ -26,33 +26,60 @@
 OBS_CHUNK = 2048
 
 
-def deposit_rows(v_ref, c_ref, w_ref, aug, block):
-    n, d_in = v_ref.shape
-    aug[:, :d_in] = v_ref[...]
-    aug[:, d_in:] = jnp.ones((n, aug.shape[1] - d_in), jnp.bfloat16)
+def lookup(codes, table, shift):
+    w = jnp.zeros(codes.shape, jnp.float32)
+    for j in range(8):
+        w = jnp.where(codes == j + shift, table[j], w)
+    return w
+
+
+def deposit_rows(aug, cells_s, w_s, block):
+    n = aug.shape[0]
     chunk = min(n, OBS_CHUNK)
     ids = lax.broadcasted_iota(jnp.int32, (CELL_BLOCK, chunk), 0).astype(jnp.float32)
     ids = ids.astype(jnp.bfloat16)
     base = block * CELL_BLOCK
     total = jnp.zeros((CELL_BLOCK, aug.shape[1]), jnp.float32)
     for start in range(0, n, chunk):
-        rel = c_ref[:, start : start + chunk] - base
+        rel = cells_s[:, start : start + chunk] - base
         rel = jnp.where((rel >= 0) & (rel < CELL_BLOCK), rel, -1).astype(jnp.float32)
-        w = w_ref[:, start : start + chunk].astype(jnp.bfloat16)
+        w = w_s[:, start : start + chunk].astype(jnp.bfloat16)
         table = jnp.where(rel.astype(jnp.bfloat16) == ids, w, jnp.zeros((), jnp.bfloat16))
         total = total + jnp.dot(table, aug[start : start + chunk, :], preferred_element_type=jnp.float32)
     return total
 
 
-def sat_kernel(v_ref, c_ref, w_ref, out, aug):
+def sat_kernel(v_ref, c_ref, o_ref, tbl, out, aug, cells_s, w_s):
     block = pl.program_id(0)
-    out[...] = deposit_rows(v_ref, c_ref, w_ref, aug, block)
-
-
-def station_kernel(acc, v_ref, c_ref, w_ref, embed, out, aug):
+
+    @pl.when(block == 0)
+    def _():
+        n, d_in = v_ref.shape
+        aug[:, :d_in] = v_ref[...]
+        aug[:, d_in:] = jnp.ones((n, aug.shape[1] - d_in), jnp.bfloat16)
+        cells_s[...] = c_ref[...]
+        w_s[...] = lookup(o_ref[...], tbl, 0)
+
+    out[...] = deposit_rows(aug, cells_s, w_s, block)
+
+
+def station_kernel(capacity, acc, got, tbl, embed, out, aug, cells_s, w_s):
     block = pl.program_id(0)
-    total = acc[...] + deposit_rows(v_ref, c_ref, w_ref, aug, block)
     d_in = out.shape[1]
+
+    @pl.when(block == 0)
+    def _():
+        bands = got.shape[0]
+        aug[:, d_in:] = jnp.ones((aug.shape[0], aug.shape[1] - d_in), jnp.bfloat16)
+        for t in range(bands):
+            aug[t * capacity : (t + 1) * capacity, :d_in] = got[t, :capacity, :]
+            meta = got[t, capacity : capacity + 6, :].astype(jnp.float32).astype(jnp.int32)
+            for h in range(2):
+                at = slice(t * capacity + h * d_in, t * capacity + (h + 1) * d_in)
+                cells_s[:, at] = meta[h : h + 1] * 64 + meta[2 + h : 3 + h]
+                w_s[:, at] = lookup(meta[4 + h : 5 + h], tbl, 1)
+
+    total = acc[...] + deposit_rows(aug, cells_s, w_s, block)
     sums = total[:, :d_in]
     density = total[:, d_in:]
     grid = sums / jnp.maximum(density, 1.0) + density * embed[...]
@@ -63,29 +90,53 @@
     return pl.BlockSpec(shape, lambda c: (0,) * len(shape))
 
 
-def deposit_call(kernel, acc, values, cells, weight, extra, out_dtype, total_cells):
+SMEM = pl.BlockSpec(memory_space=pltpu.SMEM)
+
+
+def sat_deposit(values, cells, offsets, table, total_cells):
     n, d_in = values.shape
     wide = 2 * d_in
-    ins = [values, cells.reshape(1, n), weight.astype(jnp.float32).reshape(1, n)]
-    specs = [whole((n, d_in)), whole((1, n)), whole((1, n))]
-    if acc is not None:
-        ins = [acc] + ins
-        specs = [pl.BlockSpec((CELL_BLOCK, wide), lambda c: (c, 0))] + specs
-    for e in extra:
-        ins.append(e)
-        specs.append(whole(e.shape))
-    out_cols = wide if out_dtype == jnp.float32 else d_in
     return pl.pallas_call(
-        kernel,
+        sat_kernel,
         grid=(total_cells // CELL_BLOCK,),
-        in_specs=specs,
-        out_specs=pl.BlockSpec((CELL_BLOCK, out_cols), lambda c: (c, 0)),
-        out_shape=jax.ShapeDtypeStruct((total_cells, out_cols), out_dtype),
-        scratch_shapes=[pltpu.VMEM((n, wide), jnp.bfloat16)],
+        in_specs=[whole((n, d_in)), whole((1, n)), whole((1, n)), SMEM],
+        out_specs=pl.BlockSpec((CELL_BLOCK, wide), lambda c: (c, 0)),
+        out_shape=jax.ShapeDtypeStruct((total_cells, wide), jnp.float32),
+        scratch_shapes=[
+            pltpu.VMEM((n, wide), jnp.bfloat16),
+            pltpu.VMEM((1, n), jnp.int32),
+            pltpu.VMEM((1, n), jnp.float32),
+        ],
         cost_estimate=pl.CostEstimate(
             flops=2 * total_cells * n * wide, transcendentals=0, bytes_accessed=2 * n * (d_in + 4)
         ),
-    )(*ins)
+    )(values, cells.reshape(1, n), offsets.reshape(1, n), table)
+
+
+def station_deposit(acc, got, table, embed, capacity, total_cells):
+    bands, rows, d_in = got.shape
+    n = bands * capacity
+    wide = 2 * d_in
+    return pl.pallas_call(
+        functools.partial(station_kernel, capacity),
+        grid=(total_cells // CELL_BLOCK,),
+        in_specs=[
+            pl.BlockSpec((CELL_BLOCK, wide), lambda c: (c, 0)),
+            whole((bands, rows, d_in)),
+            SMEM,
+            whole((1, d_in)),
+        ],
+        out_specs=pl.BlockSpec((CELL_BLOCK, d_in), lambda c: (c, 0)),
+        out_shape=jax.ShapeDtypeStruct((total_cells, d_in), jnp.bfloat16),
+        scratch_shapes=[
+            pltpu.VMEM((n, wide), jnp.bfloat16),
+            pltpu.VMEM((1, n), jnp.int32),
+            pltpu.VMEM((1, n), jnp.float32),
+        ],
+        cost_estimate=pl.CostEstimate(
+            flops=2 * total_cells * n * wide, transcendentals=0, bytes_accessed=2 * n * (d_in + 4)
+        ),
+    )(acc, got, table, embed.reshape(1, d_in))
 
 
 def strided(padded, weight, bias):
@@ -142,13 +193,7 @@
     pad = jnp.zeros((bands, META - 3 * capacity // d_in, d_in), jnp.bfloat16)
     packet = jnp.concatenate([sent.reshape(bands, capacity, d_in), meta_sent, pad], axis=1)
     got = lax.all_to_all(packet, "band", split_axis=0, concat_axis=0, tiled=True)
-    got_values = got[:, :capacity, :].reshape(slots, d_in)
-    got_meta = got[:, capacity : capacity + 3 * capacity // d_in, :]
-    got_meta = got_meta.reshape(bands, 3, capacity).transpose(1, 0, 2).reshape(3, slots)
-    got_meta = got_meta.astype(jnp.int32)
-    cells = got_meta[0] * 64 + got_meta[1]
-    weight = jnp.where(got_meta[2] > 0, weights_of(got_meta[2] - 1), jnp.zeros((), jnp.bfloat16))
-    return got_values, cells, weight
+    return got
 
 
 def body(
@@ -170,14 +215,12 @@
     position_index = lax.axis_index("band")
     d_in = obs_values.shape[1]
     band_cells = LAT_DEV * LON
-    got_values, got_cells, got_weight = route(obs_values, obs_band, obs_cell, obs_offset, bands)
-    sat_acc = deposit_call(
-        sat_kernel, None, sat_values, sat_cell, weights_of(sat_offset), (), jnp.float32, band_cells
-    )
-    grid0 = deposit_call(
-        station_kernel, sat_acc, got_values, got_cells, got_weight,
-        (density_embed.reshape(1, d_in),), jnp.bfloat16, band_cells,
-    ).reshape(LAT_DEV, LON, d_in)
+    table = weights_of(jnp.arange(8, dtype=jnp.int32)).astype(jnp.float32)
+    sat_acc = sat_deposit(sat_values, sat_cell, sat_offset, table, band_cells)
+    got = route(obs_values, obs_band, obs_cell, obs_offset, bands)
+    capacity = obs_values.shape[0] // 8
+    grid0 = station_deposit(sat_acc, got, table, density_embed, capacity, band_cells)
+    grid0 = grid0.reshape(LAT_DEV, LON, d_in)
     above = passed_along(grid0[-3:], "band", 1)
     hidden1 = strided(jnp.concatenate([above, grid0], axis=0), conv1_weight, conv1_bias)
     keep_rows = (jnp.arange(hidden1.shape[0]) > 0) | (position_index > 0)

time: 80.8 us -> 79.4 us (0.983)
  other arithmetic: 4.25 us -> 2.97 us
    slice x1 -> x0, local copies, waits for them, and re-layouts: 0.83 us -> none  [route(): got_values = got[:, :capacity, :].reshape(slots, d_in)]
    unnamed x39, local copies, waits for them, and re-layouts: 1.96 us -> 2.77 us
where the time goes in v5:
time: 79.4 us; the launch traced here: 78.8 us
  blocking collectives  19.2 us (24%)
  Pallas kernels  13.8 us (17%)
  matrix products  12.1 us (15%)
  waiting for transfers between devices  11.4 us (14%)
  starting transfers between devices  10.8 us (14%)
  local copies, waits for them, and re-layouts  8.03 us (10%)
  other arithmetic  2.97 us (4%)
    all_to_all x1, blocking collectives, body(): lax.all_to_all(spread, 'band', split_axis=0, concat_axis=0, tiled=True)  19.2 us
    all_to_all x1, waiting for transfers between devices, route(): lax.all_to_all(packet, 'band', split_axis=0, concat_axis=0, tiled=True)  8.23 us
    pallas_call x1, Pallas kernels, station_deposit(): pl.pallas_call(functools.partial(station_kernel, capacity), grid=(total_c...  7.41 us
    all_to_all x1, starting transfers between devices, route(): lax.all_to_all(packet, 'band', split_axis=0, concat_axis=0, tiled=True)  7.28 us
    pallas_call x1, Pallas kernels, sat_deposit(): pl.pallas_call(sat_kernel, grid=(total_cells // CELL_BLOCK,), in_specs=[w...  6.37 us
    slice x2, local copies, waits for them, and re-layouts, strided(): parted[first // 2:first // 2 + rows, first % 2, second // 2:second // 2 +...  3.59 us
    ppermute x1, starting transfers between devices, passed_along(): return lax.ppermute(value, axis, pairs)  3.56 us
    dot_general x17, matrix products, strided(): jnp.dot(piece.reshape(rows * cols, chans), weight[first, second], preferr...  3.49 us
  transfers between devices with their start and end apart: 2, of which 2 were waited for; matrix products, arithmetic and copies ran while one was open for 1% of the time, Pallas kernels for 8%

profile of v5, /device:TPU:0, one launch (start us, length us, event | category | flops | bytes accessed | tf_op | source)
XLA Modules:
  0.0 78.8 jit_solution(567882553293980203)
XLA Ops:
  0.0 0.0 copy-start
  0.0 0.0 copy-start.4
  0.0 0.0 copy-start.6
  0.0 0.0 copy-start.5
  0.0 2.2 %fusion.14 = f32[2048]{0:T(1024)S(1)} fusion(s32[2048]{0:T(1024)} %bitcast.131), kind=kOutput, calls=%fused_computation.36 | convolution fusion | flops 71399424 | bytes 16384 | tf_op jit(solution)/shard_map/dot_general | solution.py:182
  2.2 0.0 copy-done.4
  2.3 0.0 copy-done.6
  2.3 0.0 copy-done.5
  2.4 2.9 %fusion.7 = bf16[3,2048]{1,0:T(4,128)(2,1)S(1)} fusion(s32[2048]{0:T(1024)S(1)} %convert_add_fusion, bf16[1,2048]{1,0:T(2,128)(2,1)S(1)} %stack.18, bf16[1,2048]{1,0:T(2,128)(2,1)S(1)} %stack.17, bf16[1,2048]{1,0:T(2,128)(2,1)S(1)} %stack.16), kind=kOutput, calls=%fused_computation.11 | convolution fusion | flops 29403136 | bytes 32768 | tf_op jit(solution)/shard_map/dot_general | solution.py:190
  5.3 0.0 copy-done
  5.3 3.0 %fusion.5 = bf16[2048,128]{1,0:T(8,128)(2,1)S(1)} fusion(bf16[2048,128]{1,0:T(8,128)(2,1)S(1)} %copy-done, s32[2048]{0:T(1024)S(1)} %convert_add_fusion), kind=kOutput, calls=%fused_computation.9 | convolution fusion | flops 1078198272 | bytes 1056768 | tf_op jit(solution)/shard_map/dot_general | solution.py:186
  8.3 0.1 pad.14.clone
  8.4 1.0 %maximum_maximum_fusion = bf16[8,272,128]{2,1,0:T(8,128)(2,1)} fusion(bf16[8,6,128]{2,1,0:T(8,128)(2,1)S(1)} %reshape.57, bf16[8,256,128]{2,1,0:T(8,128)(2,1)S(1)} %bitcast.116, bf16[272]{0:T(512)(128)(2,1)S(1)} %pad.14.clone), kind=kLoop, calls=%fused_computation.40 | loop fusion | flops 1671168 | bytes 1094176 | tf_op jit(solution)/shard_map/concatenate | solution.py:194
  9.4 7.3 %all-to-all-start = ((bf16[8,272,128]{2,1,0:T(8,128)(2,1)}), bf16[8,272,128]{2,1,0:T(8,128)(2,1)S(1)}, u32[]{:S(2)}, u32[]{:S(2)}) async-start(bf16[8,272,128]{2,1,0:T(8,128)(2,1)} %maximum_maximum_fusion), calls=%async_computation | async-start | bytes 1114112 | tf_op jit(solution)/shard_map/all_to_all | solution.py:195
  16.7 0.6 convert_convert_fusion.tbl
  17.2 6.4 %shard_map.127.acc = f32[2048,256]{1,0:T(8,128)} custom-call(bf16[2048,128]{1,0:T(8,128)(2,1)} %v_ref.1, s32[1,2048]{1,0:T(1,128)} %bitcast.133, s32[1,2048]{1,0:T(1,128)} %bitcast.134, f32[8]{0:T(128)} %convert_convert_fusion.tbl), custom_call_target="tpu_custom_call" | custom-call | flops 2147483648 | bytes 540672 | tf_op jit(solution)/shard_map/pallas_call | solution.py:99
  23.6 8.2 %all-to-all-done.got = bf16[8,272,128]{2,1,0:T(8,128)(2,1)S(1)} async-done(((bf16[8,272,128]{2,1,0:T(8,128)(2,1)}), bf16[8,272,128]{2,1,0:T(8,128)(2,1)S(1)}, u32[]{:S(2)}, u32[]{:S(2)}) %all-to-all-start) | async-done | bytes 557088 | tf_op jit(solution)/shard_map/all_to_all | solution.py:195
  31.8 0.0 copy-start.1
  31.8 0.8 %copy-done.1 = bf16[8,272,128]{2,1,0:T(8,128)(2,1)} copy-done((bf16[8,272,128]{2,1,0:T(8,128)(2,1)}, bf16[8,272,128]{2,1,0:T(8,128)(2,1)S(1)}, u32[]{:S(2)}) %copy-start.1) | copy-done | bytes 557080
  32.7 7.4 %shard_map.128 = bf16[2048,128]{1,0:T(8,128)(2,1)} custom-call(f32[2048,256]{1,0:T(8,128)} %shard_map.127.acc, bf16[8,272,128]{2,1,0:T(8,128)(2,1)} %copy-done.1, f32[8]{0:T(128)} %convert_convert_fusion.tbl, f32[1,128]{1,0:T(1,128)} %bitcast.135), custom_call_target="tpu_custom_call" | custom-call | flops 2147483648 | bytes 540672 | tf_op jit(solution)/shard_map/pallas_call | solution.py:120
  40.1 0.9 %slice.152 = bf16[768,128]{1,0:T(8,128)(2,1)S(1)} slice(bf16[2048,128]{1,0:T(8,128)(2,1)} %shard_map.128), slice={[1280:2048], [0:128]} | slice | bytes 393216 | tf_op jit(solution)/shard_map/slice | solution.py:224
  41.0 3.6 %collective-permute-start = (bf16[3,256,128]{2,1,0:T(8,128)(2,1)S(1)}, bf16[3,256,128]{2,1,0:T(8,128)(2,1)S(1)}, u32[]{:S(2)}, u32[]{:S(2)}) collective-permute-start(bf16[3,256,128]{2,1,0:T(8,128)(2,1)S(1)} %bitcast.117), channel_id=1, source_target_pairs={{0,1},{1,2},{2,3},{3,4},{4,5},{5,6},{6,7},{8,9},{9,10},{10,11},{11... | collective-permute-start | bytes 589832 | tf_op jit(solution)/shard_map/ppermute | solution.py:18
  44.6 3.2 %collective-permute-done = bf16[3,256,128]{2,1,0:T(8,128)(2,1)S(1)} collective-permute-done((bf16[3,256,128]{2,1,0:T(8,128)(2,1)S(1)}, bf16[3,256,128]{2,1,0:T(8,128)(2,1)S(1)}, u32[]{:S(2)}, u32[]{:S(2)}) %collective-permute-start) | collective-permute-done | bytes 196640 | tf_op jit(solution)/shard_map/ppermute | solution.py:18
  47.8 1.2 %fusion.16 = bf16[12,258,128]{2,1,0:T(8,128)(2,1)S(1)} fusion(bf16[8,256,128]{2,1,0:T(8,128)(2,1)} %bitcast.107, bf16[3,256,128]{2,1,0:T(8,128)(2,1)S(1)} %collective-permute-done), kind=kLoop, calls=%fused_computation.38 | loop fusion | flops 5151744 | bytes 1513472 | tf_op jit(solution)/shard_map/concatenate | solution.py:225
  49.1 0.3 reshape.60
  49.3 3.2 %fusion.150 = (bf16[5,1,128,1,128]{4,3,2,1,0:T(2,128)(2,1)S(1)}, bf16[5,1,128,1,128]{4,3,2,1,0:T(2,128)(2,1)S(1)}, bf16[5,1,128,1,128]{4,3,2,1,0:T(2,128)(2,1)S(...) fusion(bf16[6,2,129,2,128]{4,3,2,1,0:T(2,128)(2,1)S(1)} %reshape.60), kind=kLoop, calls=%fused_computation.201 | loop fusion | bytes 2949120 | tf_op jit(solution)/shard_map/slice | solution.py:151
  52.6 0.0 copy-start.3
  52.9 0.7 copy-done.3
  53.6 0.2 fusion.98
  53.8 0.2 convolution_add_fusion.7
  53.9 0.2 convolution_add_fusion.6
  54.1 0.2 convolution_add_fusion.5
  54.3 0.0 copy-start.9
  54.3 0.2 convolution_add_fusion.4
  54.5 0.2 convolution_add_fusion.3
  54.7 0.2 convolution_add_fusion.2
  54.9 0.2 convolution_add_fusion.1
  55.1 0.0 copy-done.9
  55.1 0.9 %fusion.19 = bf16[640,128]{1,0:T(8,128)(2,1)S(1)} fusion(f32[640,128]{1,0:T(8,128)S(1)} %convolution_add_fusion.1, bf16[640,128]{1,0:T(8,128)(2,1)S(1)} %bitcast.119, f32[128]{0:T(128)S(1)} %copy-done.9, bf16[3,3,128,128]{3,2,1,0:T(8,128)(2,1)S(1)} %copy-done.3), kind=kOutput, calls=%fused_computation.43 | convolution fusion | flops 26460160 | bytes 688640 | tf_op jit(solution)/shard_map/dot_general | solution.py:158
  56.0 0.0 copy-start.2
  56.0 0.1 select_convert_fusion
  56.1 0.2 reshape.62
  56.4 0.4 fusion.151
  56.8 0.0 copy-start.7
  56.8 0.0 copy-start.8
  56.9 0.1 copy-done.2
  57.0 0.1 fusion.46
  57.2 0.2 convolution_add_fusion.15
  57.3 0.1 convolution_add_fusion.14
  57.5 0.1 convolution_add_fusion.13
  57.6 0.1 convolution_add_fusion.12
  57.8 0.1 convolution_add_fusion.11
  57.9 0.1 convolution_add_fusion.10
  58.1 0.1 convolution_add_fusion.9
  58.2 0.0 copy-done.7
  58.2 0.0 copy-done.8
  58.3 0.6 convolution_convert_fusion
  58.8 0.1 broadcast_in_dim.34
  58.9 19.2 %all_to_all.10 = bf16[8,2,64,256]{3,2,1,0:T(8,128)(2,1)S(1)} all-to-all(bf16[8,2,64,256]{3,2,1,0:T(8,128)(2,1)S(1)} %broadcast_in_dim.34), channel_id=1, replica_groups=mesh['member'=4,'band'=8] {'band'}, dimensions={0} | all-to-all | bytes 1048576 | tf_op jit(solution)/shard_map/all_to_all | solution.py:231
  78.0 0.8 %copy.36 = bf16[16,64,256]{2,1,0:T(8,128)(2,1)} copy(bf16[16,64,256]{2,1,0:T(8,128)(2,1)S(1)} %bitcast.106) | data formatting | bytes 1048576
  (28 shorter events, 0.4 us)
Async XLA Ops:
  0.0 5.3 %copy-start = (bf16[2048,128]{1,0:T(8,128)(2,1)S(1)}, bf16[2048,128]{1,0:T(8,128)(2,1)}, u32[]{:S(2)}) copy-start(bf16[2048,128]{1,0:T(8,128)(2,1)} %param.13) | copy-start | bytes 1572868
  0.0 2.2 %copy-start.4 = (s32[2048,1]{0,1:T(1,128)S(1)}, s32[2048,1]{0,1:T(1,128)}, u32[]{:S(2)}) copy-start(s32[2048,1]{0,1:T(1,128)} %param.14) | copy-start | bytes 24580
  0.0 2.3 %copy-start.6 = (s32[2048]{0:T(1024)S(1)}, s32[2048]{0:T(1024)}, u32[]{:S(2)}) copy-start(s32[2048]{0:T(1024)} %param.15) | copy-start | bytes 24580
  0.0 2.3 %copy-start.5 = (s32[2048]{0:T(1024)S(1)}, s32[2048]{0:T(1024)}, u32[]{:S(2)}) copy-start(s32[2048]{0:T(1024)} %param.16) | copy-start | bytes 24580
  9.4 22.5 %all-to-all-start = ((bf16[8,272,128]{2,1,0:T(8,128)(2,1)}), bf16[8,272,128]{2,1,0:T(8,128)(2,1)S(1)}, u32[]{:S(2)}, u32[]{:S(2)}) async-start(bf16[8,272,128]{2,1,0:T(8,128)(2,1)} %maximum_maximum_fusion), calls=%async_computation | async-start | bytes 1114112 | tf_op jit(solution)/shard_map/all_to_all | solution.py:195
  31.8 0.8 %copy-start.1 = (bf16[8,272,128]{2,1,0:T(8,128)(2,1)}, bf16[8,272,128]{2,1,0:T(8,128)(2,1)S(1)}, u32[]{:S(2)}) copy-start(bf16[8,272,128]{2,1,0:T(8,128)(2,1)S(1)} %all-to-all-done.got) | copy-start | bytes 1671172
  41.0 6.8 %collective-permute-start = (bf16[3,256,128]{2,1,0:T(8,128)(2,1)S(1)}, bf16[3,256,128]{2,1,0:T(8,128)(2,1)S(1)}, u32[]{:S(2)}, u32[]{:S(2)}) collective-permute-start(bf16[3,256,128]{2,1,0:T(8,128)(2,1)S(1)} %bitcast.117), channel_id=1, source_target_pairs={{0,1},{1,2},{2,3},{3,4},{4,5},{5,6},{6,7},{8,9},{9,10},{10,11},{11... | collective-permute-start | bytes 589832 | tf_op jit(solution)/shard_map/ppermute | solution.py:18
  52.6 1.0 %copy-start.3 = (bf16[3,3,128,128]{3,2,1,0:T(8,128)(2,1)S(1)}, bf16[3,3,128,128]{3,2,1,0:T(8,128)(2,1)}, u32[]{:S(2)}) copy-start(bf16[3,3,128,128]{3,2,1,0:T(8,128)(2,1)} %param.21) | copy-start | bytes 884740
  54.3 0.8 copy-start.9
  56.0 1.1 %copy-start.2 = (bf16[3,3,128,256]{3,2,1,0:T(8,128)(2,1)S(1)}, bf16[3,3,128,256]{3,2,1,0:T(8,128)(2,1)}, u32[]{:S(2)}) copy-start(bf16[3,3,128,256]{3,2,1,0:T(8,128)(2,1)} %param.23) | copy-start | bytes 1769476
  56.8 1.4 %copy-start.7 = (bf16[256,256]{1,0:T(8,128)(2,1)S(1)}, bf16[256,256]{1,0:T(8,128)(2,1)}, u32[]{:S(2)}) copy-start(bf16[256,256]{1,0:T(8,128)(2,1)} %param.25) | copy-start | bytes 393220
  56.8 1.4 %copy-start.8 = (f32[256]{0:T(256)S(1)}, f32[256]{0:T(256)}, u32[]{:S(2)}) copy-start(f32[256]{0:T(256)} %param.24) | copy-start | bytes 3076

commit v6 on v5

--- a/solution.py
+++ b/solution.py
@@ -139,35 +139,80 @@
     )(acc, got, table, embed.reshape(1, d_in))
 
 
-def strided(padded, weight, bias):
-    count, width, chans = padded.shape
-    grid = jnp.pad(padded, ((0, 1), (1, 1), (0, 0)))
-    parted = grid.reshape((count + 1) // 2, 2, (width + 2) // 2, 2, chans)
-    rows = (count - 1) // 2
-    cols = width // 2
-    total = jnp.zeros((rows * cols, weight.shape[3]), jnp.float32)
-    for first in range(3):
-        for second in range(3):
-            piece = parted[
-                first // 2 : first // 2 + rows,
-                first % 2,
-                second // 2 : second // 2 + cols,
-                second % 2,
-                :,
-            ]
-            total = total + jnp.dot(
-                piece.reshape(rows * cols, chans),
-                weight[first, second],
-                preferred_element_type=jnp.float32,
-            )
-    return jax.nn.gelu(total + bias, approximate=False).reshape(rows, cols, weight.shape[3])
-
-
-def project(latent, proj_weight):
-    flat = jnp.dot(
-        latent.reshape(-1, latent.shape[2]), proj_weight, preferred_element_type=jnp.float32
-    )
-    return flat.astype(jnp.bfloat16).reshape(latent.shape)
+def pick(scratch, value, start):
+    rows, cols = value.shape
+    lanes = scratch.shape[2]
+    parts = []
+    for k in range(cols // lanes):
+        scratch[k, :rows, :] = value[:, k * lanes : (k + 1) * lanes]
+        parts.append(scratch[k, pl.ds(start, rows // 2, stride=2), :])
+    return parts[0] if len(parts) == 1 else jnp.concatenate(parts, axis=1)
+
+
+def shifted_odd(scratch, value, period):
+    odd = pick(scratch, value, 1)
+    odd = pltpu.roll(odd, 1, 0)
+    first = lax.broadcasted_iota(jnp.int32, odd.shape, 0) % period == 0
+    return jnp.where(first, 0.0, odd)
+
+
+def conv_taps(source, rows, width, weights):
+    taps = []
+    for e in range(3):
+        total = None
+        for a in range(3):
+            piece = source[pl.ds(a, rows, stride=2)].reshape(rows * width, source.shape[2])
+            part = jnp.dot(piece, weights[a, e], preferred_element_type=jnp.float32)
+            total = part if total is None else total + part
+        taps.append(total)
+    return taps
+
+
+def gelu(x):
+    return 0.5 * x * (1.0 + lax.erf(x * 0.7071067811865476))
+
+
+def conv_kernel(above, grid0, w1, b1, w2, b2, wp, out, xs, s1, h1, s2):
+    lat, width, d_in = grid0.shape
+    halo = above.shape[0]
+    xs[:halo] = above[...]
+    xs[halo:] = grid0[...]
+    rows1 = (halo + lat - 1) // 2
+    half = width // 2
+    taps = conv_taps(xs, rows1, width, w1)
+    pre1 = pick(s1, taps[1], 0) + pick(s1, taps[2], 1) + shifted_odd(s1, taps[0], half) + b1[...]
+    hid = gelu(pre1)
+    keep = (lax.broadcasted_iota(jnp.int32, hid.shape, 0) >= half) | (lax.axis_index("band") > 0)
+    hid = jnp.where(keep, hid, 0.0).astype(jnp.bfloat16)
+    h1[...] = hid.reshape(rows1, half, d_in)
+    rows2 = (rows1 - 1) // 2
+    quarter = half // 2
+    taps = conv_taps(h1, rows2, half, w2)
+    pre2 = pick(s2, taps[1], 0) + pick(s2, taps[2], 1) + shifted_odd(s2, taps[0], quarter) + b2[...]
+    latent = gelu(pre2).astype(jnp.bfloat16)
+    flat = jnp.dot(latent, wp[...], preferred_element_type=jnp.float32)
+    out[...] = flat.astype(out.dtype).reshape(out.shape)
+
+
+def convolve(above, grid0, w1, b1, w2, b2, wp):
+    lat, width, d_in = grid0.shape
+    halo = above.shape[0]
+    d_lat = w2.shape[3]
+    rows1 = (halo + lat - 1) // 2
+    rows2 = (rows1 - 1) // 2
+    vmem = pl.BlockSpec(memory_space=pltpu.VMEM)
+    return pl.pallas_call(
+        conv_kernel,
+        in_specs=[vmem] * 7,
+        out_specs=vmem,
+        out_shape=jax.ShapeDtypeStruct((rows2, width // 4, d_lat), jnp.bfloat16),
+        scratch_shapes=[
+            pltpu.VMEM((halo + lat, width, d_in), jnp.bfloat16),
+            pltpu.VMEM((1, rows1 * width, 128), jnp.float32),
+            pltpu.VMEM((rows1, width // 2, d_in), jnp.bfloat16),
+            pltpu.VMEM((d_lat // 128, rows2 * width // 2, 128), jnp.float32),
+        ],
+    )(above, grid0, w1, b1.reshape(1, -1), w2, b2.reshape(1, -1), wp)
 
 
 def route(obs_values, obs_band, obs_cell, obs_offset, bands):
@@ -222,11 +267,7 @@
     grid0 = station_deposit(sat_acc, got, table, density_embed, capacity, band_cells)
     grid0 = grid0.reshape(LAT_DEV, LON, d_in)
     above = passed_along(grid0[-3:], "band", 1)
-    hidden1 = strided(jnp.concatenate([above, grid0], axis=0), conv1_weight, conv1_bias)
-    keep_rows = (jnp.arange(hidden1.shape[0]) > 0) | (position_index > 0)
-    hidden1 = jnp.where(keep_rows[:, None, None], hidden1, 0.0).astype(jnp.bfloat16)
-    latent = strided(hidden1, conv2_weight, conv2_bias).astype(jnp.bfloat16)
-    mine = project(latent, proj_weight)
+    mine = convolve(above, grid0, conv1_weight, conv1_bias, conv2_weight, conv2_bias, proj_weight)
     spread = jnp.broadcast_to(mine[None], (bands,) + mine.shape)
     gathered = lax.all_to_all(spread, "band", split_axis=0, concat_axis=0, tiled=True)
     return gathered.reshape((bands * mine.shape[0],) + mine.shape[1:])

time: 79.4 us -> 74.8 us (0.942)
  Pallas kernels: 13.8 us -> 18 us
  matrix products: 12.1 us -> 8.08 us
  local copies, waits for them, and re-layouts: 8.03 us -> 4.25 us
    pallas_call x0 -> x1, Pallas kernels: none -> 4.19 us  [convolve(): pl.pallas_call(conv_kernel, in_specs=[vmem] * 7, out_specs=vmem, out_shap...]
    dot_general x18 -> x0, matrix products: 4.05 us -> none  [the longest x17 3.49 us: strided(): jnp.dot(piece.reshape(rows * cols, chans), weight[first, second], preferr...]
    slice x2 -> x0, local copies, waits for them, and re-layouts: 3.59 us -> none  [strided(): parted[first // 2:first // 2 + rows, first % 2, second // 2:second // 2 +...]
    concatenate x1 -> x0, other arithmetic: 1.25 us -> none  [body(): jnp.concatenate([above, grid0], axis=0)]
    broadcast_in_dim x1, local copies, waits for them, and re-layouts: 0.05 us -> 0.88 us  [body(): spread = jnp.broadcast_to(mine[None], (bands,) + mine.shape)]
    unnamed x39 -> x11, local copies, waits for them, and re-layouts: 2.77 us -> 2.3 us
  transfers between devices with their start and end apart: 2 -> 2, of which waited for: 2 -> 2; matrix products, arithmetic and copies ran while one was open for 1% -> 1% of each run, Pallas kernels for 8% -> 9%
where the time goes in v6:
time: 74.8 us; the launch traced here: 74.2 us
  blocking collectives  19.1 us (26%)
  Pallas kernels  18 us (24%)
  waiting for transfers between devices  11.7 us (16%)
  starting transfers between devices  10.7 us (14%)
  matrix products  8.08 us (11%)
  local copies, waits for them, and re-layouts  4.25 us (6%)
  other arithmetic  2.31 us (3%)
    all_to_all x1, blocking collectives, body(): lax.all_to_all(spread, 'band', split_axis=0, concat_axis=0, tiled=True)  19.1 us
    all_to_all x1, waiting for transfers between devices, route(): lax.all_to_all(packet, 'band', split_axis=0, concat_axis=0, tiled=True)  8.3 us
    pallas_call x1, Pallas kernels, station_deposit(): pl.pallas_call(functools.partial(station_kernel, capacity), grid=(total_c...  7.41 us
    all_to_all x1, starting transfers between devices, route(): lax.all_to_all(packet, 'band', split_axis=0, concat_axis=0, tiled=True)  7.28 us
    pallas_call x1, Pallas kernels, sat_deposit(): pl.pallas_call(sat_kernel, grid=(total_cells // CELL_BLOCK,), in_specs=[w...  6.36 us
    pallas_call x1, Pallas kernels, convolve(): pl.pallas_call(conv_kernel, in_specs=[vmem] * 7, out_specs=vmem, out_shap...  4.19 us
    ppermute x1, waiting for transfers between devices, passed_along(): return lax.ppermute(value, axis, pairs)  3.41 us
    ppermute x1, starting transfers between devices, passed_along(): return lax.ppermute(value, axis, pairs)  3.38 us
  transfers between devices with their start and end apart: 2, of which 2 were waited for; matrix products, arithmetic and copies ran while one was open for 1% of the time, Pallas kernels for 9%

profile of v6, /device:TPU:0, one launch (start us, length us, event | category | flops | bytes accessed | tf_op | source)
XLA Modules:
  0.0 74.2 jit_solution(2159209061879514848)
XLA Ops:
  0.0 0.0 copy-start
  0.0 0.8 %add_convert_fusion = bf16[2048]{0:T(1024)(128)(2,1)S(1)} fusion(s32[2048]{0:T(1024)} %param.16), kind=kLoop, calls=%fused_computation.27 | loop fusion | flops 4096 | bytes 12288 | tf_op jit(solution)/shard_map/convert.3
  0.8 0.0 copy-start.3
  0.8 0.0 copy-start.4
  0.8 2.2 %fusion.8 = f32[2048]{0:T(1024)S(1)} fusion(s32[2048]{0:T(1024)} %bitcast.19), kind=kOutput, calls=%fused_computation.10 | convolution fusion | flops 71399424 | bytes 16384 | tf_op jit(solution)/shard_map/dot_general | solution.py:227
  3.0 0.0 copy-done.3
  3.0 0.0 copy-done.4
  3.1 2.9 %fusion.7 = bf16[3,2048]{1,0:T(4,128)(2,1)S(1)} fusion(s32[2048]{0:T(1024)S(1)} %convert_add_fusion, bf16[1,2048]{1,0:T(2,128)(2,1)S(1)} %stack.18, bf16[1,2048]{1,0:T(2,128)(2,1)S(1)} %stack.17, bf16[1,2048]{1,0:T(2,128)(2,1)S(1)} %stack.16), kind=kOutput, calls=%fused_computation.9 | convolution fusion | flops 29403136 | bytes 32768 | tf_op jit(solution)/shard_map/dot_general | solution.py:235
  6.0 0.0 copy-done
  6.0 3.0 %fusion.5 = bf16[2048,128]{1,0:T(8,128)(2,1)S(1)} fusion(bf16[2048,128]{1,0:T(8,128)(2,1)S(1)} %copy-done, s32[2048]{0:T(1024)S(1)} %convert_add_fusion), kind=kOutput, calls=%fused_computation.7 | convolution fusion | flops 1078198272 | bytes 1056768 | tf_op jit(solution)/shard_map/dot_general | solution.py:231
  9.0 0.1 pad.2.clone
  9.1 1.0 %maximum_maximum_fusion = bf16[8,272,128]{2,1,0:T(8,128)(2,1)} fusion(bf16[8,6,128]{2,1,0:T(8,128)(2,1)S(1)} %reshape.45, bf16[8,256,128]{2,1,0:T(8,128)(2,1)S(1)} %bitcast.16, bf16[272]{0:T(512)(128)(2,1)S(1)} %pad.2.clone), kind=kLoop, calls=%fused_computation.11 | loop fusion | flops 1671168 | bytes 1094176 | tf_op jit(solution)/shard_map/concatenate | solution.py:239
  10.1 7.3 %all-to-all-start = ((bf16[8,272,128]{2,1,0:T(8,128)(2,1)}), bf16[8,272,128]{2,1,0:T(8,128)(2,1)S(1)}, u32[]{:S(2)}, u32[]{:S(2)}) async-start(bf16[8,272,128]{2,1,0:T(8,128)(2,1)} %maximum_maximum_fusion), calls=%async_computation | async-start | bytes 1114112 | tf_op jit(solution)/shard_map/all_to_all | solution.py:240
  17.4 0.5 convert_convert_fusion.tbl
  17.9 6.4 %shard_map.127.acc = f32[2048,256]{1,0:T(8,128)} custom-call(bf16[2048,128]{1,0:T(8,128)(2,1)} %v_ref.1, s32[1,2048]{1,0:T(1,128)} %bitcast.23, s32[1,2048]{1,0:T(1,128)} %bitcast.24, f32[8]{0:T(128)} %convert_convert_fusion.tbl), custom_call_target="tpu_custom_call" | custom-call | flops 2147483648 | bytes 540672 | tf_op jit(solution)/shard_map/pallas_call | solution.py:99
  24.3 8.3 %all-to-all-done.got = bf16[8,272,128]{2,1,0:T(8,128)(2,1)S(1)} async-done(((bf16[8,272,128]{2,1,0:T(8,128)(2,1)}), bf16[8,272,128]{2,1,0:T(8,128)(2,1)S(1)}, u32[]{:S(2)}, u32[]{:S(2)}) %all-to-all-start) | async-done | bytes 557088 | tf_op jit(solution)/shard_map/all_to_all | solution.py:240
  32.6 0.0 copy-start.1
  32.6 0.8 %copy-done.1 = bf16[8,272,128]{2,1,0:T(8,128)(2,1)} copy-done((bf16[8,272,128]{2,1,0:T(8,128)(2,1)}, bf16[8,272,128]{2,1,0:T(8,128)(2,1)S(1)}, u32[]{:S(2)}) %copy-start.1) | copy-done | bytes 557080
  33.4 7.4 %shard_map.128 = bf16[2048,128]{1,0:T(8,128)(2,1)} custom-call(f32[2048,256]{1,0:T(8,128)} %shard_map.127.acc, bf16[8,272,128]{2,1,0:T(8,128)(2,1)} %copy-done.1, f32[8]{0:T(128)} %convert_convert_fusion.tbl, f32[1,128]{1,0:T(1,128)} %bitcast.25), custom_call_target="tpu_custom_call" | custom-call | flops 2147483648 | bytes 540672 | tf_op jit(solution)/shard_map/pallas_call | solution.py:120
  40.8 0.9 %slice.8 = bf16[768,128]{1,0:T(8,128)(2,1)S(1)} slice(bf16[2048,128]{1,0:T(8,128)(2,1)} %shard_map.128), slice={[1280:2048], [0:128]} | slice | bytes 393216 | tf_op jit(solution)/shard_map/slice | solution.py:269
  41.8 3.4 %collective-permute-start = (bf16[3,256,128]{2,1,0:T(8,128)(2,1)S(1)}, bf16[3,256,128]{2,1,0:T(8,128)(2,1)S(1)}, u32[]{:S(2)}, u32[]{:S(2)}) collective-permute-start(bf16[3,256,128]{2,1,0:T(8,128)(2,1)S(1)} %bitcast.17), channel_id=1, source_target_pairs={{0,1},{1,2},{2,3},{3,4},{4,5},{5,6},{6,7},{8,9},{9,10},{10,11},{11... | collective-permute-start | bytes 589832 | tf_op jit(solution)/shard_map/ppermute | solution.py:18
  45.1 3.4 %collective-permute-done.above = bf16[3,256,128]{2,1,0:T(8,128)(2,1)S(1)} collective-permute-done((bf16[3,256,128]{2,1,0:T(8,128)(2,1)S(1)}, bf16[3,256,128]{2,1,0:T(8,128)(2,1)S(1)}, u32[]{:S(2)}, u32[]{:S(2)}) %collective-permute-start) | collective-permute-done | bytes 196640 | tf_op jit(solution)/shard_map/ppermute | solution.py:18
  48.5 0.0 copy-start.2
  48.6 0.7 copy-done.2
  49.2 4.2 %shard_map.129 = bf16[2,64,256]{2,1,0:T(8,128)(2,1)} custom-call(bf16[3,256,128]{2,1,0:T(8,128)(2,1)} %copy-done.2, bf16[8,256,128]{2,1,0:T(8,128)(2,1)} %bitcast.15, bf16[3,3,128,128]{3,2,1,0:T(8,128)(2,1)} %w1.1, f32[1,128]{1,0:T(1,128)} %bitcast.22, bf16[3,3,128,256]{3,2,1,0:T(8,128)(2,1)} %w2.1, f32[1,256]{1,0:T(1,128)} %bitcast.21, bf16[256,256]{1,0:T(8,128)(2,1)} %wp.1), custom_call_target="tpu_custom_call" | custom-call | tf_op jit(solution)/shard_map/pallas_call | solution.py:204
  53.4 0.9 %broadcast_in_dim.5 = bf16[8,2,64,256]{3,2,1,0:T(8,128)(2,1)S(1)} broadcast(bf16[2,64,256]{2,1,0:T(8,128)(2,1)} %shard_map.129), dimensions={1,2,3} | broadcast | bytes 589824 | tf_op jit(solution)/shard_map/broadcast_in_dim | solution.py:271
  54.3 19.1 %all_to_all.10 = bf16[8,2,64,256]{3,2,1,0:T(8,128)(2,1)S(1)} all-to-all(bf16[8,2,64,256]{3,2,1,0:T(8,128)(2,1)S(1)} %broadcast_in_dim.5), channel_id=1, replica_groups=mesh['member'=4,'band'=8] {'band'}, dimensions={0} | all-to-all | bytes 1048576 | tf_op jit(solution)/shard_map/all_to_all | solution.py:272
  73.4 0.8 %copy.17 = bf16[16,64,256]{2,1,0:T(8,128)(2,1)} copy(bf16[16,64,256]{2,1,0:T(8,128)(2,1)S(1)} %bitcast.14) | data formatting | bytes 1048576
  (7 shorter events, 0.1 us)
Async XLA Ops:
  0.0 6.0 %copy-start = (bf16[2048,128]{1,0:T(8,128)(2,1)S(1)}, bf16[2048,128]{1,0:T(8,128)(2,1)}, u32[]{:S(2)}) copy-start(bf16[2048,128]{1,0:T(8,128)(2,1)} %param.13) | copy-start | bytes 1572868
  0.8 2.2 %copy-start.3 = (s32[2048,1]{0,1:T(1,128)S(1)}, s32[2048,1]{0,1:T(1,128)}, u32[]{:S(2)}) copy-start(s32[2048,1]{0,1:T(1,128)} %param.14) | copy-start | bytes 24580
  0.8 2.3 %copy-start.4 = (s32[2048]{0:T(1024)S(1)}, s32[2048]{0:T(1024)}, u32[]{:S(2)}) copy-start(s32[2048]{0:T(1024)} %param.15) | copy-start | bytes 24580
  10.1 22.5 %all-to-all-start = ((bf16[8,272,128]{2,1,0:T(8,128)(2,1)}), bf16[8,272,128]{2,1,0:T(8,128)(2,1)S(1)}, u32[]{:S(2)}, u32[]{:S(2)}) async-start(bf16[8,272,128]{2,1,0:T(8,128)(2,1)} %maximum_maximum_fusion), calls=%async_computation | async-start | bytes 1114112 | tf_op jit(solution)/shard_map/all_to_all | solution.py:240
  32.6 0.8 %copy-start.1 = (bf16[8,272,128]{2,1,0:T(8,128)(2,1)}, bf16[8,272,128]{2,1,0:T(8,128)(2,1)S(1)}, u32[]{:S(2)}) copy-start(bf16[8,272,128]{2,1,0:T(8,128)(2,1)S(1)} %all-to-all-done.got) | copy-start | bytes 1671172
  41.8 6.8 %collective-permute-start = (bf16[3,256,128]{2,1,0:T(8,128)(2,1)S(1)}, bf16[3,256,128]{2,1,0:T(8,128)(2,1)S(1)}, u32[]{:S(2)}, u32[]{:S(2)}) collective-permute-start(bf16[3,256,128]{2,1,0:T(8,128)(2,1)S(1)} %bitcast.17), channel_id=1, source_target_pairs={{0,1},{1,2},{2,3},{3,4},{4,5},{5,6},{6,7},{8,9},{9,10},{10,11},{11... | collective-permute-start | bytes 589832 | tf_op jit(solution)/shard_map/ppermute | solution.py:18
  48.5 0.7 copy-start.2

commit v7 on v6

--- a/solution.py
+++ b/solution.py
@@ -215,30 +215,62 @@
     )(above, grid0, w1, b1.reshape(1, -1), w2, b2.reshape(1, -1), wp)
 
 
+def prefix_count(mask):
+    total = mask
+    step = 1
+    lanes = lax.broadcasted_iota(jnp.int32, mask.shape, 1)
+    while step < mask.shape[1]:
+        moved = pltpu.roll(total, step, 1)
+        total = total + jnp.where(lanes >= step, moved, 0)
+        step *= 2
+    return total - mask
+
+
+def route_kernel(capacity, target, cells, offsets, values, out):
+    bands, rows, d_in = out.shape
+    n = values.shape[0]
+    t = target[...]
+    band_ids = lax.broadcasted_iota(jnp.int32, (bands, n), 0)
+    mask = (t == band_ids).astype(jnp.int32)
+    rank = jnp.sum(mask * prefix_count(mask), axis=0, keepdims=True)
+    c = cells[...]
+    meta = jnp.concatenate(
+        [c // 64, c % 64, offsets[...] + 1, jnp.zeros((5, n), jnp.int32)], axis=0
+    ).astype(jnp.float32).astype(jnp.bfloat16)
+    slots = lax.broadcasted_iota(jnp.int32, (capacity, n), 0)
+    per_row = capacity // d_in
+    for b in range(bands):
+        mine = jnp.where(t == b, rank, -1)
+        table = jnp.where(mine == slots, 1.0, 0.0).astype(jnp.bfloat16)
+        out[b, :capacity, :] = jnp.dot(
+            table, values[...], preferred_element_type=jnp.float32
+        ).astype(out.dtype)
+        sent = lax.dot_general(
+            meta, table, (((1,), (1,)), ((), ())), preferred_element_type=jnp.float32
+        ).astype(out.dtype)
+        for m in range(3):
+            for h in range(per_row):
+                row = capacity + m * per_row + h
+                out[b, row : row + 1, :] = sent[m : m + 1, h * d_in : (h + 1) * d_in]
+        out[b, capacity + 3 * per_row :, :] = jnp.zeros((rows - capacity - 3 * per_row, d_in), out.dtype)
+
+
 def route(obs_values, obs_band, obs_cell, obs_offset, bands):
     obs_rows, d_in = obs_values.shape
     capacity = obs_rows // 8
-    slots = bands * capacity
-    target = obs_band[:, 0]
-    choose = (target[:, None] == jnp.arange(bands, dtype=jnp.int32)[None, :]).astype(jnp.bfloat16)
-    earlier = (
-        jnp.arange(obs_rows, dtype=jnp.int32)[:, None] > jnp.arange(obs_rows, dtype=jnp.int32)[None, :]
-    ).astype(jnp.bfloat16)
-    before = jnp.dot(earlier, choose, preferred_element_type=jnp.float32)
-    rank = jnp.sum(before * choose.astype(jnp.float32), axis=1).astype(jnp.int32)
-    position = target * capacity + rank
-    table = (jnp.arange(slots, dtype=jnp.int32)[:, None] == position[None, :]).astype(jnp.bfloat16)
-    sent = jnp.dot(table, obs_values, preferred_element_type=jnp.float32).astype(jnp.bfloat16)
-    meta = jnp.stack(
-        [obs_cell // 64, obs_cell % 64, obs_offset + 1], axis=0
-    ).astype(jnp.bfloat16)
-    meta_sent = jnp.dot(meta, table.T, preferred_element_type=jnp.float32).astype(jnp.bfloat16)
-    meta_sent = meta_sent.reshape(3, bands, capacity).transpose(1, 0, 2)
-    meta_sent = meta_sent.reshape(bands, 3 * capacity // d_in, d_in)
-    pad = jnp.zeros((bands, META - 3 * capacity // d_in, d_in), jnp.bfloat16)
-    packet = jnp.concatenate([sent.reshape(bands, capacity, d_in), meta_sent, pad], axis=1)
-    got = lax.all_to_all(packet, "band", split_axis=0, concat_axis=0, tiled=True)
-    return got
+    vmem = pl.BlockSpec(memory_space=pltpu.VMEM)
+    packet = pl.pallas_call(
+        functools.partial(route_kernel, capacity),
+        in_specs=[vmem] * 4,
+        out_specs=vmem,
+        out_shape=jax.ShapeDtypeStruct((bands, capacity + META, d_in), jnp.bfloat16),
+    )(
+        obs_band.reshape(1, obs_rows),
+        obs_cell.reshape(1, obs_rows),
+        obs_offset.reshape(1, obs_rows),
+        obs_values,
+    )
+    return lax.all_to_all(packet, "band", split_axis=0, concat_axis=0, tiled=True)
 
 
 def body(

time: 74.8 us -> 71.6 us (0.957)
  matrix products: 8.08 us -> 0 us
  Pallas kernels: 18 us -> 24.9 us
  other arithmetic: 2.31 us -> 0.6 us
    dot_general x3 -> x0, matrix products: 8.08 us -> none  [the longest x1 2.98 us: route(): jnp.dot(table, obs_values, preferred_element_type=jnp.float32)]
    pallas_call x0 -> x1, Pallas kernels: none -> 6.94 us  [route(): pl.pallas_call(functools.partial(route_kernel, capacity), in_specs=[vmem]...]
    concatenate x1 -> x0, other arithmetic: 1.01 us -> none  [route(): jnp.concatenate([sent.reshape(bands, capacity, d_in), meta_sent, pad], ax...]
    another operation x2 -> x0, other arithmetic: 0.77 us -> none
    unnamed x11 -> x5, local copies, waits for them, and re-layouts: 2.3 us -> 2.28 us
where the time goes in v7:
time: 71.6 us; the launch traced here: 71.1 us
  Pallas kernels  24.9 us (35%)
  blocking collectives  19.2 us (27%)
  waiting for transfers between devices  11.6 us (16%)
  starting transfers between devices  10.7 us (15%)
  local copies, waits for them, and re-layouts  4.1 us (6%)
    all_to_all x1, blocking collectives, body(): lax.all_to_all(spread, 'band', split_axis=0, concat_axis=0, tiled=True)  19.2 us
    all_to_all x1, waiting for transfers between devices, route(): lax.all_to_all(packet, 'band', split_axis=0, concat_axis=0, tiled=True)  8.22 us
    pallas_call x1, Pallas kernels, station_deposit(): pl.pallas_call(functools.partial(station_kernel, capacity), grid=(total_c...  7.41 us
    all_to_all x1, starting transfers between devices, route(): lax.all_to_all(packet, 'band', split_axis=0, concat_axis=0, tiled=True)  7.28 us
    pallas_call x1, Pallas kernels, route(): pl.pallas_call(functools.partial(route_kernel, capacity), in_specs=[vmem]...  6.94 us
    pallas_call x1, Pallas kernels, sat_deposit(): pl.pallas_call(sat_kernel, grid=(total_cells // CELL_BLOCK,), in_specs=[w...  6.37 us
    pallas_call x1, Pallas kernels, convolve(): pl.pallas_call(conv_kernel, in_specs=[vmem] * 7, out_specs=vmem, out_shap...  4.17 us
    ppermute x1, waiting for transfers between devices, passed_along(): return lax.ppermute(value, axis, pairs)  3.41 us
  transfers between devices with their start and end apart: 2, of which 2 were waited for; matrix products, arithmetic and copies ran while one was open for 1% of the time, Pallas kernels for 9%

profile of v7, /device:TPU:0, one launch (start us, length us, event | category | flops | bytes accessed | tf_op | source)
XLA Modules:
  0.0 71.1 jit_solution(40443141265292427)
XLA Ops:
  0.0 6.9 %shard_map.128 = bf16[8,272,128]{2,1,0:T(8,128)(2,1)} custom-call(s32[1,2048]{1,0:T(1,128)} %bitcast.14, s32[1,2048]{1,0:T(1,128)} %bitcast.15, s32[1,2048]{1,0:T(1,128)} %bitcast.16, bf16[2048,128]{1,0:T(8,128)(2,1)} %values.1), custom_call_target="tpu_custom_call" | custom-call | tf_op jit(solution)/shard_map/pallas_call | solution.py:262
  6.9 7.3 %all-to-all-start = ((bf16[8,272,128]{2,1,0:T(8,128)(2,1)}), bf16[8,272,128]{2,1,0:T(8,128)(2,1)S(1)}, u32[]{:S(2)}, u32[]{:S(2)}) async-start(bf16[8,272,128]{2,1,0:T(8,128)(2,1)} %shard_map.128), calls=%async_computation | async-start | bytes 1114112 | tf_op jit(solution)/shard_map/all_to_all | solution.py:273
  14.2 0.6 convert_convert_fusion.tbl
  14.8 6.4 %shard_map.127.acc = f32[2048,256]{1,0:T(8,128)} custom-call(bf16[2048,128]{1,0:T(8,128)(2,1)} %v_ref.1, s32[1,2048]{1,0:T(1,128)} %bitcast.19, s32[1,2048]{1,0:T(1,128)} %bitcast.20, f32[8]{0:T(128)} %convert_convert_fusion.tbl), custom_call_target="tpu_custom_call" | custom-call | flops 2147483648 | bytes 540672 | tf_op jit(solution)/shard_map/pallas_call | solution.py:99
  21.2 8.2 %all-to-all-done.got = bf16[8,272,128]{2,1,0:T(8,128)(2,1)S(1)} async-done(((bf16[8,272,128]{2,1,0:T(8,128)(2,1)}), bf16[8,272,128]{2,1,0:T(8,128)(2,1)S(1)}, u32[]{:S(2)}, u32[]{:S(2)}) %all-to-all-start) | async-done | bytes 557088 | tf_op jit(solution)/shard_map/all_to_all | solution.py:273
  29.4 0.0 copy-start
  29.4 0.8 %copy-done = bf16[8,272,128]{2,1,0:T(8,128)(2,1)} copy-done((bf16[8,272,128]{2,1,0:T(8,128)(2,1)}, bf16[8,272,128]{2,1,0:T(8,128)(2,1)S(1)}, u32[]{:S(2)}) %copy-start) | copy-done | bytes 557080
  30.2 7.4 %shard_map.129 = bf16[2048,128]{1,0:T(8,128)(2,1)} custom-call(f32[2048,256]{1,0:T(8,128)} %shard_map.127.acc, bf16[8,272,128]{2,1,0:T(8,128)(2,1)} %copy-done, f32[8]{0:T(128)} %convert_convert_fusion.tbl, f32[1,128]{1,0:T(1,128)} %bitcast.21), custom_call_target="tpu_custom_call" | custom-call | flops 2147483648 | bytes 540672 | tf_op jit(solution)/shard_map/pallas_call | solution.py:120
  37.6 0.9 %slice.8 = bf16[768,128]{1,0:T(8,128)(2,1)S(1)} slice(bf16[2048,128]{1,0:T(8,128)(2,1)} %shard_map.129), slice={[1280:2048], [0:128]} | slice | bytes 393216 | tf_op jit(solution)/shard_map/slice | solution.py:301
  38.6 3.4 %collective-permute-start = (bf16[3,256,128]{2,1,0:T(8,128)(2,1)S(1)}, bf16[3,256,128]{2,1,0:T(8,128)(2,1)S(1)}, u32[]{:S(2)}, u32[]{:S(2)}) collective-permute-start(bf16[3,256,128]{2,1,0:T(8,128)(2,1)S(1)} %bitcast.13), channel_id=1, source_target_pairs={{0,1},{1,2},{2,3},{3,4},{4,5},{5,6},{6,7},{8,9},{9,10},{10,11},{11... | collective-permute-start | bytes 589832 | tf_op jit(solution)/shard_map/ppermute | solution.py:18
  42.0 3.4 %collective-permute-done.above = bf16[3,256,128]{2,1,0:T(8,128)(2,1)S(1)} collective-permute-done((bf16[3,256,128]{2,1,0:T(8,128)(2,1)S(1)}, bf16[3,256,128]{2,1,0:T(8,128)(2,1)S(1)}, u32[]{:S(2)}, u32[]{:S(2)}) %collective-permute-start) | collective-permute-done | bytes 196640 | tf_op jit(solution)/shard_map/ppermute | solution.py:18
  45.4 0.0 copy-start.1
  45.4 0.7 copy-done.1
  46.0 4.2 %shard_map.130 = bf16[2,64,256]{2,1,0:T(8,128)(2,1)} custom-call(bf16[3,256,128]{2,1,0:T(8,128)(2,1)} %copy-done.1, bf16[8,256,128]{2,1,0:T(8,128)(2,1)} %bitcast.12, bf16[3,3,128,128]{3,2,1,0:T(8,128)(2,1)} %w1.1, f32[1,128]{1,0:T(1,128)} %bitcast.18, bf16[3,3,128,256]{3,2,1,0:T(8,128)(2,1)} %w2.1, f32[1,256]{1,0:T(1,128)} %bitcast.17, bf16[256,256]{1,0:T(8,128)(2,1)} %wp.1), custom_call_target="tpu_custom_call" | custom-call | tf_op jit(solution)/shard_map/pallas_call | solution.py:204
  50.2 0.9 %broadcast_in_dim.2 = bf16[8,2,64,256]{3,2,1,0:T(8,128)(2,1)S(1)} broadcast(bf16[2,64,256]{2,1,0:T(8,128)(2,1)} %shard_map.130), dimensions={1,2,3} | broadcast | bytes 589824 | tf_op jit(solution)/shard_map/broadcast_in_dim | solution.py:303
  51.1 19.2 %all_to_all.10 = bf16[8,2,64,256]{3,2,1,0:T(8,128)(2,1)S(1)} all-to-all(bf16[8,2,64,256]{3,2,1,0:T(8,128)(2,1)S(1)} %broadcast_in_dim.2), channel_id=1, replica_groups=mesh['member'=4,'band'=8] {'band'}, dimensions={0} | all-to-all | bytes 1048576 | tf_op jit(solution)/shard_map/all_to_all | solution.py:304
  70.3 0.8 %copy.15 = bf16[16,64,256]{2,1,0:T(8,128)(2,1)} copy(bf16[16,64,256]{2,1,0:T(8,128)(2,1)S(1)} %bitcast.11) | data formatting | bytes 1048576
Async XLA Ops:
  6.9 22.5 %all-to-all-start = ((bf16[8,272,128]{2,1,0:T(8,128)(2,1)}), bf16[8,272,128]{2,1,0:T(8,128)(2,1)S(1)}, u32[]{:S(2)}, u32[]{:S(2)}) async-start(bf16[8,272,128]{2,1,0:T(8,128)(2,1)} %shard_map.128), calls=%async_computation | async-start | bytes 1114112 | tf_op jit(solution)/shard_map/all_to_all | solution.py:273
  29.4 0.8 %copy-start = (bf16[8,272,128]{2,1,0:T(8,128)(2,1)}, bf16[8,272,128]{2,1,0:T(8,128)(2,1)S(1)}, u32[]{:S(2)}) copy-start(bf16[8,272,128]{2,1,0:T(8,128)(2,1)S(1)} %all-to-all-done.got) | copy-start | bytes 1671172
  38.6 6.8 %collective-permute-start = (bf16[3,256,128]{2,1,0:T(8,128)(2,1)S(1)}, bf16[3,256,128]{2,1,0:T(8,128)(2,1)S(1)}, u32[]{:S(2)}, u32[]{:S(2)}) collective-permute-start(bf16[3,256,128]{2,1,0:T(8,128)(2,1)S(1)} %bitcast.13), channel_id=1, source_target_pairs={{0,1},{1,2},{2,3},{3,4},{4,5},{5,6},{6,7},{8,9},{9,10},{10,11},{11... | collective-permute-start | bytes 589832 | tf_op jit(solution)/shard_map/ppermute | solution.py:18
  45.4 0.7 copy-start.1

commit v8 on v7

--- a/solution.py
+++ b/solution.py
@@ -63,11 +63,12 @@
     out[...] = deposit_rows(aug, cells_s, w_s, block)
 
 
-def station_kernel(capacity, acc, got, tbl, embed, out, aug, cells_s, w_s):
-    block = pl.program_id(0)
+def station_kernel(capacity, first, acc, got, tbl, embed, out, aug, cells_s, w_s):
+    step = pl.program_id(0)
+    block = step + first
     d_in = out.shape[1]
 
-    @pl.when(block == 0)
+    @pl.when(step == 0)
     def _():
         bands = got.shape[0]
         aug[:, d_in:] = jnp.ones((aug.shape[0], aug.shape[1] - d_in), jnp.bfloat16)
@@ -113,28 +114,28 @@
     )(values, cells.reshape(1, n), offsets.reshape(1, n), table)
 
 
-def station_deposit(acc, got, table, embed, capacity, total_cells):
+def station_deposit(acc, got, table, embed, capacity, first, count):
     bands, rows, d_in = got.shape
     n = bands * capacity
     wide = 2 * d_in
     return pl.pallas_call(
-        functools.partial(station_kernel, capacity),
-        grid=(total_cells // CELL_BLOCK,),
+        functools.partial(station_kernel, capacity, first),
+        grid=(count,),
         in_specs=[
-            pl.BlockSpec((CELL_BLOCK, wide), lambda c: (c, 0)),
+            pl.BlockSpec((CELL_BLOCK, wide), lambda c: (c + first, 0)),
             whole((bands, rows, d_in)),
             SMEM,
             whole((1, d_in)),
         ],
         out_specs=pl.BlockSpec((CELL_BLOCK, d_in), lambda c: (c, 0)),
-        out_shape=jax.ShapeDtypeStruct((total_cells, d_in), jnp.bfloat16),
+        out_shape=jax.ShapeDtypeStruct((count * CELL_BLOCK, d_in), jnp.bfloat16),
         scratch_shapes=[
             pltpu.VMEM((n, wide), jnp.bfloat16),
             pltpu.VMEM((1, n), jnp.int32),
             pltpu.VMEM((1, n), jnp.float32),
         ],
         cost_estimate=pl.CostEstimate(
-            flops=2 * total_cells * n * wide, transcendentals=0, bytes_accessed=2 * n * (d_in + 4)
+            flops=2 * count * CELL_BLOCK * n * wide, transcendentals=0, bytes_accessed=2 * n * (d_in + 4)
         ),
     )(acc, got, table, embed.reshape(1, d_in))
 
@@ -172,11 +173,12 @@
     return 0.5 * x * (1.0 + lax.erf(x * 0.7071067811865476))
 
 
-def conv_kernel(above, grid0, w1, b1, w2, b2, wp, out, xs, s1, h1, s2):
-    lat, width, d_in = grid0.shape
-    halo = above.shape[0]
+def conv_kernel(above, low, high, w1, b1, w2, b2, wp, out, xs, s1, h1, s2):
+    halo, width, d_in = above.shape
+    lat = low.shape[0] + high.shape[0]
     xs[:halo] = above[...]
-    xs[halo:] = grid0[...]
+    xs[halo : halo + low.shape[0]] = low[...]
+    xs[halo + low.shape[0] :] = high[...]
     rows1 = (halo + lat - 1) // 2
     half = width // 2
     taps = conv_taps(xs, rows1, width, w1)
@@ -194,16 +196,16 @@
     out[...] = flat.astype(out.dtype).reshape(out.shape)
 
 
-def convolve(above, grid0, w1, b1, w2, b2, wp):
-    lat, width, d_in = grid0.shape
-    halo = above.shape[0]
+def convolve(above, low, high, w1, b1, w2, b2, wp):
+    halo, width, d_in = above.shape
+    lat = low.shape[0] + high.shape[0]
     d_lat = w2.shape[3]
     rows1 = (halo + lat - 1) // 2
     rows2 = (rows1 - 1) // 2
     vmem = pl.BlockSpec(memory_space=pltpu.VMEM)
     return pl.pallas_call(
         conv_kernel,
-        in_specs=[vmem] * 7,
+        in_specs=[vmem] * 8,
         out_specs=vmem,
         out_shape=jax.ShapeDtypeStruct((rows2, width // 4, d_lat), jnp.bfloat16),
         scratch_shapes=[
@@ -212,7 +214,7 @@
             pltpu.VMEM((rows1, width // 2, d_in), jnp.bfloat16),
             pltpu.VMEM((d_lat // 128, rows2 * width // 2, 128), jnp.float32),
         ],
-    )(above, grid0, w1, b1.reshape(1, -1), w2, b2.reshape(1, -1), wp)
+    )(above, low, high, w1, b1.reshape(1, -1), w2, b2.reshape(1, -1), wp)
 
 
 def prefix_count(mask):
@@ -296,10 +298,17 @@
     sat_acc = sat_deposit(sat_values, sat_cell, sat_offset, table, band_cells)
     got = route(obs_values, obs_band, obs_cell, obs_offset, bands)
     capacity = obs_values.shape[0] // 8
-    grid0 = station_deposit(sat_acc, got, table, density_embed, capacity, band_cells)
-    grid0 = grid0.reshape(LAT_DEV, LON, d_in)
-    above = passed_along(grid0[-3:], "band", 1)
-    mine = convolve(above, grid0, conv1_weight, conv1_bias, conv2_weight, conv2_bias, proj_weight)
+    halo = 3
+    lat_blocks = band_cells // CELL_BLOCK
+    rows_per_block = CELL_BLOCK // LON
+    high = station_deposit(
+        sat_acc, got, table, density_embed, capacity, lat_blocks - halo // rows_per_block, halo // rows_per_block
+    ).reshape(halo, LON, d_in)
+    above = passed_along(high, "band", 1)
+    low = station_deposit(
+        sat_acc, got, table, density_embed, capacity, 0, lat_blocks - halo // rows_per_block
+    ).reshape(LAT_DEV - halo, LON, d_in)
+    mine = convolve(above, low, high, conv1_weight, conv1_bias, conv2_weight, conv2_bias, proj_weight)
     spread = jnp.broadcast_to(mine[None], (bands,) + mine.shape)
     gathered = lax.all_to_all(spread, "band", split_axis=0, concat_axis=0, tiled=True)
     return gathered.reshape((bands * mine.shape[0],) + mine.shape[1:])

time: 71.6 us -> 67.3 us (0.940)
  waiting for transfers between devices: 11.6 us -> 8.28 us
  Pallas kernels: 24.9 us -> 26.7 us
  blocking collectives: 19.2 us -> 17.4 us
  local copies, waits for them, and re-layouts: 4.1 us -> 3.16 us
    ppermute x1, waiting for transfers between devices: 3.41 us -> 0.01 us  [passed_along(): return lax.ppermute(value, axis, pairs)]
    pallas_call x2 -> x3, Pallas kernels: 11.6 us -> 13.4 us  [the longest x2 9.22 us: station_deposit(): pl.pallas_call(functools.partial(station_kernel, capacity, first), grid=(...]
    all_to_all x1, blocking collectives: 19.2 us -> 17.4 us  [body(): lax.all_to_all(spread, 'band', split_axis=0, concat_axis=0, tiled=True)]
    slice x1 -> x0, local copies, waits for them, and re-layouts: 0.94 us -> none  [body(): above = passed_along(grid0[-3:], 'band', 1)]
  transfers between devices with their start and end apart: 2 -> 2, of which waited for: 2 -> 1; matrix products, arithmetic and copies ran while one was open for 1% -> 1% of each run, Pallas kernels for 9% -> 18%
where the time goes in v8:
time: 67.3 us; the launch traced here: 66.8 us
  Pallas kernels  26.7 us (40%)
  blocking collectives  17.4 us (26%)
  starting transfers between devices  10.6 us (16%)
  waiting for transfers between devices  8.28 us (12%)
  local copies, waits for them, and re-layouts  3.16 us (5%)
    all_to_all x1, blocking collectives, body(): lax.all_to_all(spread, 'band', split_axis=0, concat_axis=0, tiled=True)  17.4 us
    pallas_call x2, Pallas kernels, station_deposit(): pl.pallas_call(functools.partial(station_kernel, capacity, first), grid=(...  9.22 us
    all_to_all x1, waiting for transfers between devices, route(): lax.all_to_all(packet, 'band', split_axis=0, concat_axis=0, tiled=True)  8.28 us
    all_to_all x1, starting transfers between devices, route(): lax.all_to_all(packet, 'band', split_axis=0, concat_axis=0, tiled=True)  7.28 us
    pallas_call x1, Pallas kernels, route(): pl.pallas_call(functools.partial(route_kernel, capacity), in_specs=[vmem]...  6.94 us
    pallas_call x1, Pallas kernels, sat_deposit(): pl.pallas_call(sat_kernel, grid=(total_cells // CELL_BLOCK,), in_specs=[w...  6.37 us
    pallas_call x1, Pallas kernels, convolve(): pl.pallas_call(conv_kernel, in_specs=[vmem] * 8, out_specs=vmem, out_shap...  4.18 us
    ppermute x1, starting transfers between devices, passed_along(): return lax.ppermute(value, axis, pairs)  3.37 us
  transfers between devices with their start and end apart: 2, of which 1 were waited for; matrix products, arithmetic and copies ran while one was open for 1% of the time, Pallas kernels for 18%

profile of v8, /device:TPU:0, one launch (start us, length us, event | category | flops | bytes accessed | tf_op | source)
XLA Modules:
  0.0 66.8 jit_solution(7490863120901441317)
XLA Ops:
  0.0 6.9 %shard_map.128 = bf16[8,272,128]{2,1,0:T(8,128)(2,1)} custom-call(s32[1,2048]{1,0:T(1,128)} %bitcast.15, s32[1,2048]{1,0:T(1,128)} %bitcast.16, s32[1,2048]{1,0:T(1,128)} %bitcast.17, bf16[2048,128]{1,0:T(8,128)(2,1)} %values.1), custom_call_target="tpu_custom_call" | custom-call | tf_op jit(solution)/shard_map/pallas_call | solution.py:264
  6.9 7.3 %all-to-all-start = ((bf16[8,272,128]{2,1,0:T(8,128)(2,1)}), bf16[8,272,128]{2,1,0:T(8,128)(2,1)S(1)}, u32[]{:S(2)}, u32[]{:S(2)}) async-start(bf16[8,272,128]{2,1,0:T(8,128)(2,1)} %shard_map.128), calls=%async_computation | async-start | bytes 1114112 | tf_op jit(solution)/shard_map/all_to_all | solution.py:275
  14.2 0.5 convert_convert_fusion.tbl
  14.8 6.4 %shard_map.127.acc = f32[2048,256]{1,0:T(8,128)} custom-call(bf16[2048,128]{1,0:T(8,128)(2,1)} %v_ref.1, s32[1,2048]{1,0:T(1,128)} %bitcast.20, s32[1,2048]{1,0:T(1,128)} %bitcast.21, f32[8]{0:T(128)} %convert_convert_fusion.tbl), custom_call_target="tpu_custom_call" | custom-call | flops 2147483648 | bytes 540672 | tf_op jit(solution)/shard_map/pallas_call | solution.py:100
  21.1 8.3 %all-to-all-done.got = bf16[8,272,128]{2,1,0:T(8,128)(2,1)S(1)} async-done(((bf16[8,272,128]{2,1,0:T(8,128)(2,1)}), bf16[8,272,128]{2,1,0:T(8,128)(2,1)S(1)}, u32[]{:S(2)}, u32[]{:S(2)}) %all-to-all-start) | async-done | bytes 557088 | tf_op jit(solution)/shard_map/all_to_all | solution.py:275
  29.4 0.0 copy-start
  29.4 0.8 %copy-done = bf16[8,272,128]{2,1,0:T(8,128)(2,1)} copy-done((bf16[8,272,128]{2,1,0:T(8,128)(2,1)}, bf16[8,272,128]{2,1,0:T(8,128)(2,1)S(1)}, u32[]{:S(2)}) %copy-start) | copy-done | bytes 557080
  30.2 3.9 %shard_map.129 = bf16[768,128]{1,0:T(8,128)(2,1)} custom-call(f32[2048,256]{1,0:T(8,128)} %shard_map.127.acc, bf16[8,272,128]{2,1,0:T(8,128)(2,1)} %copy-done, f32[8]{0:T(128)} %convert_convert_fusion.tbl, f32[1,128]{1,0:T(1,128)} %bitcast.22), custom_call_target="tpu_custom_call" | custom-call | flops 805306368 | bytes 540672 | tf_op jit(solution)/shard_map/pallas_call | solution.py:121
  34.1 3.4 %collective-permute-start = (bf16[3,256,128]{2,1,0:T(8,128)(2,1)}, bf16[3,256,128]{2,1,0:T(8,128)(2,1)S(1)}, u32[]{:S(2)}, u32[]{:S(2)}) collective-permute-start(bf16[3,256,128]{2,1,0:T(8,128)(2,1)} %bitcast.13), channel_id=1, source_target_pairs={{0,1},{1,2},{2,3},{3,4},{4,5},{5,6},{6,7},{8,9},{9,10},{10,11},{11... | collective-permute-start | bytes 589832 | tf_op jit(solution)/shard_map/ppermute | solution.py:18
  37.5 5.3 %shard_map.130 = bf16[1280,128]{1,0:T(8,128)(2,1)} custom-call(f32[2048,256]{1,0:T(8,128)} %shard_map.127.acc, bf16[8,272,128]{2,1,0:T(8,128)(2,1)} %copy-done, f32[8]{0:T(128)} %convert_convert_fusion.tbl, f32[1,128]{1,0:T(1,128)} %bitcast.23), custom_call_target="tpu_custom_call" | custom-call | flops 1342177280 | bytes 540672 | tf_op jit(solution)/shard_map/pallas_call | solution.py:121
  42.8 0.0 collective-permute-done.above
  42.8 0.0 copy-start.1
  42.8 0.7 %copy-done.1 = bf16[3,256,128]{2,1,0:T(8,128)(2,1)} copy-done((bf16[3,256,128]{2,1,0:T(8,128)(2,1)}, bf16[3,256,128]{2,1,0:T(8,128)(2,1)S(1)}, u32[]{:S(2)}) %copy-start.1) | copy-done | bytes 196632
  43.5 4.2 %shard_map.131 = bf16[2,64,256]{2,1,0:T(8,128)(2,1)} custom-call(bf16[3,256,128]{2,1,0:T(8,128)(2,1)} %copy-done.1, bf16[5,256,128]{2,1,0:T(8,128)(2,1)} %bitcast.12, bf16[3,256,128]{2,1,0:T(8,128)(2,1)} %bitcast.14, bf16[3,3,128,128]{3,2,1,0:T(8,128)(2,1)} %w1.1, f32[1,128]{1,0:T(1,128)} %bitcast.19, bf16[3,3,128,256]{3,2,1,0:T(8,128)(2,1)} %w2.1, ...), custom_call_target="tpu_custom_call" | custom-call | tf_op jit(solution)/shard_map/pallas_call | solution.py:206
  47.7 0.9 %broadcast_in_dim.2 = bf16[8,2,64,256]{3,2,1,0:T(8,128)(2,1)S(1)} broadcast(bf16[2,64,256]{2,1,0:T(8,128)(2,1)} %shard_map.131), dimensions={1,2,3} | broadcast | bytes 589824 | tf_op jit(solution)/shard_map/broadcast_in_dim | solution.py:312
  48.6 17.4 %all_to_all.10 = bf16[8,2,64,256]{3,2,1,0:T(8,128)(2,1)S(1)} all-to-all(bf16[8,2,64,256]{3,2,1,0:T(8,128)(2,1)S(1)} %broadcast_in_dim.2), channel_id=1, replica_groups=mesh['member'=4,'band'=8] {'band'}, dimensions={0} | all-to-all | bytes 1048576 | tf_op jit(solution)/shard_map/all_to_all | solution.py:313
  66.0 0.8 %copy.15 = bf16[16,64,256]{2,1,0:T(8,128)(2,1)} copy(bf16[16,64,256]{2,1,0:T(8,128)(2,1)S(1)} %bitcast.11) | data formatting | bytes 1048576
Async XLA Ops:
  6.9 22.5 %all-to-all-start = ((bf16[8,272,128]{2,1,0:T(8,128)(2,1)}), bf16[8,272,128]{2,1,0:T(8,128)(2,1)S(1)}, u32[]{:S(2)}, u32[]{:S(2)}) async-start(bf16[8,272,128]{2,1,0:T(8,128)(2,1)} %shard_map.128), calls=%async_computation | async-start | bytes 1114112 | tf_op jit(solution)/shard_map/all_to_all | solution.py:275
  29.4 0.8 %copy-start = (bf16[8,272,128]{2,1,0:T(8,128)(2,1)}, bf16[8,272,128]{2,1,0:T(8,128)(2,1)S(1)}, u32[]{:S(2)}) copy-start(bf16[8,272,128]{2,1,0:T(8,128)(2,1)S(1)} %all-to-all-done.got) | copy-start | bytes 1671172
  34.1 8.7 %collective-permute-start = (bf16[3,256,128]{2,1,0:T(8,128)(2,1)}, bf16[3,256,128]{2,1,0:T(8,128)(2,1)S(1)}, u32[]{:S(2)}, u32[]{:S(2)}) collective-permute-start(bf16[3,256,128]{2,1,0:T(8,128)(2,1)} %bitcast.13), channel_id=1, source_target_pairs={{0,1},{1,2},{2,3},{3,4},{4,5},{5,6},{6,7},{8,9},{9,10},{10,11},{11... | collective-permute-start | bytes 589832 | tf_op jit(solution)/shard_map/ppermute | solution.py:18
  42.8 0.7 %copy-start.1 = (bf16[3,256,128]{2,1,0:T(8,128)(2,1)}, bf16[3,256,128]{2,1,0:T(8,128)(2,1)S(1)}, u32[]{:S(2)}) copy-start(bf16[3,256,128]{2,1,0:T(8,128)(2,1)S(1)} %collective-permute-done.above) | copy-start | bytes 589828

commit v9 on v8

--- a/solution.py
+++ b/solution.py
@@ -193,10 +193,12 @@
     pre2 = pick(s2, taps[1], 0) + pick(s2, taps[2], 1) + shifted_odd(s2, taps[0], quarter) + b2[...]
     latent = gelu(pre2).astype(jnp.bfloat16)
     flat = jnp.dot(latent, wp[...], preferred_element_type=jnp.float32)
-    out[...] = flat.astype(out.dtype).reshape(out.shape)
-
-
-def convolve(above, low, high, w1, b1, w2, b2, wp):
+    flat = flat.astype(out.dtype).reshape(out.shape[1:])
+    for b in range(out.shape[0]):
+        out[b] = flat
+
+
+def convolve(bands, above, low, high, w1, b1, w2, b2, wp):
     halo, width, d_in = above.shape
     lat = low.shape[0] + high.shape[0]
     d_lat = w2.shape[3]
@@ -207,7 +209,7 @@
         conv_kernel,
         in_specs=[vmem] * 8,
         out_specs=vmem,
-        out_shape=jax.ShapeDtypeStruct((rows2, width // 4, d_lat), jnp.bfloat16),
+        out_shape=jax.ShapeDtypeStruct((bands, rows2, width // 4, d_lat), jnp.bfloat16),
         scratch_shapes=[
             pltpu.VMEM((halo + lat, width, d_in), jnp.bfloat16),
             pltpu.VMEM((1, rows1 * width, 128), jnp.float32),
@@ -239,11 +241,13 @@
     meta = jnp.concatenate(
         [c // 64, c % 64, offsets[...] + 1, jnp.zeros((5, n), jnp.int32)], axis=0
     ).astype(jnp.float32).astype(jnp.bfloat16)
-    slots = lax.broadcasted_iota(jnp.int32, (capacity, n), 0)
+    slots = lax.broadcasted_iota(jnp.int32, (capacity, n), 0).astype(jnp.float32).astype(jnp.bfloat16)
     per_row = capacity // d_in
+    one = jnp.ones((), jnp.bfloat16)
+    zero = jnp.zeros((), jnp.bfloat16)
     for b in range(bands):
-        mine = jnp.where(t == b, rank, -1)
-        table = jnp.where(mine == slots, 1.0, 0.0).astype(jnp.bfloat16)
+        mine = jnp.where(t == b, rank, -1).astype(jnp.float32).astype(jnp.bfloat16)
+        table = jnp.where(mine == slots, one, zero)
         out[b, :capacity, :] = jnp.dot(
             table, values[...], preferred_element_type=jnp.float32
         ).astype(out.dtype)
@@ -308,10 +312,9 @@
     low = station_deposit(
         sat_acc, got, table, density_embed, capacity, 0, lat_blocks - halo // rows_per_block
     ).reshape(LAT_DEV - halo, LON, d_in)
-    mine = convolve(above, low, high, conv1_weight, conv1_bias, conv2_weight, conv2_bias, proj_weight)
-    spread = jnp.broadcast_to(mine[None], (bands,) + mine.shape)
+    spread = convolve(bands, above, low, high, conv1_weight, conv1_bias, conv2_weight, conv2_bias, proj_weight)
     gathered = lax.all_to_all(spread, "band", split_axis=0, concat_axis=0, tiled=True)
-    return gathered.reshape((bands * mine.shape[0],) + mine.shape[1:])
+    return gathered.reshape((bands * spread.shape[1],) + spread.shape[2:])
 
 
 def solution(mesh):

time: 67.3 us -> 66.8 us (level)
  local copies, waits for them, and re-layouts: 3.16 us -> 2.28 us
    broadcast_in_dim x1 -> x0, local copies, waits for them, and re-layouts: 0.88 us -> none  [body(): spread = jnp.broadcast_to(mine[None], (bands,) + mine.shape)]
where the time goes in v9:
time: 66.8 us; the launch traced here: 66.3 us
  Pallas kernels  26.9 us (40%)
  blocking collectives  17.6 us (26%)
  starting transfers between devices  10.6 us (16%)
  waiting for transfers between devices  8.31 us (12%)
  local copies, waits for them, and re-layouts  2.28 us (3%)
    all_to_all x1, blocking collectives, body(): lax.all_to_all(spread, 'band', split_axis=0, concat_axis=0, tiled=True)  17.6 us
    pallas_call x2, Pallas kernels, station_deposit(): pl.pallas_call(functools.partial(station_kernel, capacity, first), grid=(...  9.21 us
    all_to_all x1, waiting for transfers between devices, route(): lax.all_to_all(packet, 'band', split_axis=0, concat_axis=0, tiled=True)  8.31 us
    all_to_all x1, starting transfers between devices, route(): lax.all_to_all(packet, 'band', split_axis=0, concat_axis=0, tiled=True)  7.28 us
    pallas_call x1, Pallas kernels, route(): pl.pallas_call(functools.partial(route_kernel, capacity), in_specs=[vmem]...  6.93 us
    pallas_call x1, Pallas kernels, sat_deposit(): pl.pallas_call(sat_kernel, grid=(total_cells // CELL_BLOCK,), in_specs=[w...  6.36 us
    pallas_call x1, Pallas kernels, convolve(): pl.pallas_call(conv_kernel, in_specs=[vmem] * 8, out_specs=vmem, out_shap...  4.35 us
    ppermute x1, starting transfers between devices, passed_along(): return lax.ppermute(value, axis, pairs)  3.37 us
  transfers between devices with their start and end apart: 2, of which 1 were waited for; matrix products, arithmetic and copies ran while one was open for 1% of the time, Pallas kernels for 18%

profile of v9, /device:TPU:0, one launch (start us, length us, event | category | flops | bytes accessed | tf_op | source)
XLA Modules:
  0.0 66.3 jit_solution(17673422287015148562)
XLA Ops:
  0.0 6.9 %shard_map.128 = bf16[8,272,128]{2,1,0:T(8,128)(2,1)} custom-call(s32[1,2048]{1,0:T(1,128)} %bitcast.15, s32[1,2048]{1,0:T(1,128)} %bitcast.16, s32[1,2048]{1,0:T(1,128)} %bitcast.17, bf16[2048,128]{1,0:T(8,128)(2,1)} %values.1), custom_call_target="tpu_custom_call" | custom-call | tf_op jit(solution)/shard_map/pallas_call | solution.py:268
  6.9 7.3 %all-to-all-start = ((bf16[8,272,128]{2,1,0:T(8,128)(2,1)}), bf16[8,272,128]{2,1,0:T(8,128)(2,1)S(1)}, u32[]{:S(2)}, u32[]{:S(2)}) async-start(bf16[8,272,128]{2,1,0:T(8,128)(2,1)} %shard_map.128), calls=%async_computation | async-start | bytes 1114112 | tf_op jit(solution)/shard_map/all_to_all | solution.py:279
  14.2 0.5 convert_convert_fusion.tbl
  14.7 6.4 %shard_map.127.acc = f32[2048,256]{1,0:T(8,128)} custom-call(bf16[2048,128]{1,0:T(8,128)(2,1)} %v_ref.1, s32[1,2048]{1,0:T(1,128)} %bitcast.20, s32[1,2048]{1,0:T(1,128)} %bitcast.21, f32[8]{0:T(128)} %convert_convert_fusion.tbl), custom_call_target="tpu_custom_call" | custom-call | flops 2147483648 | bytes 540672 | tf_op jit(solution)/shard_map/pallas_call | solution.py:100
  21.1 8.3 %all-to-all-done.got = bf16[8,272,128]{2,1,0:T(8,128)(2,1)S(1)} async-done(((bf16[8,272,128]{2,1,0:T(8,128)(2,1)}), bf16[8,272,128]{2,1,0:T(8,128)(2,1)S(1)}, u32[]{:S(2)}, u32[]{:S(2)}) %all-to-all-start) | async-done | bytes 557088 | tf_op jit(solution)/shard_map/all_to_all | solution.py:279
  29.4 0.0 copy-start
  29.4 0.8 %copy-done = bf16[8,272,128]{2,1,0:T(8,128)(2,1)} copy-done((bf16[8,272,128]{2,1,0:T(8,128)(2,1)}, bf16[8,272,128]{2,1,0:T(8,128)(2,1)S(1)}, u32[]{:S(2)}) %copy-start) | copy-done | bytes 557080
  30.2 3.9 %shard_map.129 = bf16[768,128]{1,0:T(8,128)(2,1)} custom-call(f32[2048,256]{1,0:T(8,128)} %shard_map.127.acc, bf16[8,272,128]{2,1,0:T(8,128)(2,1)} %copy-done, f32[8]{0:T(128)} %convert_convert_fusion.tbl, f32[1,128]{1,0:T(1,128)} %bitcast.22), custom_call_target="tpu_custom_call" | custom-call | flops 805306368 | bytes 540672 | tf_op jit(solution)/shard_map/pallas_call | solution.py:121
  34.1 3.4 %collective-permute-start = (bf16[3,256,128]{2,1,0:T(8,128)(2,1)}, bf16[3,256,128]{2,1,0:T(8,128)(2,1)S(1)}, u32[]{:S(2)}, u32[]{:S(2)}) collective-permute-start(bf16[3,256,128]{2,1,0:T(8,128)(2,1)} %bitcast.13), channel_id=1, source_target_pairs={{0,1},{1,2},{2,3},{3,4},{4,5},{5,6},{6,7},{8,9},{9,10},{10,11},{11... | collective-permute-start | bytes 589832 | tf_op jit(solution)/shard_map/ppermute | solution.py:18
  37.5 5.3 %shard_map.130 = bf16[1280,128]{1,0:T(8,128)(2,1)} custom-call(f32[2048,256]{1,0:T(8,128)} %shard_map.127.acc, bf16[8,272,128]{2,1,0:T(8,128)(2,1)} %copy-done, f32[8]{0:T(128)} %convert_convert_fusion.tbl, f32[1,128]{1,0:T(1,128)} %bitcast.23), custom_call_target="tpu_custom_call" | custom-call | flops 1342177280 | bytes 540672 | tf_op jit(solution)/shard_map/pallas_call | solution.py:121
  42.8 0.0 collective-permute-done.above
  42.8 0.0 copy-start.1
  42.8 0.7 %copy-done.1 = bf16[3,256,128]{2,1,0:T(8,128)(2,1)} copy-done((bf16[3,256,128]{2,1,0:T(8,128)(2,1)}, bf16[3,256,128]{2,1,0:T(8,128)(2,1)S(1)}, u32[]{:S(2)}) %copy-start.1) | copy-done | bytes 196632
  43.5 4.3 %shard_map.131 = bf16[8,2,64,256]{3,2,1,0:T(8,128)(2,1)} custom-call(bf16[3,256,128]{2,1,0:T(8,128)(2,1)} %copy-done.1, bf16[5,256,128]{2,1,0:T(8,128)(2,1)} %bitcast.12, bf16[3,256,128]{2,1,0:T(8,128)(2,1)} %bitcast.14, bf16[3,3,128,128]{3,2,1,0:T(8,128)(2,1)} %w1.1, f32[1,128]{1,0:T(1,128)} %bitcast.19, bf16[3,3,128,256]{3,2,1,0:T(8,128)(2,1)} %w2.1, ...), custom_call_target="tpu_custom_call" | custom-call | tf_op jit(solution)/shard_map/pallas_call | solution.py:208
  47.8 17.6 %all_to_all.10 = bf16[8,2,64,256]{3,2,1,0:T(8,128)(2,1)S(1)} all-to-all(bf16[8,2,64,256]{3,2,1,0:T(8,128)(2,1)} %shard_map.131), channel_id=1, replica_groups=mesh['member'=4,'band'=8] {'band'}, dimensions={0} | all-to-all | bytes 1048576 | tf_op jit(solution)/shard_map/all_to_all | solution.py:316
  65.5 0.8 %copy.15 = bf16[16,64,256]{2,1,0:T(8,128)(2,1)} copy(bf16[16,64,256]{2,1,0:T(8,128)(2,1)S(1)} %bitcast.11) | data formatting | bytes 1048576
Async XLA Ops:
  6.9 22.5 %all-to-all-start = ((bf16[8,272,128]{2,1,0:T(8,128)(2,1)}), bf16[8,272,128]{2,1,0:T(8,128)(2,1)S(1)}, u32[]{:S(2)}, u32[]{:S(2)}) async-start(bf16[8,272,128]{2,1,0:T(8,128)(2,1)} %shard_map.128), calls=%async_computation | async-start | bytes 1114112 | tf_op jit(solution)/shard_map/all_to_all | solution.py:279
  29.4 0.8 %copy-start = (bf16[8,272,128]{2,1,0:T(8,128)(2,1)}, bf16[8,272,128]{2,1,0:T(8,128)(2,1)S(1)}, u32[]{:S(2)}) copy-start(bf16[8,272,128]{2,1,0:T(8,128)(2,1)S(1)} %all-to-all-done.got) | copy-start | bytes 1671172
  34.1 8.7 %collective-permute-start = (bf16[3,256,128]{2,1,0:T(8,128)(2,1)}, bf16[3,256,128]{2,1,0:T(8,128)(2,1)S(1)}, u32[]{:S(2)}, u32[]{:S(2)}) collective-permute-start(bf16[3,256,128]{2,1,0:T(8,128)(2,1)} %bitcast.13), channel_id=1, source_target_pairs={{0,1},{1,2},{2,3},{3,4},{4,5},{5,6},{6,7},{8,9},{9,10},{10,11},{11... | collective-permute-start | bytes 589832 | tf_op jit(solution)/shard_map/ppermute | solution.py:18
  42.8 0.7 %copy-start.1 = (bf16[3,256,128]{2,1,0:T(8,128)(2,1)}, bf16[3,256,128]{2,1,0:T(8,128)(2,1)S(1)}, u32[]{:S(2)}) copy-start(bf16[3,256,128]{2,1,0:T(8,128)(2,1)S(1)} %collective-permute-done.above) | copy-start | bytes 589828

commit v10 on v9

--- a/solution.py
+++ b/solution.py
@@ -230,7 +230,7 @@
     return total - mask
 
 
-def route_kernel(capacity, target, cells, offsets, values, out):
+def route_kernel(capacity, target, cells, offsets, values, out, vaug):
     bands, rows, d_in = out.shape
     n = values.shape[0]
     t = target[...]
@@ -238,22 +238,19 @@
     mask = (t == band_ids).astype(jnp.int32)
     rank = jnp.sum(mask * prefix_count(mask), axis=0, keepdims=True)
     c = cells[...]
-    meta = jnp.concatenate(
-        [c // 64, c % 64, offsets[...] + 1, jnp.zeros((5, n), jnp.int32)], axis=0
-    ).astype(jnp.float32).astype(jnp.bfloat16)
-    slots = lax.broadcasted_iota(jnp.int32, (capacity, n), 0).astype(jnp.float32).astype(jnp.bfloat16)
+    vaug[:, :d_in] = values[...]
+    vaug[:, d_in:] = jnp.zeros((n, vaug.shape[1] - d_in), jnp.bfloat16)
+    codes = (c // 64, c % 64, offsets[...] + 1)
+    for m, code in enumerate(codes):
+        vaug[:, d_in + m : d_in + m + 1] = code.astype(jnp.float32).astype(jnp.bfloat16)
+    slots = lax.broadcasted_iota(jnp.int32, (capacity, n), 0)
     per_row = capacity // d_in
-    one = jnp.ones((), jnp.bfloat16)
-    zero = jnp.zeros((), jnp.bfloat16)
     for b in range(bands):
-        mine = jnp.where(t == b, rank, -1).astype(jnp.float32).astype(jnp.bfloat16)
-        table = jnp.where(mine == slots, one, zero)
-        out[b, :capacity, :] = jnp.dot(
-            table, values[...], preferred_element_type=jnp.float32
-        ).astype(out.dtype)
-        sent = lax.dot_general(
-            meta, table, (((1,), (1,)), ((), ())), preferred_element_type=jnp.float32
-        ).astype(out.dtype)
+        mine = jnp.where(t == b, rank, -1)
+        table = jnp.where(mine == slots, 1.0, 0.0).astype(jnp.bfloat16)
+        res = jnp.dot(table, vaug[...], preferred_element_type=jnp.float32)
+        out[b, :capacity, :] = res[:, :d_in].astype(out.dtype)
+        sent = jnp.transpose(res[:, d_in:]).astype(out.dtype)
         for m in range(3):
             for h in range(per_row):
                 row = capacity + m * per_row + h
@@ -270,10 +267,11 @@
         in_specs=[vmem] * 4,
         out_specs=vmem,
         out_shape=jax.ShapeDtypeStruct((bands, capacity + META, d_in), jnp.bfloat16),
+        scratch_shapes=[pltpu.VMEM((obs_rows, 2 * d_in), jnp.bfloat16)],
     )(
         obs_band.reshape(1, obs_rows),
-        obs_cell.reshape(1, obs_rows),
-        obs_offset.reshape(1, obs_rows),
+        obs_cell.reshape(obs_rows, 1),
+        obs_offset.reshape(obs_rows, 1),
         obs_values,
     )
     return lax.all_to_all(packet, "band", split_axis=0, concat_axis=0, tiled=True)

time: 66.8 us -> 70.2 us (1.051)
  local copies, waits for them, and re-layouts: 2.28 us -> 6.38 us
  Pallas kernels: 26.9 us -> 26.1 us
    reshape x0 -> x2, local copies, waits for them, and re-layouts: none -> 4.11 us  [the longest x1 2.08 us: route(): obs_offset.reshape(obs_rows, 1)]
    pallas_call x1, Pallas kernels: 6.93 us -> 6.19 us  [route(): pl.pallas_call(functools.partial(route_kernel, capacity), in_specs=[vmem]...]
  transfers between devices with their start and end apart: 2 -> 2, of which waited for: 1 -> 1; matrix products, arithmetic and copies ran while one was open for 1% -> 1% of each run, Pallas kernels for 18% -> 17%
where the time goes in v10:
time: 70.2 us; the launch traced here: 69.6 us
  Pallas kernels  26.1 us (37%)
  blocking collectives  17.7 us (25%)
  starting transfers between devices  10.6 us (15%)
  waiting for transfers between devices  8.31 us (12%)
  local copies, waits for them, and re-layouts  6.38 us (9%)
    all_to_all x1, blocking collectives, body(): lax.all_to_all(spread, 'band', split_axis=0, concat_axis=0, tiled=True)  17.7 us
    pallas_call x2, Pallas kernels, station_deposit(): pl.pallas_call(functools.partial(station_kernel, capacity, first), grid=(...  9.21 us
    all_to_all x1, waiting for transfers between devices, route(): lax.all_to_all(packet, 'band', split_axis=0, concat_axis=0, tiled=True)  8.31 us
    all_to_all x1, starting transfers between devices, route(): lax.all_to_all(packet, 'band', split_axis=0, concat_axis=0, tiled=True)  7.28 us
    pallas_call x1, Pallas kernels, sat_deposit(): pl.pallas_call(sat_kernel, grid=(total_cells // CELL_BLOCK,), in_specs=[w...  6.36 us
    pallas_call x1, Pallas kernels, route(): pl.pallas_call(functools.partial(route_kernel, capacity), in_specs=[vmem]...  6.19 us
    pallas_call x1, Pallas kernels, convolve(): pl.pallas_call(conv_kernel, in_specs=[vmem] * 8, out_specs=vmem, out_shap...  4.35 us
    ppermute x1, starting transfers between devices, passed_along(): return lax.ppermute(value, axis, pairs)  3.37 us
  transfers between devices with their start and end apart: 2, of which 1 were waited for; matrix products, arithmetic and copies ran while one was open for 1% of the time, Pallas kernels for 17%

profile of v10, /device:TPU:0, one launch (start us, length us, event | category | flops | bytes accessed | tf_op | source)
XLA Modules:
  0.0 69.6 jit_solution(2570194473061274309)
XLA Ops:
  0.0 2.0 %copy.14.cells = s32[2048,1]{1,0:T(8,128)} copy(s32[2048,1]{0,1:T(1,128)} %bitcast.15) | data formatting | bytes 16384 | tf_op jit(solution)/shard_map/reshape | solution.py:273
  2.0 2.1 %copy.15.offsets = s32[2048,1]{1,0:T(8,128)} copy(s32[2048,1]{0,1:T(1,128)} %bitcast.16) | data formatting | bytes 16384 | tf_op jit(solution)/shard_map/reshape | solution.py:274
  4.1 6.2 %shard_map.128 = bf16[8,272,128]{2,1,0:T(8,128)(2,1)} custom-call(s32[1,2048]{1,0:T(1,128)} %bitcast.17, s32[2048,1]{1,0:T(8,128)} %copy.14.cells, s32[2048,1]{1,0:T(8,128)} %copy.15.offsets, bf16[2048,128]{1,0:T(8,128)(2,1)} %values.1), custom_call_target="tpu_custom_call" | custom-call | tf_op jit(solution)/shard_map/pallas_call | solution.py:265
  10.3 7.3 %all-to-all-start = ((bf16[8,272,128]{2,1,0:T(8,128)(2,1)}), bf16[8,272,128]{2,1,0:T(8,128)(2,1)S(1)}, u32[]{:S(2)}, u32[]{:S(2)}) async-start(bf16[8,272,128]{2,1,0:T(8,128)(2,1)} %shard_map.128), calls=%async_computation | async-start | bytes 1114112 | tf_op jit(solution)/shard_map/all_to_all | solution.py:277
  17.6 0.5 convert_convert_fusion.tbl
  18.1 6.4 %shard_map.127.acc = f32[2048,256]{1,0:T(8,128)} custom-call(bf16[2048,128]{1,0:T(8,128)(2,1)} %v_ref.1, s32[1,2048]{1,0:T(1,128)} %bitcast.20, s32[1,2048]{1,0:T(1,128)} %bitcast.21, f32[8]{0:T(128)} %convert_convert_fusion.tbl), custom_call_target="tpu_custom_call" | custom-call | flops 2147483648 | bytes 540672 | tf_op jit(solution)/shard_map/pallas_call | solution.py:100
  24.5 8.3 %all-to-all-done.got = bf16[8,272,128]{2,1,0:T(8,128)(2,1)S(1)} async-done(((bf16[8,272,128]{2,1,0:T(8,128)(2,1)}), bf16[8,272,128]{2,1,0:T(8,128)(2,1)S(1)}, u32[]{:S(2)}, u32[]{:S(2)}) %all-to-all-start) | async-done | bytes 557088 | tf_op jit(solution)/shard_map/all_to_all | solution.py:277
  32.8 0.0 copy-start
  32.8 0.8 %copy-done = bf16[8,272,128]{2,1,0:T(8,128)(2,1)} copy-done((bf16[8,272,128]{2,1,0:T(8,128)(2,1)}, bf16[8,272,128]{2,1,0:T(8,128)(2,1)S(1)}, u32[]{:S(2)}) %copy-start) | copy-done | bytes 557080
  33.6 3.9 %shard_map.129 = bf16[768,128]{1,0:T(8,128)(2,1)} custom-call(f32[2048,256]{1,0:T(8,128)} %shard_map.127.acc, bf16[8,272,128]{2,1,0:T(8,128)(2,1)} %copy-done, f32[8]{0:T(128)} %convert_convert_fusion.tbl, f32[1,128]{1,0:T(1,128)} %bitcast.22), custom_call_target="tpu_custom_call" | custom-call | flops 805306368 | bytes 540672 | tf_op jit(solution)/shard_map/pallas_call | solution.py:121
  37.5 3.4 %collective-permute-start = (bf16[3,256,128]{2,1,0:T(8,128)(2,1)}, bf16[3,256,128]{2,1,0:T(8,128)(2,1)S(1)}, u32[]{:S(2)}, u32[]{:S(2)}) collective-permute-start(bf16[3,256,128]{2,1,0:T(8,128)(2,1)} %bitcast.13), channel_id=1, source_target_pairs={{0,1},{1,2},{2,3},{3,4},{4,5},{5,6},{6,7},{8,9},{9,10},{10,11},{11... | collective-permute-start | bytes 589832 | tf_op jit(solution)/shard_map/ppermute | solution.py:18
  40.8 5.3 %shard_map.130 = bf16[1280,128]{1,0:T(8,128)(2,1)} custom-call(f32[2048,256]{1,0:T(8,128)} %shard_map.127.acc, bf16[8,272,128]{2,1,0:T(8,128)(2,1)} %copy-done, f32[8]{0:T(128)} %convert_convert_fusion.tbl, f32[1,128]{1,0:T(1,128)} %bitcast.23), custom_call_target="tpu_custom_call" | custom-call | flops 1342177280 | bytes 540672 | tf_op jit(solution)/shard_map/pallas_call | solution.py:121
  46.2 0.0 collective-permute-done.above
  46.2 0.0 copy-start.1
  46.2 0.7 copy-done.1
  46.8 4.3 %shard_map.131 = bf16[8,2,64,256]{3,2,1,0:T(8,128)(2,1)} custom-call(bf16[3,256,128]{2,1,0:T(8,128)(2,1)} %copy-done.1, bf16[5,256,128]{2,1,0:T(8,128)(2,1)} %bitcast.12, bf16[3,256,128]{2,1,0:T(8,128)(2,1)} %bitcast.14, bf16[3,3,128,128]{3,2,1,0:T(8,128)(2,1)} %w1.1, f32[1,128]{1,0:T(1,128)} %bitcast.19, bf16[3,3,128,256]{3,2,1,0:T(8,128)(2,1)} %w2.1, ...), custom_call_target="tpu_custom_call" | custom-call | tf_op jit(solution)/shard_map/pallas_call | solution.py:208
  51.2 17.7 %all_to_all.10 = bf16[8,2,64,256]{3,2,1,0:T(8,128)(2,1)S(1)} all-to-all(bf16[8,2,64,256]{3,2,1,0:T(8,128)(2,1)} %shard_map.131), channel_id=1, replica_groups=mesh['member'=4,'band'=8] {'band'}, dimensions={0} | all-to-all | bytes 1048576 | tf_op jit(solution)/shard_map/all_to_all | solution.py:314
  68.8 0.8 %copy.17 = bf16[16,64,256]{2,1,0:T(8,128)(2,1)} copy(bf16[16,64,256]{2,1,0:T(8,128)(2,1)S(1)} %bitcast.11) | data formatting | bytes 1048576
Async XLA Ops:
  10.3 22.5 %all-to-all-start = ((bf16[8,272,128]{2,1,0:T(8,128)(2,1)}), bf16[8,272,128]{2,1,0:T(8,128)(2,1)S(1)}, u32[]{:S(2)}, u32[]{:S(2)}) async-start(bf16[8,272,128]{2,1,0:T(8,128)(2,1)} %shard_map.128), calls=%async_computation | async-start | bytes 1114112 | tf_op jit(solution)/shard_map/all_to_all | solution.py:277
  32.8 0.8 %copy-start = (bf16[8,272,128]{2,1,0:T(8,128)(2,1)}, bf16[8,272,128]{2,1,0:T(8,128)(2,1)S(1)}, u32[]{:S(2)}) copy-start(bf16[8,272,128]{2,1,0:T(8,128)(2,1)S(1)} %all-to-all-done.got) | copy-start | bytes 1671172
  37.5 8.7 %collective-permute-start = (bf16[3,256,128]{2,1,0:T(8,128)(2,1)}, bf16[3,256,128]{2,1,0:T(8,128)(2,1)S(1)}, u32[]{:S(2)}, u32[]{:S(2)}) collective-permute-start(bf16[3,256,128]{2,1,0:T(8,128)(2,1)} %bitcast.13), channel_id=1, source_target_pairs={{0,1},{1,2},{2,3},{3,4},{4,5},{5,6},{6,7},{8,9},{9,10},{10,11},{11... | collective-permute-start | bytes 589832 | tf_op jit(solution)/shard_map/ppermute | solution.py:18
  46.2 0.7 copy-start.1

commit v11 on v9

--- a/solution.py
+++ b/solution.py
@@ -33,54 +33,48 @@
     return w
 
 
-def deposit_rows(aug, cells_s, w_s, block):
+def deposit_rows(aug, cells_s, w_s, first, count):
     n = aug.shape[0]
     chunk = min(n, OBS_CHUNK)
     ids = lax.broadcasted_iota(jnp.int32, (CELL_BLOCK, chunk), 0).astype(jnp.float32)
     ids = ids.astype(jnp.bfloat16)
-    base = block * CELL_BLOCK
-    total = jnp.zeros((CELL_BLOCK, aug.shape[1]), jnp.float32)
+    zero = jnp.zeros((), jnp.bfloat16)
+    total = jnp.zeros((count * CELL_BLOCK, aug.shape[1]), jnp.float32)
     for start in range(0, n, chunk):
-        rel = cells_s[:, start : start + chunk] - base
-        rel = jnp.where((rel >= 0) & (rel < CELL_BLOCK), rel, -1).astype(jnp.float32)
+        cells = cells_s[:, start : start + chunk]
         w = w_s[:, start : start + chunk].astype(jnp.bfloat16)
-        table = jnp.where(rel.astype(jnp.bfloat16) == ids, w, jnp.zeros((), jnp.bfloat16))
+        parts = []
+        for k in range(count):
+            rel = cells - (first + k) * CELL_BLOCK
+            rel = jnp.where((rel >= 0) & (rel < CELL_BLOCK), rel, -1).astype(jnp.float32)
+            parts.append(jnp.where(rel.astype(jnp.bfloat16) == ids, w, zero))
+        table = parts[0] if count == 1 else jnp.concatenate(parts, axis=0)
         total = total + jnp.dot(table, aug[start : start + chunk, :], preferred_element_type=jnp.float32)
     return total
 
 
-def sat_kernel(v_ref, c_ref, o_ref, tbl, out, aug, cells_s, w_s):
-    block = pl.program_id(0)
-
-    @pl.when(block == 0)
-    def _():
-        n, d_in = v_ref.shape
-        aug[:, :d_in] = v_ref[...]
-        aug[:, d_in:] = jnp.ones((n, aug.shape[1] - d_in), jnp.bfloat16)
-        cells_s[...] = c_ref[...]
-        w_s[...] = lookup(o_ref[...], tbl, 0)
-
-    out[...] = deposit_rows(aug, cells_s, w_s, block)
-
-
-def station_kernel(capacity, first, acc, got, tbl, embed, out, aug, cells_s, w_s):
-    step = pl.program_id(0)
-    block = step + first
+def sat_kernel(split, v_ref, c_ref, o_ref, tbl, low, high, aug, cells_s, w_s):
+    n, d_in = v_ref.shape
+    aug[:, :d_in] = v_ref[...]
+    aug[:, d_in:] = jnp.ones((n, aug.shape[1] - d_in), jnp.bfloat16)
+    cells_s[...] = c_ref[...]
+    w_s[...] = lookup(o_ref[...], tbl, 0)
+    high[...] = deposit_rows(aug, cells_s, w_s, split, high.shape[0] // CELL_BLOCK)
+    low[...] = deposit_rows(aug, cells_s, w_s, 0, split)
+
+
+def station_kernel(capacity, first, count, acc, got, tbl, embed, out, aug, cells_s, w_s):
     d_in = out.shape[1]
-
-    @pl.when(step == 0)
-    def _():
-        bands = got.shape[0]
-        aug[:, d_in:] = jnp.ones((aug.shape[0], aug.shape[1] - d_in), jnp.bfloat16)
-        for t in range(bands):
-            aug[t * capacity : (t + 1) * capacity, :d_in] = got[t, :capacity, :]
-            meta = got[t, capacity : capacity + 6, :].astype(jnp.float32).astype(jnp.int32)
-            for h in range(2):
-                at = slice(t * capacity + h * d_in, t * capacity + (h + 1) * d_in)
-                cells_s[:, at] = meta[h : h + 1] * 64 + meta[2 + h : 3 + h]
-                w_s[:, at] = lookup(meta[4 + h : 5 + h], tbl, 1)
-
-    total = acc[...] + deposit_rows(aug, cells_s, w_s, block)
+    bands = got.shape[0]
+    aug[:, d_in:] = jnp.ones((aug.shape[0], aug.shape[1] - d_in), jnp.bfloat16)
+    for t in range(bands):
+        aug[t * capacity : (t + 1) * capacity, :d_in] = got[t, :capacity, :]
+        meta = got[t, capacity : capacity + 6, :].astype(jnp.float32).astype(jnp.int32)
+        for h in range(2):
+            at = slice(t * capacity + h * d_in, t * capacity + (h + 1) * d_in)
+            cells_s[:, at] = meta[h : h + 1] * 64 + meta[2 + h : 3 + h]
+            w_s[:, at] = lookup(meta[4 + h : 5 + h], tbl, 1)
+    total = acc[...] + deposit_rows(aug, cells_s, w_s, first, count)
     sums = total[:, :d_in]
     density = total[:, d_in:]
     grid = sums / jnp.maximum(density, 1.0) + density * embed[...]
@@ -94,15 +88,20 @@
 SMEM = pl.BlockSpec(memory_space=pltpu.SMEM)
 
 
-def sat_deposit(values, cells, offsets, table, total_cells):
+def sat_deposit(values, cells, offsets, table, split, total_cells):
     n, d_in = values.shape
     wide = 2 * d_in
+    low_rows = split * CELL_BLOCK
+    high_rows = total_cells - low_rows
     return pl.pallas_call(
-        sat_kernel,
-        grid=(total_cells // CELL_BLOCK,),
+        functools.partial(sat_kernel, split),
+        grid=(1,),
         in_specs=[whole((n, d_in)), whole((1, n)), whole((1, n)), SMEM],
-        out_specs=pl.BlockSpec((CELL_BLOCK, wide), lambda c: (c, 0)),
-        out_shape=jax.ShapeDtypeStruct((total_cells, wide), jnp.float32),
+        out_specs=[whole((low_rows, wide)), whole((high_rows, wide))],
+        out_shape=[
+            jax.ShapeDtypeStruct((low_rows, wide), jnp.float32),
+            jax.ShapeDtypeStruct((high_rows, wide), jnp.float32),
+        ],
         scratch_shapes=[
             pltpu.VMEM((n, wide), jnp.bfloat16),
             pltpu.VMEM((1, n), jnp.int32),
@@ -118,24 +117,20 @@
     bands, rows, d_in = got.shape
     n = bands * capacity
     wide = 2 * d_in
+    cells = count * CELL_BLOCK
     return pl.pallas_call(
-        functools.partial(station_kernel, capacity, first),
-        grid=(count,),
-        in_specs=[
-            pl.BlockSpec((CELL_BLOCK, wide), lambda c: (c + first, 0)),
-            whole((bands, rows, d_in)),
-            SMEM,
-            whole((1, d_in)),
-        ],
-        out_specs=pl.BlockSpec((CELL_BLOCK, d_in), lambda c: (c, 0)),
-        out_shape=jax.ShapeDtypeStruct((count * CELL_BLOCK, d_in), jnp.bfloat16),
+        functools.partial(station_kernel, capacity, first, count),
+        grid=(1,),
+        in_specs=[whole((cells, wide)), whole((bands, rows, d_in)), SMEM, whole((1, d_in))],
+        out_specs=whole((cells, d_in)),
+        out_shape=jax.ShapeDtypeStruct((cells, d_in), jnp.bfloat16),
         scratch_shapes=[
             pltpu.VMEM((n, wide), jnp.bfloat16),
             pltpu.VMEM((1, n), jnp.int32),
             pltpu.VMEM((1, n), jnp.float32),
         ],
         cost_estimate=pl.CostEstimate(
-            flops=2 * count * CELL_BLOCK * n * wide, transcendentals=0, bytes_accessed=2 * n * (d_in + 4)
+            flops=2 * cells * n * wide, transcendentals=0, bytes_accessed=2 * n * (d_in + 4)
         ),
     )(acc, got, table, embed.reshape(1, d_in))
 
@@ -299,19 +294,18 @@
     d_in = obs_values.shape[1]
     band_cells = LAT_DEV * LON
     table = weights_of(jnp.arange(8, dtype=jnp.int32)).astype(jnp.float32)
-    sat_acc = sat_deposit(sat_values, sat_cell, sat_offset, table, band_cells)
+    halo = 3
+    lat_blocks = band_cells // CELL_BLOCK
+    high_blocks = halo * LON // CELL_BLOCK
+    low_blocks = lat_blocks - high_blocks
+    sat_low, sat_high = sat_deposit(sat_values, sat_cell, sat_offset, table, low_blocks, band_cells)
     got = route(obs_values, obs_band, obs_cell, obs_offset, bands)
     capacity = obs_values.shape[0] // 8
-    halo = 3
-    lat_blocks = band_cells // CELL_BLOCK
-    rows_per_block = CELL_BLOCK // LON
-    high = station_deposit(
-        sat_acc, got, table, density_embed, capacity, lat_blocks - halo // rows_per_block, halo // rows_per_block
-    ).reshape(halo, LON, d_in)
+    high = station_deposit(sat_high, got, table, density_embed, capacity, low_blocks, high_blocks)
+    high = high.reshape(halo, LON, d_in)
     above = passed_along(high, "band", 1)
-    low = station_deposit(
-        sat_acc, got, table, density_embed, capacity, 0, lat_blocks - halo // rows_per_block
-    ).reshape(LAT_DEV - halo, LON, d_in)
+    low = station_deposit(sat_low, got, table, density_embed, capacity, 0, low_blocks)
+    low = low.reshape(LAT_DEV - halo, LON, d_in)
     spread = convolve(bands, above, low, high, conv1_weight, conv1_bias, conv2_weight, conv2_bias, proj_weight)
     gathered = lax.all_to_all(spread, "band", split_axis=0, concat_axis=0, tiled=True)
     return gathered.reshape((bands * spread.shape[1],) + spread.shape[2:])

time: 66.8 us -> 65.9 us (0.987)
  Pallas kernels: 26.9 us -> 23 us
  waiting for transfers between devices: 8.31 us -> 10.1 us
  blocking collectives: 17.6 us -> 19 us
    pallas_call x3, Pallas kernels: 15.6 us -> 11.7 us  [the longest x2 7.09 us: station_deposit(): pl.pallas_call(functools.partial(station_kernel, capacity, first, count),...]
    all_to_all x1, waiting for transfers between devices: 8.31 us -> 10.1 us  [route(): lax.all_to_all(packet, 'band', split_axis=0, concat_axis=0, tiled=True)]
    all_to_all x1, blocking collectives: 17.6 us -> 19 us  [body(): lax.all_to_all(spread, 'band', split_axis=0, concat_axis=0, tiled=True)]
  transfers between devices with their start and end apart: 2 -> 2, of which waited for: 1 -> 1; matrix products, arithmetic and copies ran while one was open for 1% -> 1% of each run, Pallas kernels for 18% -> 13%
where the time goes in v11:
time: 65.9 us; the launch traced here: 65.5 us
  Pallas kernels  23 us (35%)
  blocking collectives  19 us (29%)
  starting transfers between devices  10.6 us (16%)
  waiting for transfers between devices  10.1 us (15%)
  local copies, waits for them, and re-layouts  2.28 us (3%)
    all_to_all x1, blocking collectives, body(): lax.all_to_all(spread, 'band', split_axis=0, concat_axis=0, tiled=True)  19 us
    all_to_all x1, waiting for transfers between devices, route(): lax.all_to_all(packet, 'band', split_axis=0, concat_axis=0, tiled=True)  10.1 us
    all_to_all x1, starting transfers between devices, route(): lax.all_to_all(packet, 'band', split_axis=0, concat_axis=0, tiled=True)  7.28 us
    pallas_call x2, Pallas kernels, station_deposit(): pl.pallas_call(functools.partial(station_kernel, capacity, first, count),...  7.09 us
    pallas_call x1, Pallas kernels, route(): pl.pallas_call(functools.partial(route_kernel, capacity), in_specs=[vmem]...  6.92 us
    pallas_call x1, Pallas kernels, sat_deposit(): pl.pallas_call(functools.partial(sat_kernel, split), grid=(1,), in_specs=...  4.61 us
    pallas_call x1, Pallas kernels, convolve(): pl.pallas_call(conv_kernel, in_specs=[vmem] * 8, out_specs=vmem, out_shap...  4.35 us
    ppermute x1, starting transfers between devices, passed_along(): return lax.ppermute(value, axis, pairs)  3.37 us
  transfers between devices with their start and end apart: 2, of which 1 were waited for; matrix products, arithmetic and copies ran while one was open for 1% of the time, Pallas kernels for 13%

profile of v11, /device:TPU:0, one launch (start us, length us, event | category | flops | bytes accessed | tf_op | source)
XLA Modules:
  0.0 65.5 jit_solution(5114776786819466332)
XLA Ops:
  0.0 6.9 %shard_map.128 = bf16[8,272,128]{2,1,0:T(8,128)(2,1)} custom-call(s32[1,2048]{1,0:T(1,128)} %bitcast.15, s32[1,2048]{1,0:T(1,128)} %bitcast.16, s32[1,2048]{1,0:T(1,128)} %bitcast.17, bf16[2048,128]{1,0:T(8,128)(2,1)} %values.1), custom_call_target="tpu_custom_call" | custom-call | tf_op jit(solution)/shard_map/pallas_call | solution.py:263
  6.9 7.3 %all-to-all-start = ((bf16[8,272,128]{2,1,0:T(8,128)(2,1)}), bf16[8,272,128]{2,1,0:T(8,128)(2,1)S(1)}, u32[]{:S(2)}, u32[]{:S(2)}) async-start(bf16[8,272,128]{2,1,0:T(8,128)(2,1)} %shard_map.128), calls=%async_computation | async-start | bytes 1114112 | tf_op jit(solution)/shard_map/all_to_all | solution.py:274
  14.2 0.5 convert_convert_fusion.tbl
  14.7 4.6 %shard_map.127 = (f32[1280,256]{1,0:T(8,128)}, f32[768,256]{1,0:T(8,128)}) custom-call(bf16[2048,128]{1,0:T(8,128)(2,1)} %v_ref.1, s32[1,2048]{1,0:T(1,128)} %bitcast.20, s32[1,2048]{1,0:T(1,128)} %bitcast.21, f32[8]{0:T(128)} %convert_convert_fusion.tbl), custom_call_target="tpu_custom_call" | custom-call | flops 2147483648 | bytes 540672 | tf_op jit(solution)/shard_map/pallas_call | solution.py:96
  19.3 10.1 %all-to-all-done.got = bf16[8,272,128]{2,1,0:T(8,128)(2,1)S(1)} async-done(((bf16[8,272,128]{2,1,0:T(8,128)(2,1)}), bf16[8,272,128]{2,1,0:T(8,128)(2,1)S(1)}, u32[]{:S(2)}, u32[]{:S(2)}) %all-to-all-start) | async-done | bytes 557088 | tf_op jit(solution)/shard_map/all_to_all | solution.py:274
  29.4 0.0 copy-start
  29.4 0.8 %copy-done = bf16[8,272,128]{2,1,0:T(8,128)(2,1)} copy-done((bf16[8,272,128]{2,1,0:T(8,128)(2,1)}, bf16[8,272,128]{2,1,0:T(8,128)(2,1)S(1)}, u32[]{:S(2)}) %copy-start) | copy-done | bytes 557080
  30.2 3.1 %shard_map.129 = bf16[768,128]{1,0:T(8,128)(2,1)} custom-call(f32[768,256]{1,0:T(8,128)} %get-tuple-element.7.acc, bf16[8,272,128]{2,1,0:T(8,128)(2,1)} %copy-done, f32[8]{0:T(128)} %convert_convert_fusion.tbl, f32[1,128]{1,0:T(1,128)} %bitcast.22), custom_call_target="tpu_custom_call" | custom-call | flops 805306368 | bytes 540672 | tf_op jit(solution)/shard_map/pallas_call | solution.py:121
  33.4 3.4 %collective-permute-start = (bf16[3,256,128]{2,1,0:T(8,128)(2,1)}, bf16[3,256,128]{2,1,0:T(8,128)(2,1)S(1)}, u32[]{:S(2)}, u32[]{:S(2)}) collective-permute-start(bf16[3,256,128]{2,1,0:T(8,128)(2,1)} %bitcast.13), channel_id=1, source_target_pairs={{0,1},{1,2},{2,3},{3,4},{4,5},{5,6},{6,7},{8,9},{9,10},{10,11},{11... | collective-permute-start | bytes 589832 | tf_op jit(solution)/shard_map/ppermute | solution.py:18
  36.7 3.9 %shard_map.130 = bf16[1280,128]{1,0:T(8,128)(2,1)} custom-call(f32[1280,256]{1,0:T(8,128)} %get-tuple-element.8.acc, bf16[8,272,128]{2,1,0:T(8,128)(2,1)} %copy-done, f32[8]{0:T(128)} %convert_convert_fusion.tbl, f32[1,128]{1,0:T(1,128)} %bitcast.23), custom_call_target="tpu_custom_call" | custom-call | flops 1342177280 | bytes 540672 | tf_op jit(solution)/shard_map/pallas_call | solution.py:121
  40.7 0.0 collective-permute-done.above
  40.7 0.0 copy-start.1
  40.7 0.7 %copy-done.1 = bf16[3,256,128]{2,1,0:T(8,128)(2,1)} copy-done((bf16[3,256,128]{2,1,0:T(8,128)(2,1)}, bf16[3,256,128]{2,1,0:T(8,128)(2,1)S(1)}, u32[]{:S(2)}) %copy-start.1) | copy-done | bytes 196632
  41.4 4.3 %shard_map.131 = bf16[8,2,64,256]{3,2,1,0:T(8,128)(2,1)} custom-call(bf16[3,256,128]{2,1,0:T(8,128)(2,1)} %copy-done.1, bf16[5,256,128]{2,1,0:T(8,128)(2,1)} %bitcast.12, bf16[3,256,128]{2,1,0:T(8,128)(2,1)} %bitcast.14, bf16[3,3,128,128]{3,2,1,0:T(8,128)(2,1)} %w1.1, f32[1,128]{1,0:T(1,128)} %bitcast.19, bf16[3,3,128,256]{3,2,1,0:T(8,128)(2,1)} %w2.1, ...), custom_call_target="tpu_custom_call" | custom-call | tf_op jit(solution)/shard_map/pallas_call | solution.py:203
  45.7 19.0 %all_to_all.10 = bf16[8,2,64,256]{3,2,1,0:T(8,128)(2,1)S(1)} all-to-all(bf16[8,2,64,256]{3,2,1,0:T(8,128)(2,1)} %shard_map.131), channel_id=1, replica_groups=mesh['member'=4,'band'=8] {'band'}, dimensions={0} | all-to-all | bytes 1048576 | tf_op jit(solution)/shard_map/all_to_all | solution.py:310
  64.7 0.8 %copy.15 = bf16[16,64,256]{2,1,0:T(8,128)(2,1)} copy(bf16[16,64,256]{2,1,0:T(8,128)(2,1)S(1)} %bitcast.11) | data formatting | bytes 1048576
Async XLA Ops:
  6.9 22.5 %all-to-all-start = ((bf16[8,272,128]{2,1,0:T(8,128)(2,1)}), bf16[8,272,128]{2,1,0:T(8,128)(2,1)S(1)}, u32[]{:S(2)}, u32[]{:S(2)}) async-start(bf16[8,272,128]{2,1,0:T(8,128)(2,1)} %shard_map.128), calls=%async_computation | async-start | bytes 1114112 | tf_op jit(solution)/shard_map/all_to_all | solution.py:274
  29.4 0.8 %copy-start = (bf16[8,272,128]{2,1,0:T(8,128)(2,1)}, bf16[8,272,128]{2,1,0:T(8,128)(2,1)S(1)}, u32[]{:S(2)}) copy-start(bf16[8,272,128]{2,1,0:T(8,128)(2,1)S(1)} %all-to-all-done.got) | copy-start | bytes 1671172
  33.4 7.3 %collective-permute-start = (bf16[3,256,128]{2,1,0:T(8,128)(2,1)}, bf16[3,256,128]{2,1,0:T(8,128)(2,1)S(1)}, u32[]{:S(2)}, u32[]{:S(2)}) collective-permute-start(bf16[3,256,128]{2,1,0:T(8,128)(2,1)} %bitcast.13), channel_id=1, source_target_pairs={{0,1},{1,2},{2,3},{3,4},{4,5},{5,6},{6,7},{8,9},{9,10},{10,11},{11... | collective-permute-start | bytes 589832 | tf_op jit(solution)/shard_map/ppermute | solution.py:18
  40.7 0.7 %copy-start.1 = (bf16[3,256,128]{2,1,0:T(8,128)(2,1)}, bf16[3,256,128]{2,1,0:T(8,128)(2,1)S(1)}, u32[]{:S(2)}) copy-start(bf16[3,256,128]{2,1,0:T(8,128)(2,1)S(1)} %collective-permute-done.above) | copy-start | bytes 589828

commit v12 on v11

--- a/solution.py
+++ b/solution.py
@@ -24,6 +24,7 @@
 
 CELL_BLOCK = 256
 OBS_CHUNK = 2048
+ROUTE_GROUP = 8
 
 
 def lookup(codes, table, shift):
@@ -240,20 +241,28 @@
     per_row = capacity // d_in
     one = jnp.ones((), jnp.bfloat16)
     zero = jnp.zeros((), jnp.bfloat16)
-    for b in range(bands):
-        mine = jnp.where(t == b, rank, -1).astype(jnp.float32).astype(jnp.bfloat16)
-        table = jnp.where(mine == slots, one, zero)
-        out[b, :capacity, :] = jnp.dot(
-            table, values[...], preferred_element_type=jnp.float32
-        ).astype(out.dtype)
+    group = min(bands, ROUTE_GROUP)
+    for g in range(0, bands, group):
+        parts = []
+        for b in range(g, g + group):
+            mine = jnp.where(t == b, rank, -1).astype(jnp.float32).astype(jnp.bfloat16)
+            parts.append(jnp.where(mine == slots, one, zero))
+        table = jnp.concatenate(parts, axis=0) if group > 1 else parts[0]
+        res = jnp.dot(table, values[...], preferred_element_type=jnp.float32).astype(out.dtype)
         sent = lax.dot_general(
             meta, table, (((1,), (1,)), ((), ())), preferred_element_type=jnp.float32
         ).astype(out.dtype)
-        for m in range(3):
-            for h in range(per_row):
-                row = capacity + m * per_row + h
-                out[b, row : row + 1, :] = sent[m : m + 1, h * d_in : (h + 1) * d_in]
-        out[b, capacity + 3 * per_row :, :] = jnp.zeros((rows - capacity - 3 * per_row, d_in), out.dtype)
+        for k in range(group):
+            b = g + k
+            out[b, :capacity, :] = res[k * capacity : (k + 1) * capacity]
+            for m in range(3):
+                for h in range(per_row):
+                    row = capacity + m * per_row + h
+                    lane = k * capacity + h * d_in
+                    out[b, row : row + 1, :] = sent[m : m + 1, lane : lane + d_in]
+            out[b, capacity + 3 * per_row :, :] = jnp.zeros(
+                (rows - capacity - 3 * per_row, d_in), out.dtype
+            )
 
 
 def route(obs_values, obs_band, obs_cell, obs_offset, bands):

time: 65.9 us -> 66.2 us (level)
  no operation moved by 1% of the time
where the time goes in v12:
time: 66.2 us; the launch traced here: 65.7 us
  Pallas kernels  23.2 us (35%)
  blocking collectives  19 us (29%)
  starting transfers between devices  10.6 us (16%)
  waiting for transfers between devices  10.1 us (15%)
  local copies, waits for them, and re-layouts  2.28 us (3%)
    all_to_all x1, blocking collectives, body(): lax.all_to_all(spread, 'band', split_axis=0, concat_axis=0, tiled=True)  19 us
    all_to_all x1, waiting for transfers between devices, route(): lax.all_to_all(packet, 'band', split_axis=0, concat_axis=0, tiled=True)  10.1 us
    all_to_all x1, starting transfers between devices, route(): lax.all_to_all(packet, 'band', split_axis=0, concat_axis=0, tiled=True)  7.28 us
    pallas_call x1, Pallas kernels, route(): pl.pallas_call(functools.partial(route_kernel, capacity), in_specs=[vmem]...  7.13 us
    pallas_call x2, Pallas kernels, station_deposit(): pl.pallas_call(functools.partial(station_kernel, capacity, first, count),...  7.09 us
    pallas_call x1, Pallas kernels, sat_deposit(): pl.pallas_call(functools.partial(sat_kernel, split), grid=(1,), in_specs=...  4.61 us
    pallas_call x1, Pallas kernels, convolve(): pl.pallas_call(conv_kernel, in_specs=[vmem] * 8, out_specs=vmem, out_shap...  4.35 us
    ppermute x1, starting transfers between devices, passed_along(): return lax.ppermute(value, axis, pairs)  3.37 us
  transfers between devices with their start and end apart: 2, of which 1 were waited for; matrix products, arithmetic and copies ran while one was open for 1% of the time, Pallas kernels for 13%

profile of v12, /device:TPU:0, one launch (start us, length us, event | category | flops | bytes accessed | tf_op | source)
XLA Modules:
  0.0 65.7 jit_solution(7424566320510585848)
XLA Ops:
  0.0 7.1 %shard_map.128 = bf16[8,272,128]{2,1,0:T(8,128)(2,1)} custom-call(s32[1,2048]{1,0:T(1,128)} %bitcast.15, s32[1,2048]{1,0:T(1,128)} %bitcast.16, s32[1,2048]{1,0:T(1,128)} %bitcast.17, bf16[2048,128]{1,0:T(8,128)(2,1)} %values.1), custom_call_target="tpu_custom_call" | custom-call | tf_op jit(solution)/shard_map/pallas_call | solution.py:272
  7.1 7.3 %all-to-all-start = ((bf16[8,272,128]{2,1,0:T(8,128)(2,1)}), bf16[8,272,128]{2,1,0:T(8,128)(2,1)S(1)}, u32[]{:S(2)}, u32[]{:S(2)}) async-start(bf16[8,272,128]{2,1,0:T(8,128)(2,1)} %shard_map.128), calls=%async_computation | async-start | bytes 1114112 | tf_op jit(solution)/shard_map/all_to_all | solution.py:283
  14.4 0.5 convert_convert_fusion.tbl
  14.9 4.6 %shard_map.127 = (f32[1280,256]{1,0:T(8,128)}, f32[768,256]{1,0:T(8,128)}) custom-call(bf16[2048,128]{1,0:T(8,128)(2,1)} %v_ref.1, s32[1,2048]{1,0:T(1,128)} %bitcast.20, s32[1,2048]{1,0:T(1,128)} %bitcast.21, f32[8]{0:T(128)} %convert_convert_fusion.tbl), custom_call_target="tpu_custom_call" | custom-call | flops 2147483648 | bytes 540672 | tf_op jit(solution)/shard_map/pallas_call | solution.py:97
  19.5 10.1 %all-to-all-done.got = bf16[8,272,128]{2,1,0:T(8,128)(2,1)S(1)} async-done(((bf16[8,272,128]{2,1,0:T(8,128)(2,1)}), bf16[8,272,128]{2,1,0:T(8,128)(2,1)S(1)}, u32[]{:S(2)}, u32[]{:S(2)}) %all-to-all-start) | async-done | bytes 557088 | tf_op jit(solution)/shard_map/all_to_all | solution.py:283
  29.6 0.0 copy-start
  29.6 0.8 %copy-done = bf16[8,272,128]{2,1,0:T(8,128)(2,1)} copy-done((bf16[8,272,128]{2,1,0:T(8,128)(2,1)}, bf16[8,272,128]{2,1,0:T(8,128)(2,1)S(1)}, u32[]{:S(2)}) %copy-start) | copy-done | bytes 557080
  30.4 3.1 %shard_map.129 = bf16[768,128]{1,0:T(8,128)(2,1)} custom-call(f32[768,256]{1,0:T(8,128)} %get-tuple-element.7.acc, bf16[8,272,128]{2,1,0:T(8,128)(2,1)} %copy-done, f32[8]{0:T(128)} %convert_convert_fusion.tbl, f32[1,128]{1,0:T(1,128)} %bitcast.22), custom_call_target="tpu_custom_call" | custom-call | flops 805306368 | bytes 540672 | tf_op jit(solution)/shard_map/pallas_call | solution.py:122
  33.6 3.4 %collective-permute-start = (bf16[3,256,128]{2,1,0:T(8,128)(2,1)}, bf16[3,256,128]{2,1,0:T(8,128)(2,1)S(1)}, u32[]{:S(2)}, u32[]{:S(2)}) collective-permute-start(bf16[3,256,128]{2,1,0:T(8,128)(2,1)} %bitcast.13), channel_id=1, source_target_pairs={{0,1},{1,2},{2,3},{3,4},{4,5},{5,6},{6,7},{8,9},{9,10},{10,11},{11... | collective-permute-start | bytes 589832 | tf_op jit(solution)/shard_map/ppermute | solution.py:18
  36.9 3.9 %shard_map.130 = bf16[1280,128]{1,0:T(8,128)(2,1)} custom-call(f32[1280,256]{1,0:T(8,128)} %get-tuple-element.8.acc, bf16[8,272,128]{2,1,0:T(8,128)(2,1)} %copy-done, f32[8]{0:T(128)} %convert_convert_fusion.tbl, f32[1,128]{1,0:T(1,128)} %bitcast.23), custom_call_target="tpu_custom_call" | custom-call | flops 1342177280 | bytes 540672 | tf_op jit(solution)/shard_map/pallas_call | solution.py:122
  40.9 0.0 collective-permute-done.above
  40.9 0.0 copy-start.1
  40.9 0.7 %copy-done.1 = bf16[3,256,128]{2,1,0:T(8,128)(2,1)} copy-done((bf16[3,256,128]{2,1,0:T(8,128)(2,1)}, bf16[3,256,128]{2,1,0:T(8,128)(2,1)S(1)}, u32[]{:S(2)}) %copy-start.1) | copy-done | bytes 196632
  41.6 4.3 %shard_map.131 = bf16[8,2,64,256]{3,2,1,0:T(8,128)(2,1)} custom-call(bf16[3,256,128]{2,1,0:T(8,128)(2,1)} %copy-done.1, bf16[5,256,128]{2,1,0:T(8,128)(2,1)} %bitcast.12, bf16[3,256,128]{2,1,0:T(8,128)(2,1)} %bitcast.14, bf16[3,3,128,128]{3,2,1,0:T(8,128)(2,1)} %w1.1, f32[1,128]{1,0:T(1,128)} %bitcast.19, bf16[3,3,128,256]{3,2,1,0:T(8,128)(2,1)} %w2.1, ...), custom_call_target="tpu_custom_call" | custom-call | tf_op jit(solution)/shard_map/pallas_call | solution.py:204
  45.9 19.0 %all_to_all.10 = bf16[8,2,64,256]{3,2,1,0:T(8,128)(2,1)S(1)} all-to-all(bf16[8,2,64,256]{3,2,1,0:T(8,128)(2,1)} %shard_map.131), channel_id=1, replica_groups=mesh['member'=4,'band'=8] {'band'}, dimensions={0} | all-to-all | bytes 1048576 | tf_op jit(solution)/shard_map/all_to_all | solution.py:319
  64.9 0.8 %copy.15 = bf16[16,64,256]{2,1,0:T(8,128)(2,1)} copy(bf16[16,64,256]{2,1,0:T(8,128)(2,1)S(1)} %bitcast.11) | data formatting | bytes 1048576
Async XLA Ops:
  7.1 22.5 %all-to-all-start = ((bf16[8,272,128]{2,1,0:T(8,128)(2,1)}), bf16[8,272,128]{2,1,0:T(8,128)(2,1)S(1)}, u32[]{:S(2)}, u32[]{:S(2)}) async-start(bf16[8,272,128]{2,1,0:T(8,128)(2,1)} %shard_map.128), calls=%async_computation | async-start | bytes 1114112 | tf_op jit(solution)/shard_map/all_to_all | solution.py:283
  29.6 0.8 %copy-start = (bf16[8,272,128]{2,1,0:T(8,128)(2,1)}, bf16[8,272,128]{2,1,0:T(8,128)(2,1)S(1)}, u32[]{:S(2)}) copy-start(bf16[8,272,128]{2,1,0:T(8,128)(2,1)S(1)} %all-to-all-done.got) | copy-start | bytes 1671172
  33.6 7.3 %collective-permute-start = (bf16[3,256,128]{2,1,0:T(8,128)(2,1)}, bf16[3,256,128]{2,1,0:T(8,128)(2,1)S(1)}, u32[]{:S(2)}, u32[]{:S(2)}) collective-permute-start(bf16[3,256,128]{2,1,0:T(8,128)(2,1)} %bitcast.13), channel_id=1, source_target_pairs={{0,1},{1,2},{2,3},{3,4},{4,5},{5,6},{6,7},{8,9},{9,10},{10,11},{11... | collective-permute-start | bytes 589832 | tf_op jit(solution)/shard_map/ppermute | solution.py:18
  40.9 0.7 %copy-start.1 = (bf16[3,256,128]{2,1,0:T(8,128)(2,1)}, bf16[3,256,128]{2,1,0:T(8,128)(2,1)S(1)}, u32[]{:S(2)}) copy-start(bf16[3,256,128]{2,1,0:T(8,128)(2,1)S(1)} %collective-permute-done.above) | copy-start | bytes 589828

commit v13 on v11

--- a/solution.py
+++ b/solution.py
@@ -225,7 +225,7 @@
     return total - mask
 
 
-def route_kernel(capacity, target, cells, offsets, values, out):
+def route_kernel(capacity, target, cells, offsets, values, out, vaug):
     bands, rows, d_in = out.shape
     n = values.shape[0]
     t = target[...]
@@ -234,8 +234,10 @@
     rank = jnp.sum(mask * prefix_count(mask), axis=0, keepdims=True)
     c = cells[...]
     meta = jnp.concatenate(
-        [c // 64, c % 64, offsets[...] + 1, jnp.zeros((5, n), jnp.int32)], axis=0
-    ).astype(jnp.float32).astype(jnp.bfloat16)
+        [c // 64, c % 64, offsets[...] + 1, jnp.zeros((d_in - 3, n), jnp.int32)], axis=0
+    ).astype(jnp.float32)
+    vaug[:, :d_in] = values[...]
+    vaug[:, d_in:] = jnp.transpose(meta).astype(jnp.bfloat16)
     slots = lax.broadcasted_iota(jnp.int32, (capacity, n), 0).astype(jnp.float32).astype(jnp.bfloat16)
     per_row = capacity // d_in
     one = jnp.ones((), jnp.bfloat16)
@@ -243,12 +245,9 @@
     for b in range(bands):
         mine = jnp.where(t == b, rank, -1).astype(jnp.float32).astype(jnp.bfloat16)
         table = jnp.where(mine == slots, one, zero)
-        out[b, :capacity, :] = jnp.dot(
-            table, values[...], preferred_element_type=jnp.float32
-        ).astype(out.dtype)
-        sent = lax.dot_general(
-            meta, table, (((1,), (1,)), ((), ())), preferred_element_type=jnp.float32
-        ).astype(out.dtype)
+        res = jnp.dot(table, vaug[...], preferred_element_type=jnp.float32)
+        out[b, :capacity, :] = res[:, :d_in].astype(out.dtype)
+        sent = jnp.transpose(res[:, d_in:]).astype(out.dtype)
         for m in range(3):
             for h in range(per_row):
                 row = capacity + m * per_row + h
@@ -265,6 +264,7 @@
         in_specs=[vmem] * 4,
         out_specs=vmem,
         out_shape=jax.ShapeDtypeStruct((bands, capacity + META, d_in), jnp.bfloat16),
+        scratch_shapes=[pltpu.VMEM((obs_rows, 2 * d_in), jnp.bfloat16)],
     )(
         obs_band.reshape(1, obs_rows),
         obs_cell.reshape(1, obs_rows),

time: 65.9 us -> 64.1 us (0.973)
  Pallas kernels: 23 us -> 21.2 us
    pallas_call x1, Pallas kernels: 6.92 us -> 5.12 us  [route(): pl.pallas_call(functools.partial(route_kernel, capacity), in_specs=[vmem]...]
where the time goes in v13:
time: 64.1 us; the launch traced here: 63.7 us
  Pallas kernels  21.2 us (33%)
  blocking collectives  19 us (30%)
  starting transfers between devices  10.6 us (17%)
  waiting for transfers between devices  10.1 us (16%)
  local copies, waits for them, and re-layouts  2.28 us (4%)
    all_to_all x1, blocking collectives, body(): lax.all_to_all(spread, 'band', split_axis=0, concat_axis=0, tiled=True)  19 us
    all_to_all x1, waiting for transfers between devices, route(): lax.all_to_all(packet, 'band', split_axis=0, concat_axis=0, tiled=True)  10.1 us
    all_to_all x1, starting transfers between devices, route(): lax.all_to_all(packet, 'band', split_axis=0, concat_axis=0, tiled=True)  7.28 us
    pallas_call x2, Pallas kernels, station_deposit(): pl.pallas_call(functools.partial(station_kernel, capacity, first, count),...  7.09 us
    pallas_call x1, Pallas kernels, route(): pl.pallas_call(functools.partial(route_kernel, capacity), in_specs=[vmem]...  5.12 us
    pallas_call x1, Pallas kernels, sat_deposit(): pl.pallas_call(functools.partial(sat_kernel, split), grid=(1,), in_specs=...  4.61 us
    pallas_call x1, Pallas kernels, convolve(): pl.pallas_call(conv_kernel, in_specs=[vmem] * 8, out_specs=vmem, out_shap...  4.35 us
    ppermute x1, starting transfers between devices, passed_along(): return lax.ppermute(value, axis, pairs)  3.37 us
  transfers between devices with their start and end apart: 2, of which 1 were waited for; matrix products, arithmetic and copies ran while one was open for 1% of the time, Pallas kernels for 13%

profile of v13, /device:TPU:0, one launch (start us, length us, event | category | flops | bytes accessed | tf_op | source)
XLA Modules:
  0.0 63.7 jit_solution(3786099596384670456)
XLA Ops:
  0.0 5.1 %shard_map.128 = bf16[8,272,128]{2,1,0:T(8,128)(2,1)} custom-call(s32[1,2048]{1,0:T(1,128)} %bitcast.15, s32[1,2048]{1,0:T(1,128)} %bitcast.16, s32[1,2048]{1,0:T(1,128)} %bitcast.17, bf16[2048,128]{1,0:T(8,128)(2,1)} %values.1), custom_call_target="tpu_custom_call" | custom-call | tf_op jit(solution)/shard_map/pallas_call | solution.py:262
  5.1 7.3 %all-to-all-start = ((bf16[8,272,128]{2,1,0:T(8,128)(2,1)}), bf16[8,272,128]{2,1,0:T(8,128)(2,1)S(1)}, u32[]{:S(2)}, u32[]{:S(2)}) async-start(bf16[8,272,128]{2,1,0:T(8,128)(2,1)} %shard_map.128), calls=%async_computation | async-start | bytes 1114112 | tf_op jit(solution)/shard_map/all_to_all | solution.py:274
  12.4 0.5 convert_convert_fusion.tbl
  12.9 4.6 %shard_map.127 = (f32[1280,256]{1,0:T(8,128)}, f32[768,256]{1,0:T(8,128)}) custom-call(bf16[2048,128]{1,0:T(8,128)(2,1)} %v_ref.1, s32[1,2048]{1,0:T(1,128)} %bitcast.20, s32[1,2048]{1,0:T(1,128)} %bitcast.21, f32[8]{0:T(128)} %convert_convert_fusion.tbl), custom_call_target="tpu_custom_call" | custom-call | flops 2147483648 | bytes 540672 | tf_op jit(solution)/shard_map/pallas_call | solution.py:96
  17.5 10.1 %all-to-all-done.got = bf16[8,272,128]{2,1,0:T(8,128)(2,1)S(1)} async-done(((bf16[8,272,128]{2,1,0:T(8,128)(2,1)}), bf16[8,272,128]{2,1,0:T(8,128)(2,1)S(1)}, u32[]{:S(2)}, u32[]{:S(2)}) %all-to-all-start) | async-done | bytes 557088 | tf_op jit(solution)/shard_map/all_to_all | solution.py:274
  27.6 0.0 copy-start
  27.6 0.8 %copy-done = bf16[8,272,128]{2,1,0:T(8,128)(2,1)} copy-done((bf16[8,272,128]{2,1,0:T(8,128)(2,1)}, bf16[8,272,128]{2,1,0:T(8,128)(2,1)S(1)}, u32[]{:S(2)}) %copy-start) | copy-done | bytes 557080
  28.4 3.1 %shard_map.129 = bf16[768,128]{1,0:T(8,128)(2,1)} custom-call(f32[768,256]{1,0:T(8,128)} %get-tuple-element.7.acc, bf16[8,272,128]{2,1,0:T(8,128)(2,1)} %copy-done, f32[8]{0:T(128)} %convert_convert_fusion.tbl, f32[1,128]{1,0:T(1,128)} %bitcast.22), custom_call_target="tpu_custom_call" | custom-call | flops 805306368 | bytes 540672 | tf_op jit(solution)/shard_map/pallas_call | solution.py:121
  31.5 3.4 %collective-permute-start = (bf16[3,256,128]{2,1,0:T(8,128)(2,1)}, bf16[3,256,128]{2,1,0:T(8,128)(2,1)S(1)}, u32[]{:S(2)}, u32[]{:S(2)}) collective-permute-start(bf16[3,256,128]{2,1,0:T(8,128)(2,1)} %bitcast.13), channel_id=1, source_target_pairs={{0,1},{1,2},{2,3},{3,4},{4,5},{5,6},{6,7},{8,9},{9,10},{10,11},{11... | collective-permute-start | bytes 589832 | tf_op jit(solution)/shard_map/ppermute | solution.py:18
  34.9 3.9 %shard_map.130 = bf16[1280,128]{1,0:T(8,128)(2,1)} custom-call(f32[1280,256]{1,0:T(8,128)} %get-tuple-element.8.acc, bf16[8,272,128]{2,1,0:T(8,128)(2,1)} %copy-done, f32[8]{0:T(128)} %convert_convert_fusion.tbl, f32[1,128]{1,0:T(1,128)} %bitcast.23), custom_call_target="tpu_custom_call" | custom-call | flops 1342177280 | bytes 540672 | tf_op jit(solution)/shard_map/pallas_call | solution.py:121
  38.9 0.0 collective-permute-done.above
  38.9 0.0 copy-start.1
  38.9 0.7 %copy-done.1 = bf16[3,256,128]{2,1,0:T(8,128)(2,1)} copy-done((bf16[3,256,128]{2,1,0:T(8,128)(2,1)}, bf16[3,256,128]{2,1,0:T(8,128)(2,1)S(1)}, u32[]{:S(2)}) %copy-start.1) | copy-done | bytes 196632
  39.5 4.3 %shard_map.131 = bf16[8,2,64,256]{3,2,1,0:T(8,128)(2,1)} custom-call(bf16[3,256,128]{2,1,0:T(8,128)(2,1)} %copy-done.1, bf16[5,256,128]{2,1,0:T(8,128)(2,1)} %bitcast.12, bf16[3,256,128]{2,1,0:T(8,128)(2,1)} %bitcast.14, bf16[3,3,128,128]{3,2,1,0:T(8,128)(2,1)} %w1.1, f32[1,128]{1,0:T(1,128)} %bitcast.19, bf16[3,3,128,256]{3,2,1,0:T(8,128)(2,1)} %w2.1, ...), custom_call_target="tpu_custom_call" | custom-call | tf_op jit(solution)/shard_map/pallas_call | solution.py:203
  43.9 19.0 %all_to_all.10 = bf16[8,2,64,256]{3,2,1,0:T(8,128)(2,1)S(1)} all-to-all(bf16[8,2,64,256]{3,2,1,0:T(8,128)(2,1)} %shard_map.131), channel_id=1, replica_groups=mesh['member'=4,'band'=8] {'band'}, dimensions={0} | all-to-all | bytes 1048576 | tf_op jit(solution)/shard_map/all_to_all | solution.py:310
  62.9 0.8 %copy.15 = bf16[16,64,256]{2,1,0:T(8,128)(2,1)} copy(bf16[16,64,256]{2,1,0:T(8,128)(2,1)S(1)} %bitcast.11) | data formatting | bytes 1048576
Async XLA Ops:
  5.1 22.5 %all-to-all-start = ((bf16[8,272,128]{2,1,0:T(8,128)(2,1)}), bf16[8,272,128]{2,1,0:T(8,128)(2,1)S(1)}, u32[]{:S(2)}, u32[]{:S(2)}) async-start(bf16[8,272,128]{2,1,0:T(8,128)(2,1)} %shard_map.128), calls=%async_computation | async-start | bytes 1114112 | tf_op jit(solution)/shard_map/all_to_all | solution.py:274
  27.6 0.8 %copy-start = (bf16[8,272,128]{2,1,0:T(8,128)(2,1)}, bf16[8,272,128]{2,1,0:T(8,128)(2,1)S(1)}, u32[]{:S(2)}) copy-start(bf16[8,272,128]{2,1,0:T(8,128)(2,1)S(1)} %all-to-all-done.got) | copy-start | bytes 1671172
  31.5 7.3 %collective-permute-start = (bf16[3,256,128]{2,1,0:T(8,128)(2,1)}, bf16[3,256,128]{2,1,0:T(8,128)(2,1)S(1)}, u32[]{:S(2)}, u32[]{:S(2)}) collective-permute-start(bf16[3,256,128]{2,1,0:T(8,128)(2,1)} %bitcast.13), channel_id=1, source_target_pairs={{0,1},{1,2},{2,3},{3,4},{4,5},{5,6},{6,7},{8,9},{9,10},{10,11},{11... | collective-permute-start | bytes 589832 | tf_op jit(solution)/shard_map/ppermute | solution.py:18
  38.9 0.7 %copy-start.1 = (bf16[3,256,128]{2,1,0:T(8,128)(2,1)}, bf16[3,256,128]{2,1,0:T(8,128)(2,1)S(1)}, u32[]{:S(2)}) copy-start(bf16[3,256,128]{2,1,0:T(8,128)(2,1)S(1)} %collective-permute-done.above) | copy-start | bytes 589828
